TPU v7x, 512 devices: a whole 4x4x16 slice. The times are simulated.
512 devices in a mesh: leaf: 32 (over z, core), sub: 16 (over x, y).
Axes of the slice: x: 4, y: 4, z: 16, core: 2. Of those that a mesh axis runs over, the one named last changes fastest.
Arguments:
- right_side: float32 [2048, 32, 256], P(('leaf', 'sub'))
- points: float32 [2048, 3, 256], P(('leaf', 'sub')), may hold values from 0 to 32, as said below
- near_boxes: int32 [2048, 27], P(('leaf', 'sub')), may hold values from -1 to 2047, as said below
Outputs:
- solution_field: float32 [2048, 32, 256], P(('leaf', 'sub'))
- residual: float32 [2048, 32, 256], P(('leaf', 'sub'))
Inputs may be any that keep to these rules, and one draw needn't show every extreme that they name: `near_boxes`: each box's points lie in one unit cube with integer corner. A box lists itself and exactly the boxes whose cubes touch its own (faces, edges or corners), and -1 in its other entries. Every listed box lies on a device whose grid position differs by at most one in each of the three grid dimensions, where a device's index over leaf+sub is gx * 4 * 8 + gy * 8 + gz. Each box's points lie in its unit cube, the cubes of one device forming a block of 2 x 2 x 1.
All inputs are finite; a program needn't handle non-finite values.
Results may differ from a plain program's by a relative error of at most 0.0003.
Values sent between devices are 32-bit elements; how exact they have to be, the bound alone decides.
No kernel may reach another device: no remote copies, remote signals or barrier semaphores. Data moves between devices by JAX's collectives and lax.ppermute only.
A program may use at most 64 MiB of HBM per device.

v0:
```python
import jax
import jax.numpy as jnp
from jax import lax
from jax.sharding import PartitionSpec as P

ITERS = 2
GRID_Y = 4


NOISE_LEVEL = 0.3
KERNEL_SCALE = 0.15
SUPPORT = 0.5


def passed_along(block, axis, distance):
    devices = range(lax.axis_size(axis))
    route = [(i - distance, i) for i in devices if i - distance in devices]
    return lax.ppermute(block, axis, route)


def wendland(centers, others):
    summed = jnp.zeros((others.shape[0], others.shape[2], centers.shape[1]), jnp.float32)
    for component in range(3):
        difference = others[:, component, :, None] - centers[component][None, None, :]
        summed = summed + difference * difference
    radius = jnp.sqrt(summed) / SUPPORT
    inside = jnp.maximum(1.0 - radius, 0.0)
    return inside * inside * inside * inside * (4.0 * radius + 1.0)


def apply_box(entry):
    centers, others, near_values = entry
    kernel = wendland(centers, others)
    return jnp.einsum(
        "mrj,mji->ri",
        near_values,
        kernel,
        precision=lax.Precision.HIGHEST,
        preferred_element_type=jnp.float32,
    )


def grid_offsets(count_mid, count_low):
    listing = []
    for step_x in (-1, 0, 1):
        for step_y in (-1, 0, 1):
            for step_z in (-1, 0, 1):
                listing.append(step_x * count_mid * count_low + step_y * count_low + step_z)
    return listing


def collect_direct(tile_in, count_mid, count_low, mover):
    pieces = []
    for offset in grid_offsets(count_mid, count_low):
        if offset == 0:
            pieces.append(tile_in)
        else:
            pieces.append(mover(tile_in, -offset))
    stacked = jnp.stack(pieces, axis=0)
    return stacked.reshape((-1,) + tile_in.shape[1:])


def locate(near_boxes, per_dev, count_mid, count_low):
    own_dev = lax.axis_index(("leaf", "sub"))
    present = (near_boxes >= 0).astype(jnp.float32)
    clamped = jnp.maximum(near_boxes, 0)
    owner_dev = clamped // per_dev
    plane = count_mid * count_low
    step_x = owner_dev // plane - own_dev // plane
    step_y = owner_dev // count_low % count_mid - own_dev // count_low % count_mid
    step_z = owner_dev % count_low - own_dev % count_low
    positions = (((step_x + 1) * 3 + step_y + 1) * 3 + step_z + 1) * per_dev + clamped % per_dev
    positions = jnp.clip(positions, 0, 27 * per_dev - 1)
    return (positions, present)


def column_sums(first, second):
    return jnp.sum(first * second, axis=(0, 2))


def spread(column):
    return column[None, :, None]


def squares(residual):
    return lax.psum(column_sums(residual, residual), ("leaf", "sub"))


def per_device(right_side, points, near_boxes):
    count_low = lax.axis_size("sub") // 2
    count_mid = GRID_Y
    per_dev = points.shape[0]
    point_tiles = collect_direct(
        points,
        count_mid,
        count_low,
        lambda moving, amount: passed_along(moving, ("leaf", "sub"), amount),
    )
    positions, present = locate(near_boxes, per_dev, count_mid, count_low)
    others = point_tiles[positions]
    solution_field = jnp.zeros_like(right_side)
    residual = right_side
    direction = right_side
    norm_now = squares(residual)
    for iteration in range(ITERS):
        gathered = collect_direct(
            direction,
            count_mid,
            count_low,
            lambda moving, amount: passed_along(moving, ("leaf", "sub"), amount),
        )
        near_values = gathered[positions] * present[:, :, None, None]
        products = lax.map(apply_box, (points, others, near_values))
        image_vec = KERNEL_SCALE * products + NOISE_LEVEL * direction
        curve = lax.psum(column_sums(direction, image_vec), ("leaf", "sub"))
        step_size = norm_now / curve
        solution_field = solution_field + spread(step_size) * direction
        residual = residual - spread(step_size) * image_vec
        norm_next = squares(residual)
        direction = residual + spread(norm_next / norm_now) * direction
        norm_now = norm_next
    return (solution_field, residual)


def solution(mesh):
    placed = (
        P(("leaf", "sub"), None, None),
        P(("leaf", "sub"), None, None),
        P(("leaf", "sub"), None),
    )
    return jax.shard_map(
        per_device,
        mesh=mesh,
        in_specs=placed,
        out_specs=(P(("leaf", "sub"), None, None), P(("leaf", "sub"), None, None)),
        check_vma=False,
    )
```

profile of v0, /device:TPU:1, one launch (start us, length us, event | category | flops | bytes accessed | tf_op | source)
XLA Modules:
  0.0 891.9 jit_solution(12877085652996151127)
XLA Ops:
  0.6 8.0 collective-permute-start
  32.3 6.3 collective-permute-start.27
  46.9 8.3 collective-permute-start.29
  56.2 7.1 collective-permute-start.30
  71.4 7.3 collective-permute-start.32
  79.7 11.5 %collective-permute-start.33 = (f32[4,3,256]{2,0,1:T(4,128)}, f32[4,3,256]{2,0,1:T(4,128)S(1)}, u32[]{:S(2)}, u32[]{:S(2)}) collective-permute-start(f32[4,3,256]{2,0,1:T(4,128)} %param.8), channel_id=1, source_target_pairs={{0,24},{1,25},{2,26},{3,27},{4,28},{5,29},{6,30},{7,31},{8,32},{9,... | collective-permute-start | bytes 36872 | tf_op jit(solution)/shard_map/ppermute | solution.py:18
  161.8 7.6 collective-permute-done.43
  170.7 9.7 %collective-permute-done.44 = f32[4,3,256]{2,0,1:T(4,128)S(1)} collective-permute-done((f32[4,3,256]{2,0,1:T(4,128)}, f32[4,3,256]{2,0,1:T(4,128)S(1)}, u32[]{:S(2)}, u32[]{:S(2)}) %collective-permute-start.44) | collective-permute-done | bytes 12320 | tf_op jit(solution)/shard_map/ppermute | solution.py:18
  181.7 7.2 collective-permute-done.45
  190.2 18.6 %collective-permute-done.46 = f32[4,3,256]{2,0,1:T(4,128)S(1)} collective-permute-done((f32[4,3,256]{2,0,1:T(4,128)}, f32[4,3,256]{2,0,1:T(4,128)S(1)}, u32[]{:S(2)}, u32[]{:S(2)}) %collective-permute-start.46) | collective-permute-done | bytes 12320 | tf_op jit(solution)/shard_map/ppermute | solution.py:18
  210.1 10.7 %collective-permute-done.47 = f32[4,3,256]{2,0,1:T(4,128)S(1)} collective-permute-done((f32[4,3,256]{2,0,1:T(4,128)}, f32[4,3,256]{2,0,1:T(4,128)S(1)}, u32[]{:S(2)}, u32[]{:S(2)}) %collective-permute-start.47) | collective-permute-done | bytes 12320 | tf_op jit(solution)/shard_map/ppermute | solution.py:18
  227.7 7.8 collective-permute-done.49
  236.8 11.9 %collective-permute-done.50 = f32[4,3,256]{2,0,1:T(4,128)S(1)} collective-permute-done((f32[4,3,256]{2,0,1:T(4,128)}, f32[4,3,256]{2,0,1:T(4,128)S(1)}, u32[]{:S(2)}, u32[]{:S(2)}) %collective-permute-start.50) | collective-permute-done | bytes 12320 | tf_op jit(solution)/shard_map/ppermute | solution.py:18
  250.0 7.1 collective-permute-done.51
  263.0 6.4 collective-permute-start.5
  269.4 11.4 %collective-permute-start.6 = (f32[4,32,256]{2,1,0:T(8,128)S(1)}, f32[4,32,256]{2,1,0:T(8,128)S(1)}, u32[]{:S(2)}, u32[]{:S(2)}) collective-permute-start(f32[4,32,256]{2,1,0:T(8,128)S(1)} %copy-done.2), channel_id=1, source_target_pairs={{0,25},{1,26},{2,27},{3,28},{4,29},{5,30},{6,31},{7,32},{8,33},{9,... | collective-permute-start | bytes 393224 | tf_op jit(solution)/shard_map/ppermute | solution.py:18
  282.8 7.2 collective-permute-start.8
  355.1 43.8 %while.24 = (s32[]{:T(128)}, f32[4,32,256]{2,1,0:T(8,128)S(1)}, f32[4,27,32,256]{3,2,1,0:T(8,128)}, f32[4,27,3,256]{3,1,2,0:T(8,128)}, f32[4,3,256]{2,0,1:T(4,128)S(1)}, /*index=5*/s32[]{:T(128)}, s32[]{:T(128)}, s32[]{}, s32[]{}) while((s32[]{:T(128)}, f32[4,32,256]{2,1,0:T(8,128)S(1)}, f32[4,27,32,256]{3,2,1,0:T(8,128)}, ...), condition=%wide.region_3.4_spmd, body=%wide.region_2.3_spmd.sunk | while | flops 709558272 | bytes 1357957 | solution.py:113
  356.1 10.0 %fusion.104 = f32[4,32,256]{2,1,0:T(8,128)S(1)} fusion(f32[4,32,256]{2,1,0:T(8,128)S(1)} %get-tuple-element.288, s32[]{:T(128)} %get-tuple-element.287, f32[256]{0:T(256)S(1)} %bitcast.242, f32[27,256]{1,0:T(8,128)S(1)} %get-tuple-element.262, f32[256]{0:T(256)S(1)} %bitcast.241, f32[27,256]{1,0:T(8,128)S(1)} %get-tuple-element.264, ...), kind=kOutput, calls=%fused_computation.31.clone.1 | convolution fusion | flops 709558272 | bytes 1019904 | tf_op jit(solution)/shard_map/while/body/eval_jaxpr/mrj,mji->ri/dot_general | solution.py:34
  367.0 10.0 %fusion.104 = f32[4,32,256]{2,1,0:T(8,128)S(1)} fusion(f32[4,32,256]{2,1,0:T(8,128)S(1)} %get-tuple-element.288, s32[]{:T(128)} %get-tuple-element.287, f32[256]{0:T(256)S(1)} %bitcast.242, f32[27,256]{1,0:T(8,128)S(1)} %get-tuple-element.262, f32[256]{0:T(256)S(1)} %bitcast.241, f32[27,256]{1,0:T(8,128)S(1)} %get-tuple-element.264, ...), kind=kOutput, calls=%fused_computation.31.clone.1 | convolution fusion | flops 709558272 | bytes 1019904 | tf_op jit(solution)/shard_map/while/body/eval_jaxpr/mrj,mji->ri/dot_general | solution.py:34
  378.0 10.0 %fusion.104 = f32[4,32,256]{2,1,0:T(8,128)S(1)} fusion(f32[4,32,256]{2,1,0:T(8,128)S(1)} %get-tuple-element.288, s32[]{:T(128)} %get-tuple-element.287, f32[256]{0:T(256)S(1)} %bitcast.242, f32[27,256]{1,0:T(8,128)S(1)} %get-tuple-element.262, f32[256]{0:T(256)S(1)} %bitcast.241, f32[27,256]{1,0:T(8,128)S(1)} %get-tuple-element.264, ...), kind=kOutput, calls=%fused_computation.31.clone.1 | convolution fusion | flops 709558272 | bytes 1019904 | tf_op jit(solution)/shard_map/while/body/eval_jaxpr/mrj,mji->ri/dot_general | solution.py:34
  388.9 10.0 %fusion.104 = f32[4,32,256]{2,1,0:T(8,128)S(1)} fusion(f32[4,32,256]{2,1,0:T(8,128)S(1)} %get-tuple-element.288, s32[]{:T(128)} %get-tuple-element.287, f32[256]{0:T(256)S(1)} %bitcast.242, f32[27,256]{1,0:T(8,128)S(1)} %get-tuple-element.262, f32[256]{0:T(256)S(1)} %bitcast.241, f32[27,256]{1,0:T(8,128)S(1)} %get-tuple-element.264, ...), kind=kOutput, calls=%fused_computation.31.clone.1 | convolution fusion | flops 709558272 | bytes 1019904 | tf_op jit(solution)/shard_map/while/body/eval_jaxpr/mrj,mji->ri/dot_general | solution.py:34
  399.1 121.1 %all-reduce = (f32[32]{0:T(128)S(1)}, f32[32]{0:T(128)S(1)}) all-reduce(f32[32]{0:T(128)S(1)} %get-tuple-element.155, f32[32]{0:T(128)S(1)} %get-tuple-element.154), channel_id=1, replica_groups=mesh['leaf'=32,'sub'=16] {'leaf','sub'}, use_global_device_ids=true, to_apply=%region_1.2 | all-reduce | flops 64 | bytes 512 | tf_op jit(solution)/shard_map/psum | solution.py:86
  520.4 99.5 %psum.30 = f32[32]{0:T(128)S(1)} all-reduce(f32[32]{0:T(128)S(1)} %multiply_reduce_fusion.1), channel_id=1, replica_groups=mesh['leaf'=32,'sub'=16] {'leaf','sub'}, use_global_device_ids=true, to_apply=%region_7.8 | all-reduce | flops 32 | bytes 256 | tf_op jit(solution)/shard_map/psum | solution.py:86
  640.4 7.1 collective-permute-start.57
  673.4 7.0 collective-permute-start.65
  728.6 43.9 %while.25 = (s32[]{:T(128)}, f32[4,32,256]{2,1,0:T(8,128)S(1)}, f32[4,27,32,256]{3,2,1,0:T(8,128)}, f32[4,27,3,256]{3,1,2,0:T(8,128)}, f32[4,3,256]{2,0,1:T(4,128)S(1)}, /*index=5*/s32[]{:T(128)}, s32[]{:T(128)}, s32[]{}, s32[]{}) while((s32[]{:T(128)}, f32[4,32,256]{2,1,0:T(8,128)S(1)}, f32[4,27,32,256]{3,2,1,0:T(8,128)}, ...), condition=%wide.region_9.10_spmd, body=%wide.region_8.9_spmd.sunk | while | flops 709558272 | bytes 1357957 | solution.py:113
  729.7 10.0 %fusion.107 = f32[4,32,256]{2,1,0:T(8,128)S(1)} fusion(f32[4,32,256]{2,1,0:T(8,128)S(1)} %get-tuple-element.315, s32[]{:T(128)} %get-tuple-element.314, f32[256]{0:T(256)S(1)} %bitcast.245, f32[27,256]{1,0:T(8,128)S(1)} %get-tuple-element.273, f32[256]{0:T(256)S(1)} %bitcast.244, f32[27,256]{1,0:T(8,128)S(1)} %get-tuple-element.275, ...), kind=kOutput, calls=%fused_computation.74.clone.1 | convolution fusion | flops 709558272 | bytes 1019904 | tf_op jit(solution)/shard_map/while/body/eval_jaxpr/mrj,mji->ri/dot_general | solution.py:34
  740.6 10.0 %fusion.107 = f32[4,32,256]{2,1,0:T(8,128)S(1)} fusion(f32[4,32,256]{2,1,0:T(8,128)S(1)} %get-tuple-element.315, s32[]{:T(128)} %get-tuple-element.314, f32[256]{0:T(256)S(1)} %bitcast.245, f32[27,256]{1,0:T(8,128)S(1)} %get-tuple-element.273, f32[256]{0:T(256)S(1)} %bitcast.244, f32[27,256]{1,0:T(8,128)S(1)} %get-tuple-element.275, ...), kind=kOutput, calls=%fused_computation.74.clone.1 | convolution fusion | flops 709558272 | bytes 1019904 | tf_op jit(solution)/shard_map/while/body/eval_jaxpr/mrj,mji->ri/dot_general | solution.py:34
  751.6 10.0 %fusion.107 = f32[4,32,256]{2,1,0:T(8,128)S(1)} fusion(f32[4,32,256]{2,1,0:T(8,128)S(1)} %get-tuple-element.315, s32[]{:T(128)} %get-tuple-element.314, f32[256]{0:T(256)S(1)} %bitcast.245, f32[27,256]{1,0:T(8,128)S(1)} %get-tuple-element.273, f32[256]{0:T(256)S(1)} %bitcast.244, f32[27,256]{1,0:T(8,128)S(1)} %get-tuple-element.275, ...), kind=kOutput, calls=%fused_computation.74.clone.1 | convolution fusion | flops 709558272 | bytes 1019904 | tf_op jit(solution)/shard_map/while/body/eval_jaxpr/mrj,mji->ri/dot_general | solution.py:34
  762.5 10.0 %fusion.107 = f32[4,32,256]{2,1,0:T(8,128)S(1)} fusion(f32[4,32,256]{2,1,0:T(8,128)S(1)} %get-tuple-element.315, s32[]{:T(128)} %get-tuple-element.314, f32[256]{0:T(256)S(1)} %bitcast.245, f32[27,256]{1,0:T(8,128)S(1)} %get-tuple-element.273, f32[256]{0:T(256)S(1)} %bitcast.244, f32[27,256]{1,0:T(8,128)S(1)} %get-tuple-element.275, ...), kind=kOutput, calls=%fused_computation.74.clone.1 | convolution fusion | flops 709558272 | bytes 1019904 | tf_op jit(solution)/shard_map/while/body/eval_jaxpr/mrj,mji->ri/dot_general | solution.py:34
  772.7 118.4 %psum.31 = f32[32]{0:T(128)S(1)} all-reduce(f32[32]{0:T(128)S(1)} %multiply_reduce_fusion), channel_id=1, replica_groups=mesh['leaf'=32,'sub'=16] {'leaf','sub'}, use_global_device_ids=true, to_apply=%region_11.12 | all-reduce | flops 32 | bytes 256 | tf_op jit(solution)/shard_map/psum | solution.py:115
  (291 shorter events, 302.4 us)
Async XLA Ops:
  0.6 262.3 %collective-permute-start = (f32[4,32,256]{2,1,0:T(8,128)}, f32[4,32,256]{2,1,0:T(8,128)S(1)}, u32[]{:S(2)}, u32[]{:S(2)}) collective-permute-start(f32[4,32,256]{2,1,0:T(8,128)} %param.7), channel_id=1, source_target_pairs={{0,41},{1,42},{2,43},{3,44},{4,45},{5,46},{6,47},{7,48},{8,49},{9,... | collective-permute-start | bytes 393224 | tf_op jit(solution)/shard_map/ppermute | solution.py:18
  8.6 260.8 %collective-permute-start.1 = (f32[4,32,256]{2,1,0:T(8,128)}, f32[4,32,256]{2,1,0:T(8,128)S(1)}, u32[]{:S(2)}, u32[]{:S(2)}) collective-permute-start(f32[4,32,256]{2,1,0:T(8,128)} %param.7), channel_id=1, source_target_pairs={{0,40},{1,41},{2,42},{3,43},{4,44},{5,45},{6,46},{7,47},{8,48},{9,... | collective-permute-start | bytes 393224 | tf_op jit(solution)/shard_map/ppermute | solution.py:18
  14.0 266.8 %collective-permute-start.2 = (f32[4,32,256]{2,1,0:T(8,128)}, f32[4,32,256]{2,1,0:T(8,128)S(1)}, u32[]{:S(2)}, u32[]{:S(2)}) collective-permute-start(f32[4,32,256]{2,1,0:T(8,128)} %param.7), channel_id=1, source_target_pairs={{0,39},{1,40},{2,41},{3,42},{4,43},{5,44},{6,45},{7,46},{8,47},{9,... | collective-permute-start | bytes 393224 | tf_op jit(solution)/shard_map/ppermute | solution.py:18
  20.2 262.6 %collective-permute-start.3 = (f32[4,32,256]{2,1,0:T(8,128)}, f32[4,32,256]{2,1,0:T(8,128)S(1)}, u32[]{:S(2)}, u32[]{:S(2)}) collective-permute-start(f32[4,32,256]{2,1,0:T(8,128)} %param.7), channel_id=1, source_target_pairs={{0,33},{1,34},{2,35},{3,36},{4,37},{5,38},{6,39},{7,40},{8,41},{9,... | collective-permute-start | bytes 393224 | tf_op jit(solution)/shard_map/ppermute | solution.py:18
  188.9 19.9 %collective-permute-start.46 = (f32[4,3,256]{2,0,1:T(4,128)}, f32[4,3,256]{2,0,1:T(4,128)S(1)}, u32[]{:S(2)}, u32[]{:S(2)}) collective-permute-start(f32[4,3,256]{2,0,1:T(4,128)} %param.8), channel_id=1, source_target_pairs={{31,0},{32,1},{33,2},{34,3},{35,4},{36,5},{37,6},{38,7},{39,8},{40... | collective-permute-start | bytes 36872 | tf_op jit(solution)/shard_map/ppermute | solution.py:18
  257.0 33.0 %collective-permute-start.4 = (f32[4,32,256]{2,1,0:T(8,128)}, f32[4,32,256]{2,1,0:T(8,128)S(1)}, u32[]{:S(2)}, u32[]{:S(2)}) collective-permute-start(f32[4,32,256]{2,1,0:T(8,128)} %param.7), channel_id=1, source_target_pairs={{0,32},{1,33},{2,34},{3,35},{4,36},{5,37},{6,38},{7,39},{8,40},{9,... | collective-permute-start | bytes 393224 | tf_op jit(solution)/shard_map/ppermute | solution.py:18
  263.0 29.1 %collective-permute-start.5 = (f32[4,32,256]{2,1,0:T(8,128)}, f32[4,32,256]{2,1,0:T(8,128)S(1)}, u32[]{:S(2)}, u32[]{:S(2)}) collective-permute-start(f32[4,32,256]{2,1,0:T(8,128)} %param.7), channel_id=1, source_target_pairs={{0,31},{1,32},{2,33},{3,34},{4,35},{5,36},{6,37},{7,38},{8,39},{9,... | collective-permute-start | bytes 393224 | tf_op jit(solution)/shard_map/ppermute | solution.py:18
  269.4 28.2 %collective-permute-start.6 = (f32[4,32,256]{2,1,0:T(8,128)S(1)}, f32[4,32,256]{2,1,0:T(8,128)S(1)}, u32[]{:S(2)}, u32[]{:S(2)}) collective-permute-start(f32[4,32,256]{2,1,0:T(8,128)S(1)} %copy-done.2), channel_id=1, source_target_pairs={{0,25},{1,26},{2,27},{3,28},{4,29},{5,30},{6,31},{7,32},{8,33},{9,... | collective-permute-start | bytes 393224 | tf_op jit(solution)/shard_map/ppermute | solution.py:18
  280.8 18.7 %collective-permute-start.7 = (f32[4,32,256]{2,1,0:T(8,128)S(1)}, f32[4,32,256]{2,1,0:T(8,128)S(1)}, u32[]{:S(2)}, u32[]{:S(2)}) collective-permute-start(f32[4,32,256]{2,1,0:T(8,128)S(1)} %copy-done.2), channel_id=1, source_target_pairs={{0,24},{1,25},{2,26},{3,27},{4,28},{5,29},{6,30},{7,31},{8,32},{9,... | collective-permute-start | bytes 393224 | tf_op jit(solution)/shard_map/ppermute | solution.py:18
  282.8 19.8 %collective-permute-start.8 = (f32[4,32,256]{2,1,0:T(8,128)S(1)}, f32[4,32,256]{2,1,0:T(8,128)S(1)}, u32[]{:S(2)}, u32[]{:S(2)}) collective-permute-start(f32[4,32,256]{2,1,0:T(8,128)S(1)} %copy-done.2), channel_id=1, source_target_pairs={{0,23},{1,24},{2,25},{3,26},{4,27},{5,28},{6,29},{7,30},{8,31},{9,... | collective-permute-start | bytes 393224 | tf_op jit(solution)/shard_map/ppermute | solution.py:18
  290.1 18.4 %collective-permute-start.9 = (f32[4,32,256]{2,1,0:T(8,128)S(1)}, f32[4,32,256]{2,1,0:T(8,128)S(1)}, u32[]{:S(2)}, u32[]{:S(2)}) collective-permute-start(f32[4,32,256]{2,1,0:T(8,128)S(1)} %copy-done.2), channel_id=1, source_target_pairs={{0,9},{1,10},{2,11},{3,12},{4,13},{5,14},{6,15},{7,16},{8,17},{9,1... | collective-permute-start | bytes 393224 | tf_op jit(solution)/shard_map/ppermute | solution.py:18
  292.1 19.5 %collective-permute-start.10 = (f32[4,32,256]{2,1,0:T(8,128)S(1)}, f32[4,32,256]{2,1,0:T(8,128)S(1)}, u32[]{:S(2)}, u32[]{:S(2)}) collective-permute-start(f32[4,32,256]{2,1,0:T(8,128)S(1)} %copy-done.2), channel_id=1, source_target_pairs={{0,8},{1,9},{2,10},{3,11},{4,12},{5,13},{6,14},{7,15},{8,16},{9,17... | collective-permute-start | bytes 393224 | tf_op jit(solution)/shard_map/ppermute | solution.py:18
  297.6 18.0 %collective-permute-start.11 = (f32[4,32,256]{2,1,0:T(8,128)S(1)}, f32[4,32,256]{2,1,0:T(8,128)S(1)}, u32[]{:S(2)}, u32[]{:S(2)}) collective-permute-start(f32[4,32,256]{2,1,0:T(8,128)S(1)} %copy-done.2), channel_id=1, source_target_pairs={{0,7},{1,8},{2,9},{3,10},{4,11},{5,12},{6,13},{7,14},{8,15},{9,16}... | collective-permute-start | bytes 393224 | tf_op jit(solution)/shard_map/ppermute | solution.py:18
  299.5 18.0 %collective-permute-start.12 = (f32[4,32,256]{2,1,0:T(8,128)S(1)}, f32[4,32,256]{2,1,0:T(8,128)S(1)}, u32[]{:S(2)}, u32[]{:S(2)}) collective-permute-start(f32[4,32,256]{2,1,0:T(8,128)S(1)} %copy-done.2), channel_id=1, source_target_pairs={{0,1},{1,2},{2,3},{3,4},{4,5},{5,6},{6,7},{7,8},{8,9},{9,10},{10,1... | collective-permute-start | bytes 393224 | tf_op jit(solution)/shard_map/ppermute | solution.py:18
  302.7 16.2 %collective-permute-start.13 = (f32[4,32,256]{2,1,0:T(8,128)S(1)}, f32[4,32,256]{2,1,0:T(8,128)S(1)}, u32[]{:S(2)}, u32[]{:S(2)}) collective-permute-start(f32[4,32,256]{2,1,0:T(8,128)S(1)} %copy-done.2), channel_id=1, source_target_pairs={{1,0},{2,1},{3,2},{4,3},{5,4},{6,5},{7,6},{8,7},{9,8},{10,9},{11,1... | collective-permute-start | bytes 393224 | tf_op jit(solution)/shard_map/ppermute | solution.py:18
  323.7 19.1 %collective-permute-start.21 = (f32[4,32,256]{2,1,0:T(8,128)S(1)}, f32[4,32,256]{2,1,0:T(8,128)S(1)}, u32[]{:S(2)}, u32[]{:S(2)}) collective-permute-start(f32[4,32,256]{2,1,0:T(8,128)S(1)} %copy-done.2), channel_id=1, source_target_pairs={{32,0},{33,1},{34,2},{35,3},{36,4},{37,5},{38,6},{39,7},{40,8},{41... | collective-permute-start | bytes 393224 | tf_op jit(solution)/shard_map/ppermute | solution.py:18
  326.9 15.9 %collective-permute-start.22 = (f32[4,32,256]{2,1,0:T(8,128)S(1)}, f32[4,32,256]{2,1,0:T(8,128)S(1)}, u32[]{:S(2)}, u32[]{:S(2)}) collective-permute-start(f32[4,32,256]{2,1,0:T(8,128)S(1)} %copy-done.2), channel_id=1, source_target_pairs={{33,0},{34,1},{35,2},{36,3},{37,4},{38,5},{39,6},{40,7},{41,8},{42... | collective-permute-start | bytes 393224 | tf_op jit(solution)/shard_map/ppermute | solution.py:18
  620.6 19.9 %collective-permute-start.52 = (f32[4,32,256]{2,1,0:T(8,128)S(1)}, f32[4,32,256]{2,1,0:T(8,128)S(1)}, u32[]{:S(2)}, u32[]{:S(2)}) collective-permute-start(f32[4,32,256]{2,1,0:T(8,128)S(1)} %multiply_add_fusion.2), channel_id=1, source_target_pairs={{0,41},{1,42},{2,43},{3,44},{4,45},{5,46},{6,47},{7,48},{8,49},{9,... | collective-permute-start | bytes 393224 | tf_op jit(solution)/shard_map/ppermute | solution.py:18
  625.6 21.9 %collective-permute-start.53 = (f32[4,32,256]{2,1,0:T(8,128)S(1)}, f32[4,32,256]{2,1,0:T(8,128)S(1)}, u32[]{:S(2)}, u32[]{:S(2)}) collective-permute-start(f32[4,32,256]{2,1,0:T(8,128)S(1)} %multiply_add_fusion.2), channel_id=1, source_target_pairs={{0,40},{1,41},{2,42},{3,43},{4,44},{5,45},{6,46},{7,47},{8,48},{9,... | collective-permute-start | bytes 393224 | tf_op jit(solution)/shard_map/ppermute | solution.py:18
  629.2 21.2 %collective-permute-start.54 = (f32[4,32,256]{2,1,0:T(8,128)S(1)}, f32[4,32,256]{2,1,0:T(8,128)S(1)}, u32[]{:S(2)}, u32[]{:S(2)}) collective-permute-start(f32[4,32,256]{2,1,0:T(8,128)S(1)} %multiply_add_fusion.2), channel_id=1, source_target_pairs={{0,39},{1,40},{2,41},{3,42},{4,43},{5,44},{6,45},{7,46},{8,47},{9,... | collective-permute-start | bytes 393224 | tf_op jit(solution)/shard_map/ppermute | solution.py:18
  632.6 22.1 %collective-permute-start.55 = (f32[4,32,256]{2,1,0:T(8,128)S(1)}, f32[4,32,256]{2,1,0:T(8,128)S(1)}, u32[]{:S(2)}, u32[]{:S(2)}) collective-permute-start(f32[4,32,256]{2,1,0:T(8,128)S(1)} %multiply_add_fusion.2), channel_id=1, source_target_pairs={{0,33},{1,34},{2,35},{3,36},{4,37},{5,38},{6,39},{7,40},{8,41},{9,... | collective-permute-start | bytes 393224 | tf_op jit(solution)/shard_map/ppermute | solution.py:18
  637.9 22.1 %collective-permute-start.56 = (f32[4,32,256]{2,1,0:T(8,128)S(1)}, f32[4,32,256]{2,1,0:T(8,128)S(1)}, u32[]{:S(2)}, u32[]{:S(2)}) collective-permute-start(f32[4,32,256]{2,1,0:T(8,128)S(1)} %multiply_add_fusion.2), channel_id=1, source_target_pairs={{0,32},{1,33},{2,34},{3,35},{4,36},{5,37},{6,38},{7,39},{8,40},{9,... | collective-permute-start | bytes 393224 | tf_op jit(solution)/shard_map/ppermute | solution.py:18
  640.4 23.7 %collective-permute-start.57 = (f32[4,32,256]{2,1,0:T(8,128)S(1)}, f32[4,32,256]{2,1,0:T(8,128)S(1)}, u32[]{:S(2)}, u32[]{:S(2)}) collective-permute-start(f32[4,32,256]{2,1,0:T(8,128)S(1)} %multiply_add_fusion.2), channel_id=1, source_target_pairs={{0,31},{1,32},{2,33},{3,34},{4,35},{5,36},{6,37},{7,38},{8,39},{9,... | collective-permute-start | bytes 393224 | tf_op jit(solution)/shard_map/ppermute | solution.py:18
  647.6 19.8 %collective-permute-start.58 = (f32[4,32,256]{2,1,0:T(8,128)S(1)}, f32[4,32,256]{2,1,0:T(8,128)S(1)}, u32[]{:S(2)}, u32[]{:S(2)}) collective-permute-start(f32[4,32,256]{2,1,0:T(8,128)S(1)} %multiply_add_fusion.2), channel_id=1, source_target_pairs={{0,25},{1,26},{2,27},{3,28},{4,29},{5,30},{6,31},{7,32},{8,33},{9,... | collective-permute-start | bytes 393224 | tf_op jit(solution)/shard_map/ppermute | solution.py:18
  650.4 21.0 %collective-permute-start.59 = (f32[4,32,256]{2,1,0:T(8,128)S(1)}, f32[4,32,256]{2,1,0:T(8,128)S(1)}, u32[]{:S(2)}, u32[]{:S(2)}) collective-permute-start(f32[4,32,256]{2,1,0:T(8,128)S(1)} %multiply_add_fusion.2), channel_id=1, source_target_pairs={{0,24},{1,25},{2,26},{3,27},{4,28},{5,29},{6,30},{7,31},{8,32},{9,... | collective-permute-start | bytes 393224 | tf_op jit(solution)/shard_map/ppermute | solution.py:18
  654.7 18.6 %collective-permute-start.60 = (f32[4,32,256]{2,1,0:T(8,128)S(1)}, f32[4,32,256]{2,1,0:T(8,128)S(1)}, u32[]{:S(2)}, u32[]{:S(2)}) collective-permute-start(f32[4,32,256]{2,1,0:T(8,128)S(1)} %multiply_add_fusion.2), channel_id=1, source_target_pairs={{0,23},{1,24},{2,25},{3,26},{4,27},{5,28},{6,29},{7,30},{8,31},{9,... | collective-permute-start | bytes 393224 | tf_op jit(solution)/shard_map/ppermute | solution.py:18
  659.9 20.4 %collective-permute-start.61 = (f32[4,32,256]{2,1,0:T(8,128)S(1)}, f32[4,32,256]{2,1,0:T(8,128)S(1)}, u32[]{:S(2)}, u32[]{:S(2)}) collective-permute-start(f32[4,32,256]{2,1,0:T(8,128)S(1)} %multiply_add_fusion.2), channel_id=1, source_target_pairs={{0,9},{1,10},{2,11},{3,12},{4,13},{5,14},{6,15},{7,16},{8,17},{9,1... | collective-permute-start | bytes 393224 | tf_op jit(solution)/shard_map/ppermute | solution.py:18
  664.2 18.1 %collective-permute-start.62 = (f32[4,32,256]{2,1,0:T(8,128)S(1)}, f32[4,32,256]{2,1,0:T(8,128)S(1)}, u32[]{:S(2)}, u32[]{:S(2)}) collective-permute-start(f32[4,32,256]{2,1,0:T(8,128)S(1)} %multiply_add_fusion.2), channel_id=1, source_target_pairs={{0,8},{1,9},{2,10},{3,11},{4,12},{5,13},{6,14},{7,15},{8,16},{9,17... | collective-permute-start | bytes 393224 | tf_op jit(solution)/shard_map/ppermute | solution.py:18
  667.3 19.5 %collective-permute-start.63 = (f32[4,32,256]{2,1,0:T(8,128)S(1)}, f32[4,32,256]{2,1,0:T(8,128)S(1)}, u32[]{:S(2)}, u32[]{:S(2)}) collective-permute-start(f32[4,32,256]{2,1,0:T(8,128)S(1)} %multiply_add_fusion.2), channel_id=1, source_target_pairs={{0,7},{1,8},{2,9},{3,10},{4,11},{5,12},{6,13},{7,14},{8,15},{9,16}... | collective-permute-start | bytes 393224 | tf_op jit(solution)/shard_map/ppermute | solution.py:18
  671.4 17.4 %collective-permute-start.64 = (f32[4,32,256]{2,1,0:T(8,128)S(1)}, f32[4,32,256]{2,1,0:T(8,128)S(1)}, u32[]{:S(2)}, u32[]{:S(2)}) collective-permute-start(f32[4,32,256]{2,1,0:T(8,128)S(1)} %multiply_add_fusion.2), channel_id=1, source_target_pairs={{0,1},{1,2},{2,3},{3,4},{4,5},{5,6},{6,7},{7,8},{8,9},{9,10},{10,1... | collective-permute-start | bytes 393224 | tf_op jit(solution)/shard_map/ppermute | solution.py:18
  673.4 16.7 %collective-permute-start.65 = (f32[4,32,256]{2,1,0:T(8,128)S(1)}, f32[4,32,256]{2,1,0:T(8,128)S(1)}, u32[]{:S(2)}, u32[]{:S(2)}) collective-permute-start(f32[4,32,256]{2,1,0:T(8,128)S(1)} %multiply_add_fusion.2), channel_id=1, source_target_pairs={{1,0},{2,1},{3,2},{4,3},{5,4},{6,5},{7,6},{8,7},{9,8},{10,9},{11,1... | collective-permute-start | bytes 393224 | tf_op jit(solution)/shard_map/ppermute | solution.py:18
  694.9 16.2 %collective-permute-start.73 = (f32[4,32,256]{2,1,0:T(8,128)S(1)}, f32[4,32,256]{2,1,0:T(8,128)S(1)}, u32[]{:S(2)}, u32[]{:S(2)}) collective-permute-start(f32[4,32,256]{2,1,0:T(8,128)S(1)} %multiply_add_fusion.2), channel_id=1, source_target_pairs={{32,0},{33,1},{34,2},{35,3},{36,4},{37,5},{38,6},{39,7},{40,8},{41... | collective-permute-start | bytes 393224 | tf_op jit(solution)/shard_map/ppermute | solution.py:18
  (60 other events, 2017.9 us)
where the time goes:
time: 895 us; the launch traced here: 892 us
  blocking collectives  339 us (38%)
  starting transfers between devices  287 us (32%)
  waiting for transfers between devices  154 us (17%)
  matrix products  79.9 us (9%)
  local copies, waits for them, and re-layouts  20.7 us (2%)
    ppermute x78, starting transfers between devices, passed_along(): return lax.ppermute(block, axis, route)  287 us
    psum x2, blocking collectives, squares(): return lax.psum(column_sums(residual, residual), ('leaf', 'sub'))  221 us
    ppermute x78, waiting for transfers between devices, passed_along(): return lax.ppermute(block, axis, route)  154 us
    psum x1, blocking collectives, per_device(): curve = lax.psum(column_sums(direction, image_vec), ('leaf', 'sub'))  118 us
    dot_general x8, matrix products, apply_box(): jnp.einsum('mrj,mji->ri', near_values, kernel, precision=lax.Precision.HI...  79.9 us
  transfers between devices with their start and end apart: 78, of which 42 were waited for; matrix products, arithmetic and copies ran while one was open for 1% of the time, Pallas kernels for 0%

commit v1 on v0

v1 whole, which is shorter than its diff:
```python
import jax
import jax.numpy as jnp
from jax import lax
from jax.sharding import PartitionSpec as P

GRID_Y = 4


NOISE_LEVEL = 0.3
KERNEL_SCALE = 0.15
SUPPORT = 0.5

AXES = ("leaf", "sub")


def grid_shape():
    count_low = lax.axis_size("sub") // 2
    count_mid = GRID_Y
    total = lax.axis_size("leaf") * lax.axis_size("sub")
    return (total // (count_mid * count_low), count_mid, count_low)


def neighbour_route(shape, dim, step):
    sizes = shape
    route = []
    for dev in range(sizes[0] * sizes[1] * sizes[2]):
        pos = [dev // (sizes[1] * sizes[2]), dev // sizes[2] % sizes[1], dev % sizes[2]]
        pos[dim] += step
        if 0 <= pos[dim] < sizes[dim]:
            source = (pos[0] * sizes[1] + pos[1]) * sizes[2] + pos[2]
            route.append((source, dev))
    return route


HALO_ORDER = (1, 2, 0)


def collect_halo(tile_in, shape):
    current = tile_in
    for dim in HALO_ORDER:
        lower = lax.ppermute(current, AXES, neighbour_route(shape, dim, -1))
        upper = lax.ppermute(current, AXES, neighbour_route(shape, dim, 1))
        current = jnp.concatenate([lower, current, upper], axis=0)
    return current


def wendland(centers, others):
    summed = jnp.zeros((others.shape[0], others.shape[2], centers.shape[1]), jnp.float32)
    for component in range(3):
        difference = others[:, component, :, None] - centers[component][None, None, :]
        summed = summed + difference * difference
    radius = jnp.sqrt(summed) / SUPPORT
    inside = jnp.maximum(1.0 - radius, 0.0)
    return inside * inside * inside * inside * (4.0 * radius + 1.0)


def locate(near_boxes, per_dev, shape):
    count_mid, count_low = shape[1], shape[2]
    own_dev = lax.axis_index(AXES)
    present = (near_boxes >= 0).astype(jnp.float32)
    clamped = jnp.maximum(near_boxes, 0)
    owner_dev = clamped // per_dev
    plane = count_mid * count_low
    step_x = owner_dev // plane - own_dev // plane
    step_y = owner_dev // count_low % count_mid - own_dev // count_low % count_mid
    step_z = owner_dev % count_low - own_dev % count_low
    positions = (((step_x + 1) * 3 + step_z + 1) * 3 + step_y + 1) * per_dev + clamped % per_dev
    positions = jnp.clip(positions, 0, 27 * per_dev - 1)
    return (positions, present)


def column_sums(first, second):
    return jnp.sum(first * second, axis=(0, 2))


def spread(column):
    return column[None, :, None]


def per_device(right_side, points, near_boxes):
    shape = grid_shape()
    per_dev = points.shape[0]
    positions, present = locate(near_boxes, per_dev, shape)
    point_tiles = collect_halo(points, shape)
    others = point_tiles[positions]
    kernel = jax.vmap(wendland)(points, others) * present[:, :, None, None]
    kernel = lax.optimization_barrier(kernel)

    def operate(values):
        gathered = collect_halo(values, shape)
        near_values = gathered[positions]
        products = jnp.einsum(
            "bmrj,bmji->bri",
            near_values,
            kernel,
            precision=lax.Precision.HIGHEST,
            preferred_element_type=jnp.float32,
        )
        return KERNEL_SCALE * products + NOISE_LEVEL * values

    residual0 = right_side
    direction0 = right_side
    image0 = operate(direction0)
    first = lax.psum(
        jnp.stack([column_sums(residual0, residual0), column_sums(direction0, image0)]),
        AXES,
    )
    norm0, curve0 = first[0], first[1]
    step0 = norm0 / curve0
    solution_field = spread(step0) * direction0
    residual1 = residual0 - spread(step0) * image0
    image_res = operate(residual1)
    second = lax.psum(
        jnp.stack(
            [
                column_sums(residual1, residual1),
                column_sums(residual1, image_res),
                column_sums(residual1, image0),
                column_sums(direction0, image_res),
            ]
        ),
        AXES,
    )
    norm1 = second[0]
    ratio = norm1 / norm0
    curve1 = second[1] + ratio * (second[2] + second[3]) + ratio * ratio * curve0
    step1 = norm1 / curve1
    direction1 = residual1 + spread(ratio) * direction0
    image1 = image_res + spread(ratio) * image0
    solution_field = solution_field + spread(step1) * direction1
    residual2 = residual1 - spread(step1) * image1
    return (solution_field, residual2)


def solution(mesh):
    placed = (
        P(AXES, None, None),
        P(AXES, None, None),
        P(AXES, None),
    )
    return jax.shard_map(
        per_device,
        mesh=mesh,
        in_specs=placed,
        out_specs=(P(AXES, None, None), P(AXES, None, None)),
        check_vma=False,
    )
```

time: 895 us -> 419 us (0.47)
  starting transfers between devices: 287 us -> 48.4 us
  blocking collectives: 339 us -> 225 us
  waiting for transfers between devices: 154 us -> 44.8 us
  matrix products: 79.9 us -> 42.2 us
  other arithmetic: 8.83 us -> 32.9 us
    ppermute x78 -> x18, starting transfers between devices: 287 us -> 48.4 us  [the longest x9 25.4 us: collect_halo(): upper = lax.ppermute(current, AXES, neighbour_route(shape, dim, 1))]
    psum x3 -> x2, blocking collectives: 339 us -> 225 us  [the longest x1 120 us: per_device(): lax.psum(jnp.stack([column_sums(residual0, residual0), column_sums(direct...]
    ppermute x78 -> x18, waiting for transfers between devices: 154 us -> 44.8 us  [the longest x9 37.1 us: collect_halo(): lower = lax.ppermute(current, AXES, neighbour_route(shape, dim, -1))]
    dot_general x8 -> x2, matrix products: 79.9 us -> 42.2 us  [operate(): jnp.einsum('bmrj,bmji->bri', near_values, kernel, precision=lax.Precision...]
    mul x2 -> x1, other arithmetic: 5.48 us -> 27.8 us  [per_device(): kernel = jax.vmap(wendland)(points, others) * present[:, :, None, None]]
  transfers between devices with their start and end apart: 78 -> 18, of which waited for: 42 -> 7; matrix products, arithmetic and copies ran while one was open for 1% -> 11% of each run, Pallas kernels for 0% -> 0%
where the time goes in v1:
time: 419 us; the launch traced here: 418 us
  blocking collectives  225 us (54%)
  starting transfers between devices  48.4 us (12%)
  waiting for transfers between devices  44.8 us (11%)
  matrix products  42.2 us (10%)
  other arithmetic  32.9 us (8%)
  local copies, waits for them, and re-layouts  23.4 us (6%)
    psum x1, blocking collectives, per_device(): lax.psum(jnp.stack([column_sums(residual0, residual0), column_sums(direct...  120 us
    psum x1, blocking collectives, per_device(): lax.psum(jnp.stack([column_sums(residual1, residual1), column_sums(residu...  105 us
    dot_general x2, matrix products, operate(): jnp.einsum('bmrj,bmji->bri', near_values, kernel, precision=lax.Precision...  42.2 us
    ppermute x9, waiting for transfers between devices, collect_halo(): lower = lax.ppermute(current, AXES, neighbour_route(shape, dim, -1))  37.1 us
    mul x1, other arithmetic, per_device(): kernel = jax.vmap(wendland)(points, others) * present[:, :, None, None]  27.8 us
    ppermute x9, starting transfers between devices, collect_halo(): upper = lax.ppermute(current, AXES, neighbour_route(shape, dim, 1))  25.4 us
    ppermute x9, starting transfers between devices, collect_halo(): lower = lax.ppermute(current, AXES, neighbour_route(shape, dim, -1))  23 us
    unnamed x40, local copies, waits for them, and re-layouts  13.5 us
  transfers between devices with their start and end apart: 18, of which 7 were waited for; matrix products, arithmetic and copies ran while one was open for 11% of the time, Pallas kernels for 0%

profile of v1, /device:TPU:1, one launch (start us, length us, event | category | flops | bytes accessed | tf_op | source)
XLA Modules:
  0.0 417.6 jit_solution(7296141983901313690)
XLA Ops:
  1.4 6.0 %collective-permute-start.7 = (f32[4,3,256]{2,1,0:T(4,128)S(1)}, f32[4,3,256]{2,1,0:T(4,128)S(1)}, u32[]{:S(2)}, u32[]{:S(2)}) collective-permute-start(f32[4,3,256]{2,1,0:T(4,128)S(1)} %copy.5), channel_id=1, source_target_pairs={{8,0},{9,1},{10,2},{11,3},{12,4},{13,5},{14,6},{15,7},{16,8},{17,9... | collective-permute-start | bytes 36872 | tf_op jit(solution)/shard_map/ppermute | solution.py:42
  7.4 1.9 collective-permute-start.6
  9.3 7.8 %collective-permute-start.1 = (f32[4,32,256]{2,1,0:T(8,128)}, f32[4,32,256]{2,1,0:T(8,128)S(1)}, u32[]{:S(2)}, u32[]{:S(2)}) collective-permute-start(f32[4,32,256]{2,1,0:T(8,128)} %param.3), channel_id=1, source_target_pairs={{8,0},{9,1},{10,2},{11,3},{12,4},{13,5},{14,6},{15,7},{16,8},{17,9... | collective-permute-start | bytes 393224 | tf_op jit(solution)/shard_map/ppermute | solution.py:42
  17.1 1.9 collective-permute-start
  22.0 1.3 collective-permute-start.8
  23.3 1.3 collective-permute-start.9
  25.4 2.8 collective-permute-done.9
  28.2 1.3 collective-permute-start.11
  29.5 4.0 collective-permute-start.10
  34.5 1.3 collective-permute-start.3
  35.8 4.0 collective-permute-start.2
  41.8 2.7 collective-permute-done.2
  44.6 1.3 collective-permute-start.5
  45.9 4.1 collective-permute-start.4
  50.0 27.8 %fusion.1 = f32[4,27,256,256]{3,2,1,0:T(8,128)} fusion(f32[4,27]{1,0:T(4,128)S(1)} %compare_convert_fusion, f32[4,256]{1,0:T(4,128)S(1)} %get-tuple-element.16, f32[4,27,256]{2,1,0:T(8,128)S(1)} %get-tuple-element.20, f32[4,256]{1,0:T(4,128)S(1)} %get-tuple-element.17, f32[4,27,256]{2,1,0:T(8,128)S(1)} %get-tuple-element.21, ...), kind=kLoop, calls=%fused_computation.5 | loop fusion | flops 127401984 | bytes 28656048 | tf_op jit(solution)/shard_map/mul | solution.py:86
  83.7 2.8 gather_fusion
  86.5 20.8 %multiply_reduce_fusion.5 = (f32[32]{0:T(128)S(1)}, f32[32]{0:T(128)S(1)}, f32[4,32,256]{2,1,0:T(8,128)}) fusion(f32[4,32,256]{2,1,0:T(8,128)} %param.3, f32[4,27,32,256]{3,2,1,0:T(8,128)S(1)} %bitcast.63, f32[4,27,256,256]{3,2,1,0:T(8,128)} %fusion.1), kind=kOutput, calls=%fused_computation.24 | convolution fusion | flops 2718138368 | bytes 32112896 | tf_op jit(solution)/shard_map/bmrj,bmji->bri/dot_general | solution.py:92
  107.3 120.3 %psum.14 = f32[2,32]{1,0:T(2,128)S(1)} all-reduce(f32[2,32]{1,0:T(2,128)S(1)} %pad_maximum_fusion.2), channel_id=1, replica_groups=mesh['leaf'=32,'sub'=16] {'leaf','sub'}, use_global_device_ids=true, to_apply=%region_2.3 | all-reduce | flops 64 | bytes 512 | tf_op jit(solution)/shard_map/psum | solution.py:104
  228.6 3.6 collective-permute-start.13
  232.3 3.1 collective-permute-start.12
  236.3 3.8 collective-permute-done.12
  240.1 1.3 collective-permute-start.14
  241.4 1.3 collective-permute-start.15
  242.7 7.0 %collective-permute-done.14 = f32[12,32,256]{2,1,0:T(8,128)S(1)} collective-permute-done((f32[12,32,256]{2,1,0:T(8,128)S(1)}, f32[12,32,256]{2,1,0:T(8,128)S(1)}, u32[]{:S(2)}, u32[]{:S(2)}) %collective-permute-start.14) | collective-permute-done | bytes 393248 | tf_op jit(solution)/shard_map/ppermute | solution.py:41
  249.8 4.0 collective-permute-done.15
  253.9 1.4 collective-permute-start.16
  255.2 1.5 collective-permute-start.17
  256.7 23.7 %collective-permute-done.16 = f32[36,32,256]{2,1,0:T(8,128)S(1)} collective-permute-done((f32[36,32,256]{2,1,0:T(8,128)S(1)}, f32[36,32,256]{2,1,0:T(8,128)S(1)}, u32[]{:S(2)}, u32[]{:S(2)}) %collective-permute-start.16) | collective-permute-done | bytes 1179680 | tf_op jit(solution)/shard_map/ppermute | solution.py:41
  286.2 2.8 gather_fusion.2
  289.0 21.4 %multiply_reduce_fusion.3 = (f32[32]{0:T(128)S(1)}, f32[32]{0:T(128)S(1)}, f32[32]{0:T(128)}, f32[32]{0:T(128)}, f32[4,32,256]{2,1,0:T(8,128)}) fusion(f32[4,32,256]{2,1,0:T(8,128)} %copy-done.1, f32[4,32,256]{2,1,0:T(8,128)} %get-tuple-element.18, f32[4,32,256]{2,1,0:T(8,128)} %param.3, f32[4,27,32,256]{3,2,1,0:T(8,128)S(1)} %bitcast.64, ...), kind=kOutput, calls=%fused_computation.21 | convolution fusion | flops 2718269440 | bytes 32375296 | tf_op jit(solution)/shard_map/bmrj,bmji->bri/dot_general | solution.py:92
  311.1 104.5 %psum.15 = f32[4,32]{1,0:T(4,128)S(1)} all-reduce(f32[4,32]{1,0:T(4,128)S(1)} %pad_maximum_fusion.1), channel_id=1, replica_groups=mesh['leaf'=32,'sub'=16] {'leaf','sub'}, use_global_device_ids=true, to_apply=%region_7.8 | all-reduce | flops 128 | bytes 1024 | tf_op jit(solution)/shard_map/psum | solution.py:113
  415.7 1.9 multiply_subtract_fusion
  (74 shorter events, 21.9 us)
Async XLA Ops:
  0.6 43.9 %copy-start = (f32[4,32,256]{2,1,0:T(8,128)S(1)}, f32[4,32,256]{2,1,0:T(8,128)}, u32[]{:S(2)}) copy-start(f32[4,32,256]{2,1,0:T(8,128)} %param.3) | copy-start | bytes 393220
  1.4 20.6 %collective-permute-start.7 = (f32[4,3,256]{2,1,0:T(4,128)S(1)}, f32[4,3,256]{2,1,0:T(4,128)S(1)}, u32[]{:S(2)}, u32[]{:S(2)}) collective-permute-start(f32[4,3,256]{2,1,0:T(4,128)S(1)} %copy.5), channel_id=1, source_target_pairs={{8,0},{9,1},{10,2},{11,3},{12,4},{13,5},{14,6},{15,7},{16,8},{17,9... | collective-permute-start | bytes 36872 | tf_op jit(solution)/shard_map/ppermute | solution.py:42
  7.4 13.9 %collective-permute-start.6 = (f32[4,3,256]{2,1,0:T(4,128)S(1)}, f32[4,3,256]{2,1,0:T(4,128)S(1)}, u32[]{:S(2)}, u32[]{:S(2)}) collective-permute-start(f32[4,3,256]{2,1,0:T(4,128)S(1)} %copy.5), channel_id=1, source_target_pairs={{0,8},{1,9},{2,10},{3,11},{4,12},{5,13},{6,14},{7,15},{8,16},{9,17... | collective-permute-start | bytes 36872 | tf_op jit(solution)/shard_map/ppermute | solution.py:41
  9.3 25.1 %collective-permute-start.1 = (f32[4,32,256]{2,1,0:T(8,128)}, f32[4,32,256]{2,1,0:T(8,128)S(1)}, u32[]{:S(2)}, u32[]{:S(2)}) collective-permute-start(f32[4,32,256]{2,1,0:T(8,128)} %param.3), channel_id=1, source_target_pairs={{8,0},{9,1},{10,2},{11,3},{12,4},{13,5},{14,6},{15,7},{16,8},{17,9... | collective-permute-start | bytes 393224 | tf_op jit(solution)/shard_map/ppermute | solution.py:42
  17.1 16.4 %collective-permute-start = (f32[4,32,256]{2,1,0:T(8,128)}, f32[4,32,256]{2,1,0:T(8,128)S(1)}, u32[]{:S(2)}, u32[]{:S(2)}) collective-permute-start(f32[4,32,256]{2,1,0:T(8,128)} %param.3), channel_id=1, source_target_pairs={{0,8},{1,9},{2,10},{3,11},{4,12},{5,13},{6,14},{7,15},{8,16},{9,17... | collective-permute-start | bytes 393224 | tf_op jit(solution)/shard_map/ppermute | solution.py:41
  22.0 2.6 collective-permute-start.8
  23.3 4.8 %collective-permute-start.9 = (f32[12,3,256]{2,1,0:T(4,128)S(1)}, f32[12,3,256]{2,1,0:T(4,128)S(1)}, u32[]{:S(2)}, u32[]{:S(2)}) collective-permute-start(f32[12,3,256]{2,1,0:T(4,128)S(1)} %constant_dynamic-update-slice_fusion.15), channel_id=1, source_target_pairs={{1,0},{2,1},{3,2},{4,3},{5,4},{6,5},{7,6},{9,8},{10,9},{11,10},{12... | collective-permute-start | bytes 110600 | tf_op jit(solution)/shard_map/ppermute | solution.py:42
  28.2 12.4 %collective-permute-start.11 = (f32[36,3,256]{2,1,0:T(4,128)S(1)}, f32[36,3,256]{2,1,0:T(4,128)S(1)}, u32[]{:S(2)}, u32[]{:S(2)}) collective-permute-start(f32[36,3,256]{2,1,0:T(4,128)S(1)} %constant_dynamic-update-slice_fusion.18), channel_id=1, source_target_pairs={{32,0},{33,1},{34,2},{35,3},{36,4},{37,5},{38,6},{39,7},{40,8},{41... | collective-permute-start | bytes 331784 | tf_op jit(solution)/shard_map/ppermute | solution.py:42
  29.5 10.3 %collective-permute-start.10 = (f32[36,3,256]{2,1,0:T(4,128)S(1)}, f32[36,3,256]{2,1,0:T(4,128)S(1)}, u32[]{:S(2)}, u32[]{:S(2)}) collective-permute-start(f32[36,3,256]{2,1,0:T(4,128)S(1)} %constant_dynamic-update-slice_fusion.18), channel_id=1, source_target_pairs={{0,32},{1,33},{2,34},{3,35},{4,36},{5,37},{6,38},{7,39},{8,40},{9,... | collective-permute-start | bytes 331784 | tf_op jit(solution)/shard_map/ppermute | solution.py:41
  34.5 10.1 %collective-permute-start.3 = (f32[12,32,256]{2,1,0:T(8,128)S(1)}, f32[12,32,256]{2,1,0:T(8,128)S(1)}, u32[]{:S(2)}, u32[]{:S(2)}) collective-permute-start(f32[12,32,256]{2,1,0:T(8,128)S(1)} %constant_dynamic-update-slice_fusion), channel_id=1, source_target_pairs={{1,0},{2,1},{3,2},{4,3},{5,4},{6,5},{7,6},{9,8},{10,9},{11,10},{12... | collective-permute-start | bytes 1179656 | tf_op jit(solution)/shard_map/ppermute | solution.py:42
  35.8 8.7 %collective-permute-start.2 = (f32[12,32,256]{2,1,0:T(8,128)S(1)}, f32[12,32,256]{2,1,0:T(8,128)S(1)}, u32[]{:S(2)}, u32[]{:S(2)}) collective-permute-start(f32[12,32,256]{2,1,0:T(8,128)S(1)} %constant_dynamic-update-slice_fusion), channel_id=1, source_target_pairs={{0,1},{1,2},{2,3},{3,4},{4,5},{5,6},{6,7},{8,9},{9,10},{10,11},{11... | collective-permute-start | bytes 1179656 | tf_op jit(solution)/shard_map/ppermute | solution.py:41
  44.6 37.9 %collective-permute-start.5 = (f32[36,32,256]{2,1,0:T(8,128)S(1)}, f32[36,32,256]{2,1,0:T(8,128)S(1)}, u32[]{:S(2)}, u32[]{:S(2)}) collective-permute-start(f32[36,32,256]{2,1,0:T(8,128)S(1)} %constant_dynamic-update-slice_fusion.3), channel_id=1, source_target_pairs={{32,0},{33,1},{34,2},{35,3},{36,4},{37,5},{38,6},{39,7},{40,8},{41... | collective-permute-start | bytes 3538952 | tf_op jit(solution)/shard_map/ppermute | solution.py:42
  45.9 31.9 %collective-permute-start.4 = (f32[36,32,256]{2,1,0:T(8,128)S(1)}, f32[36,32,256]{2,1,0:T(8,128)S(1)}, u32[]{:S(2)}, u32[]{:S(2)}) collective-permute-start(f32[36,32,256]{2,1,0:T(8,128)S(1)} %constant_dynamic-update-slice_fusion.3), channel_id=1, source_target_pairs={{0,32},{1,33},{2,34},{3,35},{4,36},{5,37},{6,38},{7,39},{8,40},{9,... | collective-permute-start | bytes 3538952 | tf_op jit(solution)/shard_map/ppermute | solution.py:41
  228.6 56.5 %copy-start.1 = (f32[4,32,256]{2,1,0:T(8,128)}, f32[4,32,256]{2,1,0:T(8,128)S(1)}, u32[]{:S(2)}) copy-start(f32[4,32,256]{2,1,0:T(8,128)S(1)} %multiply_subtract_fusion.1) | copy-start | bytes 393220
  228.6 7.6 %collective-permute-start.13 = (f32[4,32,256]{2,1,0:T(8,128)S(1)}, f32[4,32,256]{2,1,0:T(8,128)S(1)}, u32[]{:S(2)}, u32[]{:S(2)}) collective-permute-start(f32[4,32,256]{2,1,0:T(8,128)S(1)} %multiply_subtract_fusion.1), channel_id=1, source_target_pairs={{8,0},{9,1},{10,2},{11,3},{12,4},{13,5},{14,6},{15,7},{16,8},{17,9... | collective-permute-start | bytes 393224 | tf_op jit(solution)/shard_map/ppermute | solution.py:42
  232.3 7.8 %collective-permute-start.12 = (f32[4,32,256]{2,1,0:T(8,128)S(1)}, f32[4,32,256]{2,1,0:T(8,128)S(1)}, u32[]{:S(2)}, u32[]{:S(2)}) collective-permute-start(f32[4,32,256]{2,1,0:T(8,128)S(1)} %multiply_subtract_fusion.1), channel_id=1, source_target_pairs={{0,8},{1,9},{2,10},{3,11},{4,12},{5,13},{6,14},{7,15},{8,16},{9,17... | collective-permute-start | bytes 393224 | tf_op jit(solution)/shard_map/ppermute | solution.py:41
  240.1 9.6 %collective-permute-start.14 = (f32[12,32,256]{2,1,0:T(8,128)S(1)}, f32[12,32,256]{2,1,0:T(8,128)S(1)}, u32[]{:S(2)}, u32[]{:S(2)}) collective-permute-start(f32[12,32,256]{2,1,0:T(8,128)S(1)} %pad_maximum_fusion), channel_id=1, source_target_pairs={{0,1},{1,2},{2,3},{3,4},{4,5},{5,6},{6,7},{8,9},{9,10},{10,11},{11... | collective-permute-start | bytes 1179656 | tf_op jit(solution)/shard_map/ppermute | solution.py:41
  241.4 12.4 %collective-permute-start.15 = (f32[12,32,256]{2,1,0:T(8,128)S(1)}, f32[12,32,256]{2,1,0:T(8,128)S(1)}, u32[]{:S(2)}, u32[]{:S(2)}) collective-permute-start(f32[12,32,256]{2,1,0:T(8,128)S(1)} %pad_maximum_fusion), channel_id=1, source_target_pairs={{1,0},{2,1},{3,2},{4,3},{5,4},{6,5},{7,6},{9,8},{10,9},{11,10},{12... | collective-permute-start | bytes 1179656 | tf_op jit(solution)/shard_map/ppermute | solution.py:42
  253.9 26.5 %collective-permute-start.16 = (f32[36,32,256]{2,1,0:T(8,128)S(1)}, f32[36,32,256]{2,1,0:T(8,128)S(1)}, u32[]{:S(2)}, u32[]{:S(2)}) collective-permute-start(f32[36,32,256]{2,1,0:T(8,128)S(1)} %constant_dynamic-update-slice_fusion.30), channel_id=1, source_target_pairs={{0,32},{1,33},{2,34},{3,35},{4,36},{5,37},{6,38},{7,39},{8,40},{9,... | collective-permute-start | bytes 3538952 | tf_op jit(solution)/shard_map/ppermute | solution.py:41
  255.2 29.9 %collective-permute-start.17 = (f32[36,32,256]{2,1,0:T(8,128)S(1)}, f32[36,32,256]{2,1,0:T(8,128)S(1)}, u32[]{:S(2)}, u32[]{:S(2)}) collective-permute-start(f32[36,32,256]{2,1,0:T(8,128)S(1)} %constant_dynamic-update-slice_fusion.30), channel_id=1, source_target_pairs={{32,0},{33,1},{34,2},{35,3},{36,4},{37,5},{38,6},{39,7},{40,8},{41... | collective-permute-start | bytes 3538952 | tf_op jit(solution)/shard_map/ppermute | solution.py:42

commit v2 on v1

--- a/solution.py
+++ b/solution.py
@@ -69,6 +69,15 @@
     return (positions, present)
 
 
+def all_sum(value):
+    total = lax.axis_size("leaf") * lax.axis_size("sub")
+    bit = 1
+    while bit < total:
+        value = value + lax.ppermute(value, AXES, [(i, i ^ bit) for i in range(total)])
+        bit *= 2
+    return value
+
+
 def column_sums(first, second):
     return jnp.sum(first * second, axis=(0, 2))
 
@@ -101,16 +110,15 @@
     residual0 = right_side
     direction0 = right_side
     image0 = operate(direction0)
-    first = lax.psum(
-        jnp.stack([column_sums(residual0, residual0), column_sums(direction0, image0)]),
-        AXES,
+    first = all_sum(
+        jnp.stack([column_sums(residual0, residual0), column_sums(direction0, image0)])
     )
     norm0, curve0 = first[0], first[1]
     step0 = norm0 / curve0
     solution_field = spread(step0) * direction0
     residual1 = residual0 - spread(step0) * image0
     image_res = operate(residual1)
-    second = lax.psum(
+    second = all_sum(
         jnp.stack(
             [
                 column_sums(residual1, residual1),
@@ -118,8 +126,7 @@
                 column_sums(residual1, image0),
                 column_sums(direction0, image_res),
             ]
-        ),
-        AXES,
+        )
     )
     norm1 = second[0]
     ratio = norm1 / norm0

time: 419 us -> 342 us (0.82)
  blocking collectives: 225 us -> 0 us
  starting transfers between devices: 48.4 us -> 165 us
  waiting for transfers between devices: 44.8 us -> 72.1 us
    psum x2 -> x0, blocking collectives: 225 us -> none  [the longest x1 120 us: per_device(): lax.psum(jnp.stack([column_sums(residual0, residual0), column_sums(direct...]
    ppermute x0 -> x18, starting transfers between devices: none -> 111 us  [all_sum(): lax.ppermute(value, AXES, [(i, i ^ bit) for i in range(total)])]
    ppermute x0 -> x18, waiting for transfers between devices: none -> 26.5 us  [all_sum(): lax.ppermute(value, AXES, [(i, i ^ bit) for i in range(total)])]
    unnamed x40 -> x44, local copies, waits for them, and re-layouts: 13.5 us -> 13.6 us
  transfers between devices with their start and end apart: 18 -> 36, of which waited for: 7 -> 24; matrix products, arithmetic and copies ran while one was open for 11% -> 13% of each run, Pallas kernels for 0% -> 0%
where the time goes in v2:
time: 342 us; the launch traced here: 337 us
  starting transfers between devices  165 us (48%)
  waiting for transfers between devices  72.1 us (21%)
  matrix products  41.7 us (12%)
  other arithmetic  33.1 us (10%)
  local copies, waits for them, and re-layouts  23.5 us (7%)
    ppermute x18, starting transfers between devices, all_sum(): lax.ppermute(value, AXES, [(i, i ^ bit) for i in range(total)])  111 us
    dot_general x2, matrix products, operate(): jnp.einsum('bmrj,bmji->bri', near_values, kernel, precision=lax.Precision...  41.7 us
    ppermute x9, waiting for transfers between devices, collect_halo(): lower = lax.ppermute(current, AXES, neighbour_route(shape, dim, -1))  38.9 us
    ppermute x9, starting transfers between devices, collect_halo(): upper = lax.ppermute(current, AXES, neighbour_route(shape, dim, 1))  29.5 us
    mul x1, other arithmetic, per_device(): kernel = jax.vmap(wendland)(points, others) * present[:, :, None, None]  27.8 us
    ppermute x18, waiting for transfers between devices, all_sum(): lax.ppermute(value, AXES, [(i, i ^ bit) for i in range(total)])  26.5 us
    ppermute x9, starting transfers between devices, collect_halo(): lower = lax.ppermute(current, AXES, neighbour_route(shape, dim, -1))  24.5 us
    unnamed x44, local copies, waits for them, and re-layouts  13.6 us
  transfers between devices with their start and end apart: 36, of which 24 were waited for; matrix products, arithmetic and copies ran while one was open for 13% of the time, Pallas kernels for 0%

profile of v2, /device:TPU:1, one launch (start us, length us, event | category | flops | bytes accessed | tf_op | source)
XLA Modules:
  0.0 336.7 jit_solution(3673034645874916273)
XLA Ops:
  1.4 6.0 %collective-permute-start.7 = (f32[4,3,256]{2,1,0:T(4,128)S(1)}, f32[4,3,256]{2,1,0:T(4,128)S(1)}, u32[]{:S(2)}, u32[]{:S(2)}) collective-permute-start(f32[4,3,256]{2,1,0:T(4,128)S(1)} %copy.5), channel_id=1, source_target_pairs={{8,0},{9,1},{10,2},{11,3},{12,4},{13,5},{14,6},{15,7},{16,8},{17,9... | collective-permute-start | bytes 36872 | tf_op jit(solution)/shard_map/ppermute | solution.py:42
  9.3 7.8 %collective-permute-start.1 = (f32[4,32,256]{2,1,0:T(8,128)}, f32[4,32,256]{2,1,0:T(8,128)S(1)}, u32[]{:S(2)}, u32[]{:S(2)}) collective-permute-start(f32[4,32,256]{2,1,0:T(8,128)} %param.3), channel_id=1, source_target_pairs={{8,0},{9,1},{10,2},{11,3},{12,4},{13,5},{14,6},{15,7},{16,8},{17,9... | collective-permute-start | bytes 393224 | tf_op jit(solution)/shard_map/ppermute | solution.py:42
  29.5 4.0 %collective-permute-start.10 = (f32[36,3,256]{2,1,0:T(4,128)S(1)}, f32[36,3,256]{2,1,0:T(4,128)S(1)}, u32[]{:S(2)}, u32[]{:S(2)}) collective-permute-start(f32[36,3,256]{2,1,0:T(4,128)S(1)} %constant_dynamic-update-slice_fusion.18), channel_id=1, source_target_pairs={{0,32},{1,33},{2,34},{3,35},{4,36},{5,37},{6,38},{7,39},{8,40},{9,... | collective-permute-start | bytes 331784 | tf_op jit(solution)/shard_map/ppermute | solution.py:41
  35.8 4.0 %collective-permute-start.2 = (f32[12,32,256]{2,1,0:T(8,128)S(1)}, f32[12,32,256]{2,1,0:T(8,128)S(1)}, u32[]{:S(2)}, u32[]{:S(2)}) collective-permute-start(f32[12,32,256]{2,1,0:T(8,128)S(1)} %constant_dynamic-update-slice_fusion), channel_id=1, source_target_pairs={{0,1},{1,2},{2,3},{3,4},{4,5},{5,6},{6,7},{8,9},{9,10},{10,11},{11... | collective-permute-start | bytes 1179656 | tf_op jit(solution)/shard_map/ppermute | solution.py:41
  45.9 4.1 %collective-permute-start.4 = (f32[36,32,256]{2,1,0:T(8,128)S(1)}, f32[36,32,256]{2,1,0:T(8,128)S(1)}, u32[]{:S(2)}, u32[]{:S(2)}) collective-permute-start(f32[36,32,256]{2,1,0:T(8,128)S(1)} %constant_dynamic-update-slice_fusion.3), channel_id=1, source_target_pairs={{0,32},{1,33},{2,34},{3,35},{4,36},{5,37},{6,38},{7,39},{8,40},{9,... | collective-permute-start | bytes 3538952 | tf_op jit(solution)/shard_map/ppermute | solution.py:41
  50.0 27.8 %fusion.1 = f32[4,27,256,256]{3,2,1,0:T(8,128)} fusion(f32[4,27]{1,0:T(4,128)S(1)} %compare_convert_fusion, f32[4,256]{1,0:T(4,128)S(1)} %get-tuple-element.16, f32[4,27,256]{2,1,0:T(8,128)S(1)} %get-tuple-element.20, f32[4,256]{1,0:T(4,128)S(1)} %get-tuple-element.17, f32[4,27,256]{2,1,0:T(8,128)S(1)} %get-tuple-element.21, ...), kind=kLoop, calls=%fused_computation.5 | loop fusion | flops 127401984 | bytes 28656048 | tf_op jit(solution)/shard_map/mul | solution.py:95
  83.7 2.8 gather_fusion
  86.5 20.8 %multiply_reduce_fusion.5 = (f32[32]{0:T(128)S(1)}, f32[32]{0:T(128)S(1)}, f32[4,32,256]{2,1,0:T(8,128)}) fusion(f32[4,32,256]{2,1,0:T(8,128)} %param.3, f32[4,27,32,256]{3,2,1,0:T(8,128)S(1)} %bitcast.63, f32[4,27,256,256]{3,2,1,0:T(8,128)} %fusion.1), kind=kOutput, calls=%fused_computation.24 | convolution fusion | flops 2718138368 | bytes 32112896 | tf_op jit(solution)/shard_map/bmrj,bmji->bri/dot_general | solution.py:101
  107.3 4.1 %collective-permute-start.12 = (f32[2,32]{1,0:T(2,128)S(1)}, f32[2,32]{1,0:T(2,128)S(1)}, u32[]{:S(2)}, u32[]{:S(2)}) collective-permute-start(f32[2,32]{1,0:T(2,128)S(1)} %pad_maximum_fusion.2), channel_id=1, source_target_pairs={{0,1},{1,0},{2,3},{3,2},{4,5},{5,4},{6,7},{7,6},{8,9},{9,8},{10,11... | collective-permute-start | bytes 776 | tf_op jit(solution)/shard_map/ppermute | solution.py:76
  112.4 6.5 %collective-permute-start.13 = (f32[2,32]{1,0:T(2,128)S(1)}, f32[2,32]{1,0:T(2,128)S(1)}, u32[]{:S(2)}, u32[]{:S(2)}) collective-permute-start(f32[2,32]{1,0:T(2,128)S(1)} %fusion.25), channel_id=1, source_target_pairs={{0,2},{1,3},{2,0},{3,1},{4,6},{5,7},{6,4},{7,5},{8,10},{9,11},{10,... | collective-permute-start | bytes 776 | tf_op jit(solution)/shard_map/ppermute | solution.py:76
  119.8 6.8 %collective-permute-start.14 = (f32[2,32]{1,0:T(2,128)S(1)}, f32[2,32]{1,0:T(2,128)S(1)}, u32[]{:S(2)}, u32[]{:S(2)}) collective-permute-start(f32[2,32]{1,0:T(2,128)S(1)} %fusion.33), channel_id=1, source_target_pairs={{0,4},{1,5},{2,6},{3,7},{4,0},{5,1},{6,2},{7,3},{8,12},{9,13},{10,... | collective-permute-start | bytes 776 | tf_op jit(solution)/shard_map/ppermute | solution.py:76
  129.7 3.6 %collective-permute-done.15 = f32[2,32]{1,0:T(2,128)S(1)} collective-permute-done((f32[2,32]{1,0:T(2,128)S(1)}, f32[2,32]{1,0:T(2,128)S(1)}, u32[]{:S(2)}, u32[]{:S(2)}) %collective-permute-start.15) | collective-permute-done | bytes 288 | tf_op jit(solution)/shard_map/ppermute | solution.py:76
  133.3 11.6 %collective-permute-start.16 = (f32[2,32]{1,0:T(2,128)S(1)}, f32[2,32]{1,0:T(2,128)S(1)}, u32[]{:S(2)}, u32[]{:S(2)}) collective-permute-start(f32[2,32]{1,0:T(2,128)S(1)} %add.174), channel_id=1, source_target_pairs={{0,16},{1,17},{2,18},{3,19},{4,20},{5,21},{6,22},{7,23},{8,24},{9,... | collective-permute-start | bytes 776 | tf_op jit(solution)/shard_map/ppermute | solution.py:76
  145.8 3.5 %collective-permute-start.17 = (f32[2,32]{1,0:T(2,128)S(1)}, f32[2,32]{1,0:T(2,128)S(1)}, u32[]{:S(2)}, u32[]{:S(2)}) collective-permute-start(f32[2,32]{1,0:T(2,128)S(1)} %add.175), channel_id=1, source_target_pairs={{0,32},{1,33},{2,34},{3,35},{4,36},{5,37},{6,38},{7,39},{8,40},{9,... | collective-permute-start | bytes 776 | tf_op jit(solution)/shard_map/ppermute | solution.py:76
  150.2 7.3 %collective-permute-start.18 = (f32[2,32]{1,0:T(2,128)S(1)}, f32[2,32]{1,0:T(2,128)S(1)}, u32[]{:S(2)}, u32[]{:S(2)}) collective-permute-start(f32[2,32]{1,0:T(2,128)S(1)} %add.176), channel_id=1, source_target_pairs={{0,64},{1,65},{2,66},{3,67},{4,68},{5,69},{6,70},{7,71},{8,72},{9,... | collective-permute-start | bytes 776 | tf_op jit(solution)/shard_map/ppermute | solution.py:76
  158.5 8.8 %collective-permute-start.19 = (f32[2,32]{1,0:T(2,128)S(1)}, f32[2,32]{1,0:T(2,128)S(1)}, u32[]{:S(2)}, u32[]{:S(2)}) collective-permute-start(f32[2,32]{1,0:T(2,128)S(1)} %add.177), channel_id=1, source_target_pairs={{0,128},{1,129},{2,130},{3,131},{4,132},{5,133},{6,134},{7,135},{8... | collective-permute-start | bytes 776 | tf_op jit(solution)/shard_map/ppermute | solution.py:76
  168.2 11.2 %collective-permute-start.20 = (f32[2,32]{1,0:T(2,128)S(1)}, f32[2,32]{1,0:T(2,128)S(1)}, u32[]{:S(2)}, u32[]{:S(2)}) collective-permute-start(f32[2,32]{1,0:T(2,128)S(1)} %add.178), channel_id=1, source_target_pairs={{0,256},{1,257},{2,258},{3,259},{4,260},{5,261},{6,262},{7,263},{8... | collective-permute-start | bytes 776 | tf_op jit(solution)/shard_map/ppermute | solution.py:76
  182.3 7.8 %collective-permute-start.22 = (f32[4,32,256]{2,1,0:T(8,128)S(1)}, f32[4,32,256]{2,1,0:T(8,128)S(1)}, u32[]{:S(2)}, u32[]{:S(2)}) collective-permute-start(f32[4,32,256]{2,1,0:T(8,128)S(1)} %multiply_subtract_fusion.1), channel_id=1, source_target_pairs={{8,0},{9,1},{10,2},{11,3},{12,4},{13,5},{14,6},{15,7},{16,8},{17,9... | collective-permute-start | bytes 393224 | tf_op jit(solution)/shard_map/ppermute | solution.py:42
  192.1 5.8 %collective-permute-done.21 = f32[4,32,256]{2,1,0:T(8,128)S(1)} collective-permute-done((f32[4,32,256]{2,1,0:T(8,128)S(1)}, f32[4,32,256]{2,1,0:T(8,128)S(1)}, u32[]{:S(2)}, u32[]{:S(2)}) %collective-permute-start.21) | collective-permute-done | bytes 131104 | tf_op jit(solution)/shard_map/ppermute | solution.py:41
  200.9 6.4 %collective-permute-done.23 = f32[12,32,256]{2,1,0:T(8,128)S(1)} collective-permute-done((f32[12,32,256]{2,1,0:T(8,128)S(1)}, f32[12,32,256]{2,1,0:T(8,128)S(1)}, u32[]{:S(2)}, u32[]{:S(2)}) %collective-permute-start.23) | collective-permute-done | bytes 393248 | tf_op jit(solution)/shard_map/ppermute | solution.py:41
  207.4 4.0 %collective-permute-done.24 = f32[12,32,256]{2,1,0:T(8,128)S(1)} collective-permute-done((f32[12,32,256]{2,1,0:T(8,128)S(1)}, f32[12,32,256]{2,1,0:T(8,128)S(1)}, u32[]{:S(2)}, u32[]{:S(2)}) %collective-permute-start.24) | collective-permute-done | bytes 393248 | tf_op jit(solution)/shard_map/ppermute | solution.py:42
  211.5 3.7 %collective-permute-start.25 = (f32[36,32,256]{2,1,0:T(8,128)S(1)}, f32[36,32,256]{2,1,0:T(8,128)S(1)}, u32[]{:S(2)}, u32[]{:S(2)}) collective-permute-start(f32[36,32,256]{2,1,0:T(8,128)S(1)} %constant_dynamic-update-slice_fusion.30), channel_id=1, source_target_pairs={{0,32},{1,33},{2,34},{3,35},{4,36},{5,37},{6,38},{7,39},{8,40},{9,... | collective-permute-start | bytes 3538952 | tf_op jit(solution)/shard_map/ppermute | solution.py:41
  216.7 24.0 %collective-permute-done.25 = f32[36,32,256]{2,1,0:T(8,128)S(1)} collective-permute-done((f32[36,32,256]{2,1,0:T(8,128)S(1)}, f32[36,32,256]{2,1,0:T(8,128)S(1)}, u32[]{:S(2)}, u32[]{:S(2)}) %collective-permute-start.25) | collective-permute-done | bytes 1179680 | tf_op jit(solution)/shard_map/ppermute | solution.py:41
  246.6 2.8 gather_fusion.2
  249.3 20.8 %multiply_reduce_fusion.3 = (f32[32]{0:T(128)S(1)}, f32[32]{0:T(128)S(1)}, f32[32]{0:T(128)S(1)}, f32[32]{0:T(128)S(1)}, f32[4,32,256]{2,1,0:T(8,128)}) fusion(f32[4,32,256]{2,1,0:T(8,128)} %copy-done.1, f32[4,32,256]{2,1,0:T(8,128)} %get-tuple-element.18, f32[4,32,256]{2,1,0:T(8,128)} %param.3, f32[4,27,32,256]{3,2,1,0:T(8,128)S(1)} %bitcast.64, ...), kind=kOutput, calls=%fused_computation.21 | convolution fusion | flops 2718269440 | bytes 32375296 | tf_op jit(solution)/shard_map/bmrj,bmji->bri/dot_general | solution.py:101
  274.5 7.5 %collective-permute-start.28 = (f32[4,32]{1,0:T(4,128)S(1)}, f32[4,32]{1,0:T(4,128)S(1)}, u32[]{:S(2)}, u32[]{:S(2)}) collective-permute-start(f32[4,32]{1,0:T(4,128)S(1)} %fusion.26), channel_id=1, source_target_pairs={{0,2},{1,3},{2,0},{3,1},{4,6},{5,7},{6,4},{7,5},{8,10},{9,11},{10,... | collective-permute-start | bytes 1544 | tf_op jit(solution)/shard_map/ppermute | solution.py:76
  289.3 3.9 %collective-permute-done.30 = f32[4,32]{1,0:T(4,128)S(1)} collective-permute-done((f32[4,32]{1,0:T(4,128)S(1)}, f32[4,32]{1,0:T(4,128)S(1)}, u32[]{:S(2)}, u32[]{:S(2)}) %collective-permute-start.30) | collective-permute-done | bytes 544 | tf_op jit(solution)/shard_map/ppermute | solution.py:76
  293.2 7.2 %collective-permute-start.31 = (f32[4,32]{1,0:T(4,128)S(1)}, f32[4,32]{1,0:T(4,128)S(1)}, u32[]{:S(2)}, u32[]{:S(2)}) collective-permute-start(f32[4,32]{1,0:T(4,128)S(1)} %add.184), channel_id=1, source_target_pairs={{0,16},{1,17},{2,18},{3,19},{4,20},{5,21},{6,22},{7,23},{8,24},{9,... | collective-permute-start | bytes 1544 | tf_op jit(solution)/shard_map/ppermute | solution.py:76
  301.2 4.1 %collective-permute-start.32 = (f32[4,32]{1,0:T(4,128)S(1)}, f32[4,32]{1,0:T(4,128)S(1)}, u32[]{:S(2)}, u32[]{:S(2)}) collective-permute-start(f32[4,32]{1,0:T(4,128)S(1)} %add.185), channel_id=1, source_target_pairs={{0,32},{1,33},{2,34},{3,35},{4,36},{5,37},{6,38},{7,39},{8,40},{9,... | collective-permute-start | bytes 1544 | tf_op jit(solution)/shard_map/ppermute | solution.py:76
  306.3 4.7 %collective-permute-start.33 = (f32[4,32]{1,0:T(4,128)S(1)}, f32[4,32]{1,0:T(4,128)S(1)}, u32[]{:S(2)}, u32[]{:S(2)}) collective-permute-start(f32[4,32]{1,0:T(4,128)S(1)} %add.186), channel_id=1, source_target_pairs={{0,64},{1,65},{2,66},{3,67},{4,68},{5,69},{6,70},{7,71},{8,72},{9,... | collective-permute-start | bytes 1544 | tf_op jit(solution)/shard_map/ppermute | solution.py:76
  312.0 8.0 %collective-permute-start.34 = (f32[4,32]{1,0:T(4,128)S(1)}, f32[4,32]{1,0:T(4,128)S(1)}, u32[]{:S(2)}, u32[]{:S(2)}) collective-permute-start(f32[4,32]{1,0:T(4,128)S(1)} %add.187), channel_id=1, source_target_pairs={{0,128},{1,129},{2,130},{3,131},{4,132},{5,133},{6,134},{7,135},{8... | collective-permute-start | bytes 1544 | tf_op jit(solution)/shard_map/ppermute | solution.py:76
  321.0 11.2 %collective-permute-start.35 = (f32[4,32]{1,0:T(4,128)S(1)}, f32[4,32]{1,0:T(4,128)S(1)}, u32[]{:S(2)}, u32[]{:S(2)}) collective-permute-start(f32[4,32]{1,0:T(4,128)S(1)} %add.188), channel_id=1, source_target_pairs={{0,256},{1,257},{2,258},{3,259},{4,260},{5,261},{6,262},{7,263},{8... | collective-permute-start | bytes 1544 | tf_op jit(solution)/shard_map/ppermute | solution.py:76
  (130 shorter events, 72.8 us)
Async XLA Ops:
  1.4 20.6 %collective-permute-start.7 = (f32[4,3,256]{2,1,0:T(4,128)S(1)}, f32[4,3,256]{2,1,0:T(4,128)S(1)}, u32[]{:S(2)}, u32[]{:S(2)}) collective-permute-start(f32[4,3,256]{2,1,0:T(4,128)S(1)} %copy.5), channel_id=1, source_target_pairs={{8,0},{9,1},{10,2},{11,3},{12,4},{13,5},{14,6},{15,7},{16,8},{17,9... | collective-permute-start | bytes 36872 | tf_op jit(solution)/shard_map/ppermute | solution.py:42
  7.4 13.9 %collective-permute-start.6 = (f32[4,3,256]{2,1,0:T(4,128)S(1)}, f32[4,3,256]{2,1,0:T(4,128)S(1)}, u32[]{:S(2)}, u32[]{:S(2)}) collective-permute-start(f32[4,3,256]{2,1,0:T(4,128)S(1)} %copy.5), channel_id=1, source_target_pairs={{0,8},{1,9},{2,10},{3,11},{4,12},{5,13},{6,14},{7,15},{8,16},{9,17... | collective-permute-start | bytes 36872 | tf_op jit(solution)/shard_map/ppermute | solution.py:41
  9.3 25.1 %collective-permute-start.1 = (f32[4,32,256]{2,1,0:T(8,128)}, f32[4,32,256]{2,1,0:T(8,128)S(1)}, u32[]{:S(2)}, u32[]{:S(2)}) collective-permute-start(f32[4,32,256]{2,1,0:T(8,128)} %param.3), channel_id=1, source_target_pairs={{8,0},{9,1},{10,2},{11,3},{12,4},{13,5},{14,6},{15,7},{16,8},{17,9... | collective-permute-start | bytes 393224 | tf_op jit(solution)/shard_map/ppermute | solution.py:42
  17.1 16.4 %collective-permute-start = (f32[4,32,256]{2,1,0:T(8,128)}, f32[4,32,256]{2,1,0:T(8,128)S(1)}, u32[]{:S(2)}, u32[]{:S(2)}) collective-permute-start(f32[4,32,256]{2,1,0:T(8,128)} %param.3), channel_id=1, source_target_pairs={{0,8},{1,9},{2,10},{3,11},{4,12},{5,13},{6,14},{7,15},{8,16},{9,17... | collective-permute-start | bytes 393224 | tf_op jit(solution)/shard_map/ppermute | solution.py:41
  23.3 4.8 %collective-permute-start.9 = (f32[12,3,256]{2,1,0:T(4,128)S(1)}, f32[12,3,256]{2,1,0:T(4,128)S(1)}, u32[]{:S(2)}, u32[]{:S(2)}) collective-permute-start(f32[12,3,256]{2,1,0:T(4,128)S(1)} %constant_dynamic-update-slice_fusion.15), channel_id=1, source_target_pairs={{1,0},{2,1},{3,2},{4,3},{5,4},{6,5},{7,6},{9,8},{10,9},{11,10},{12... | collective-permute-start | bytes 110600 | tf_op jit(solution)/shard_map/ppermute | solution.py:42
  28.2 12.4 %collective-permute-start.11 = (f32[36,3,256]{2,1,0:T(4,128)S(1)}, f32[36,3,256]{2,1,0:T(4,128)S(1)}, u32[]{:S(2)}, u32[]{:S(2)}) collective-permute-start(f32[36,3,256]{2,1,0:T(4,128)S(1)} %constant_dynamic-update-slice_fusion.18), channel_id=1, source_target_pairs={{32,0},{33,1},{34,2},{35,3},{36,4},{37,5},{38,6},{39,7},{40,8},{41... | collective-permute-start | bytes 331784 | tf_op jit(solution)/shard_map/ppermute | solution.py:42
  29.5 10.3 %collective-permute-start.10 = (f32[36,3,256]{2,1,0:T(4,128)S(1)}, f32[36,3,256]{2,1,0:T(4,128)S(1)}, u32[]{:S(2)}, u32[]{:S(2)}) collective-permute-start(f32[36,3,256]{2,1,0:T(4,128)S(1)} %constant_dynamic-update-slice_fusion.18), channel_id=1, source_target_pairs={{0,32},{1,33},{2,34},{3,35},{4,36},{5,37},{6,38},{7,39},{8,40},{9,... | collective-permute-start | bytes 331784 | tf_op jit(solution)/shard_map/ppermute | solution.py:41
  34.5 10.1 %collective-permute-start.3 = (f32[12,32,256]{2,1,0:T(8,128)S(1)}, f32[12,32,256]{2,1,0:T(8,128)S(1)}, u32[]{:S(2)}, u32[]{:S(2)}) collective-permute-start(f32[12,32,256]{2,1,0:T(8,128)S(1)} %constant_dynamic-update-slice_fusion), channel_id=1, source_target_pairs={{1,0},{2,1},{3,2},{4,3},{5,4},{6,5},{7,6},{9,8},{10,9},{11,10},{12... | collective-permute-start | bytes 1179656 | tf_op jit(solution)/shard_map/ppermute | solution.py:42
  35.8 8.7 %collective-permute-start.2 = (f32[12,32,256]{2,1,0:T(8,128)S(1)}, f32[12,32,256]{2,1,0:T(8,128)S(1)}, u32[]{:S(2)}, u32[]{:S(2)}) collective-permute-start(f32[12,32,256]{2,1,0:T(8,128)S(1)} %constant_dynamic-update-slice_fusion), channel_id=1, source_target_pairs={{0,1},{1,2},{2,3},{3,4},{4,5},{5,6},{6,7},{8,9},{9,10},{10,11},{11... | collective-permute-start | bytes 1179656 | tf_op jit(solution)/shard_map/ppermute | solution.py:41
  44.6 37.9 %collective-permute-start.5 = (f32[36,32,256]{2,1,0:T(8,128)S(1)}, f32[36,32,256]{2,1,0:T(8,128)S(1)}, u32[]{:S(2)}, u32[]{:S(2)}) collective-permute-start(f32[36,32,256]{2,1,0:T(8,128)S(1)} %constant_dynamic-update-slice_fusion.3), channel_id=1, source_target_pairs={{32,0},{33,1},{34,2},{35,3},{36,4},{37,5},{38,6},{39,7},{40,8},{41... | collective-permute-start | bytes 3538952 | tf_op jit(solution)/shard_map/ppermute | solution.py:42
  45.9 31.8 %collective-permute-start.4 = (f32[36,32,256]{2,1,0:T(8,128)S(1)}, f32[36,32,256]{2,1,0:T(8,128)S(1)}, u32[]{:S(2)}, u32[]{:S(2)}) collective-permute-start(f32[36,32,256]{2,1,0:T(8,128)S(1)} %constant_dynamic-update-slice_fusion.3), channel_id=1, source_target_pairs={{0,32},{1,33},{2,34},{3,35},{4,36},{5,37},{6,38},{7,39},{8,40},{9,... | collective-permute-start | bytes 3538952 | tf_op jit(solution)/shard_map/ppermute | solution.py:41
  107.3 5.1 %collective-permute-start.12 = (f32[2,32]{1,0:T(2,128)S(1)}, f32[2,32]{1,0:T(2,128)S(1)}, u32[]{:S(2)}, u32[]{:S(2)}) collective-permute-start(f32[2,32]{1,0:T(2,128)S(1)} %pad_maximum_fusion.2), channel_id=1, source_target_pairs={{0,1},{1,0},{2,3},{3,2},{4,5},{5,4},{6,7},{7,6},{8,9},{9,8},{10,11... | collective-permute-start | bytes 776 | tf_op jit(solution)/shard_map/ppermute | solution.py:76
  112.4 7.4 %collective-permute-start.13 = (f32[2,32]{1,0:T(2,128)S(1)}, f32[2,32]{1,0:T(2,128)S(1)}, u32[]{:S(2)}, u32[]{:S(2)}) collective-permute-start(f32[2,32]{1,0:T(2,128)S(1)} %fusion.25), channel_id=1, source_target_pairs={{0,2},{1,3},{2,0},{3,1},{4,6},{5,7},{6,4},{7,5},{8,10},{9,11},{10,... | collective-permute-start | bytes 776 | tf_op jit(solution)/shard_map/ppermute | solution.py:76
  119.8 7.7 %collective-permute-start.14 = (f32[2,32]{1,0:T(2,128)S(1)}, f32[2,32]{1,0:T(2,128)S(1)}, u32[]{:S(2)}, u32[]{:S(2)}) collective-permute-start(f32[2,32]{1,0:T(2,128)S(1)} %fusion.33), channel_id=1, source_target_pairs={{0,4},{1,5},{2,6},{3,7},{4,0},{5,1},{6,2},{7,3},{8,12},{9,13},{10,... | collective-permute-start | bytes 776 | tf_op jit(solution)/shard_map/ppermute | solution.py:76
  127.5 5.8 %collective-permute-start.15 = (f32[2,32]{1,0:T(2,128)S(1)}, f32[2,32]{1,0:T(2,128)S(1)}, u32[]{:S(2)}, u32[]{:S(2)}) collective-permute-start(f32[2,32]{1,0:T(2,128)S(1)} %add.173), channel_id=1, source_target_pairs={{0,8},{1,9},{2,10},{3,11},{4,12},{5,13},{6,14},{7,15},{8,0},{9,1},... | collective-permute-start | bytes 776 | tf_op jit(solution)/shard_map/ppermute | solution.py:76
  133.3 12.4 %collective-permute-start.16 = (f32[2,32]{1,0:T(2,128)S(1)}, f32[2,32]{1,0:T(2,128)S(1)}, u32[]{:S(2)}, u32[]{:S(2)}) collective-permute-start(f32[2,32]{1,0:T(2,128)S(1)} %add.174), channel_id=1, source_target_pairs={{0,16},{1,17},{2,18},{3,19},{4,20},{5,21},{6,22},{7,23},{8,24},{9,... | collective-permute-start | bytes 776 | tf_op jit(solution)/shard_map/ppermute | solution.py:76
  150.2 8.3 %collective-permute-start.18 = (f32[2,32]{1,0:T(2,128)S(1)}, f32[2,32]{1,0:T(2,128)S(1)}, u32[]{:S(2)}, u32[]{:S(2)}) collective-permute-start(f32[2,32]{1,0:T(2,128)S(1)} %add.176), channel_id=1, source_target_pairs={{0,64},{1,65},{2,66},{3,67},{4,68},{5,69},{6,70},{7,71},{8,72},{9,... | collective-permute-start | bytes 776 | tf_op jit(solution)/shard_map/ppermute | solution.py:76
  158.5 9.8 %collective-permute-start.19 = (f32[2,32]{1,0:T(2,128)S(1)}, f32[2,32]{1,0:T(2,128)S(1)}, u32[]{:S(2)}, u32[]{:S(2)}) collective-permute-start(f32[2,32]{1,0:T(2,128)S(1)} %add.177), channel_id=1, source_target_pairs={{0,128},{1,129},{2,130},{3,131},{4,132},{5,133},{6,134},{7,135},{8... | collective-permute-start | bytes 776 | tf_op jit(solution)/shard_map/ppermute | solution.py:76
  168.2 13.0 %collective-permute-start.20 = (f32[2,32]{1,0:T(2,128)S(1)}, f32[2,32]{1,0:T(2,128)S(1)}, u32[]{:S(2)}, u32[]{:S(2)}) collective-permute-start(f32[2,32]{1,0:T(2,128)S(1)} %add.178), channel_id=1, source_target_pairs={{0,256},{1,257},{2,258},{3,259},{4,260},{5,261},{6,262},{7,263},{8... | collective-permute-start | bytes 776 | tf_op jit(solution)/shard_map/ppermute | solution.py:76
  182.3 9.7 %collective-permute-start.22 = (f32[4,32,256]{2,1,0:T(8,128)S(1)}, f32[4,32,256]{2,1,0:T(8,128)S(1)}, u32[]{:S(2)}, u32[]{:S(2)}) collective-permute-start(f32[4,32,256]{2,1,0:T(8,128)S(1)} %multiply_subtract_fusion.1), channel_id=1, source_target_pairs={{8,0},{9,1},{10,2},{11,3},{12,4},{13,5},{14,6},{15,7},{16,8},{17,9... | collective-permute-start | bytes 393224 | tf_op jit(solution)/shard_map/ppermute | solution.py:42
  190.1 7.8 %collective-permute-start.21 = (f32[4,32,256]{2,1,0:T(8,128)S(1)}, f32[4,32,256]{2,1,0:T(8,128)S(1)}, u32[]{:S(2)}, u32[]{:S(2)}) collective-permute-start(f32[4,32,256]{2,1,0:T(8,128)S(1)} %multiply_subtract_fusion.1), channel_id=1, source_target_pairs={{0,8},{1,9},{2,10},{3,11},{4,12},{5,13},{6,14},{7,15},{8,16},{9,17... | collective-permute-start | bytes 393224 | tf_op jit(solution)/shard_map/ppermute | solution.py:41
  198.0 9.4 %collective-permute-start.23 = (f32[12,32,256]{2,1,0:T(8,128)S(1)}, f32[12,32,256]{2,1,0:T(8,128)S(1)}, u32[]{:S(2)}, u32[]{:S(2)}) collective-permute-start(f32[12,32,256]{2,1,0:T(8,128)S(1)} %pad_maximum_fusion), channel_id=1, source_target_pairs={{0,1},{1,2},{2,3},{3,4},{4,5},{5,6},{6,7},{8,9},{9,10},{10,11},{11... | collective-permute-start | bytes 1179656 | tf_op jit(solution)/shard_map/ppermute | solution.py:41
  199.6 11.8 %collective-permute-start.24 = (f32[12,32,256]{2,1,0:T(8,128)S(1)}, f32[12,32,256]{2,1,0:T(8,128)S(1)}, u32[]{:S(2)}, u32[]{:S(2)}) collective-permute-start(f32[12,32,256]{2,1,0:T(8,128)S(1)} %pad_maximum_fusion), channel_id=1, source_target_pairs={{1,0},{2,1},{3,2},{4,3},{5,4},{6,5},{7,6},{9,8},{10,9},{11,10},{12... | collective-permute-start | bytes 1179656 | tf_op jit(solution)/shard_map/ppermute | solution.py:42
  211.5 29.2 %collective-permute-start.25 = (f32[36,32,256]{2,1,0:T(8,128)S(1)}, f32[36,32,256]{2,1,0:T(8,128)S(1)}, u32[]{:S(2)}, u32[]{:S(2)}) collective-permute-start(f32[36,32,256]{2,1,0:T(8,128)S(1)} %constant_dynamic-update-slice_fusion.30), channel_id=1, source_target_pairs={{0,32},{1,33},{2,34},{3,35},{4,36},{5,37},{6,38},{7,39},{8,40},{9,... | collective-permute-start | bytes 3538952 | tf_op jit(solution)/shard_map/ppermute | solution.py:41
  215.2 30.2 %collective-permute-start.26 = (f32[36,32,256]{2,1,0:T(8,128)S(1)}, f32[36,32,256]{2,1,0:T(8,128)S(1)}, u32[]{:S(2)}, u32[]{:S(2)}) collective-permute-start(f32[36,32,256]{2,1,0:T(8,128)S(1)} %constant_dynamic-update-slice_fusion.30), channel_id=1, source_target_pairs={{32,0},{33,1},{34,2},{35,3},{36,4},{37,5},{38,6},{39,7},{40,8},{41... | collective-permute-start | bytes 3538952 | tf_op jit(solution)/shard_map/ppermute | solution.py:42
  274.5 8.5 %collective-permute-start.28 = (f32[4,32]{1,0:T(4,128)S(1)}, f32[4,32]{1,0:T(4,128)S(1)}, u32[]{:S(2)}, u32[]{:S(2)}) collective-permute-start(f32[4,32]{1,0:T(4,128)S(1)} %fusion.26), channel_id=1, source_target_pairs={{0,2},{1,3},{2,0},{3,1},{4,6},{5,7},{6,4},{7,5},{8,10},{9,11},{10,... | collective-permute-start | bytes 1544 | tf_op jit(solution)/shard_map/ppermute | solution.py:76
  287.4 5.8 %collective-permute-start.30 = (f32[4,32]{1,0:T(4,128)S(1)}, f32[4,32]{1,0:T(4,128)S(1)}, u32[]{:S(2)}, u32[]{:S(2)}) collective-permute-start(f32[4,32]{1,0:T(4,128)S(1)} %add.183), channel_id=1, source_target_pairs={{0,8},{1,9},{2,10},{3,11},{4,12},{5,13},{6,14},{7,15},{8,0},{9,1},... | collective-permute-start | bytes 1544 | tf_op jit(solution)/shard_map/ppermute | solution.py:76
  293.2 8.0 %collective-permute-start.31 = (f32[4,32]{1,0:T(4,128)S(1)}, f32[4,32]{1,0:T(4,128)S(1)}, u32[]{:S(2)}, u32[]{:S(2)}) collective-permute-start(f32[4,32]{1,0:T(4,128)S(1)} %add.184), channel_id=1, source_target_pairs={{0,16},{1,17},{2,18},{3,19},{4,20},{5,21},{6,22},{7,23},{8,24},{9,... | collective-permute-start | bytes 1544 | tf_op jit(solution)/shard_map/ppermute | solution.py:76
  301.2 5.1 %collective-permute-start.32 = (f32[4,32]{1,0:T(4,128)S(1)}, f32[4,32]{1,0:T(4,128)S(1)}, u32[]{:S(2)}, u32[]{:S(2)}) collective-permute-start(f32[4,32]{1,0:T(4,128)S(1)} %add.185), channel_id=1, source_target_pairs={{0,32},{1,33},{2,34},{3,35},{4,36},{5,37},{6,38},{7,39},{8,40},{9,... | collective-permute-start | bytes 1544 | tf_op jit(solution)/shard_map/ppermute | solution.py:76
  306.3 5.7 %collective-permute-start.33 = (f32[4,32]{1,0:T(4,128)S(1)}, f32[4,32]{1,0:T(4,128)S(1)}, u32[]{:S(2)}, u32[]{:S(2)}) collective-permute-start(f32[4,32]{1,0:T(4,128)S(1)} %add.186), channel_id=1, source_target_pairs={{0,64},{1,65},{2,66},{3,67},{4,68},{5,69},{6,70},{7,71},{8,72},{9,... | collective-permute-start | bytes 1544 | tf_op jit(solution)/shard_map/ppermute | solution.py:76
  312.0 8.9 %collective-permute-start.34 = (f32[4,32]{1,0:T(4,128)S(1)}, f32[4,32]{1,0:T(4,128)S(1)}, u32[]{:S(2)}, u32[]{:S(2)}) collective-permute-start(f32[4,32]{1,0:T(4,128)S(1)} %add.187), channel_id=1, source_target_pairs={{0,128},{1,129},{2,130},{3,131},{4,132},{5,133},{6,134},{7,135},{8... | collective-permute-start | bytes 1544 | tf_op jit(solution)/shard_map/ppermute | solution.py:76
  321.0 13.0 %collective-permute-start.35 = (f32[4,32]{1,0:T(4,128)S(1)}, f32[4,32]{1,0:T(4,128)S(1)}, u32[]{:S(2)}, u32[]{:S(2)}) collective-permute-start(f32[4,32]{1,0:T(4,128)S(1)} %add.188), channel_id=1, source_target_pairs={{0,256},{1,257},{2,258},{3,259},{4,260},{5,261},{6,262},{7,263},{8... | collective-permute-start | bytes 1544 | tf_op jit(solution)/shard_map/ppermute | solution.py:76
  (8 other events, 143.5 us)

commit v3 on v2

--- a/solution.py
+++ b/solution.py
@@ -113,11 +113,12 @@
     first = all_sum(
         jnp.stack([column_sums(residual0, residual0), column_sums(direction0, image0)])
     )
+    image_sq = operate(image0)
     norm0, curve0 = first[0], first[1]
     step0 = norm0 / curve0
     solution_field = spread(step0) * direction0
     residual1 = residual0 - spread(step0) * image0
-    image_res = operate(residual1)
+    image_res = image0 - spread(step0) * image_sq
     second = all_sum(
         jnp.stack(
             [

time: 342 us -> 342 us (level)
  starting transfers between devices: 165 us -> 159 us
    ppermute x18, starting transfers between devices: 111 us -> 102 us  [all_sum(): lax.ppermute(value, AXES, [(i, i ^ bit) for i in range(total)])]
    unnamed x44 -> x43, local copies, waits for them, and re-layouts: 13.6 us -> 14.4 us
  transfers between devices with their start and end apart: 36 -> 36, of which waited for: 24 -> 24; matrix products, arithmetic and copies ran while one was open for 13% -> 15% of each run, Pallas kernels for 0% -> 0%
where the time goes in v3:
time: 342 us; the launch traced here: 336 us
  starting transfers between devices  159 us (46%)
  waiting for transfers between devices  73.4 us (21%)
  matrix products  42.2 us (12%)
  other arithmetic  35.6 us (10%)
  local copies, waits for them, and re-layouts  24.3 us (7%)
    ppermute x18, starting transfers between devices, all_sum(): lax.ppermute(value, AXES, [(i, i ^ bit) for i in range(total)])  102 us
    dot_general x2, matrix products, operate(): jnp.einsum('bmrj,bmji->bri', near_values, kernel, precision=lax.Precision...  42.2 us
    ppermute x9, waiting for transfers between devices, collect_halo(): lower = lax.ppermute(current, AXES, neighbour_route(shape, dim, -1))  38.8 us
    ppermute x9, starting transfers between devices, collect_halo(): upper = lax.ppermute(current, AXES, neighbour_route(shape, dim, 1))  30.5 us
    ppermute x18, waiting for transfers between devices, all_sum(): lax.ppermute(value, AXES, [(i, i ^ bit) for i in range(total)])  28.6 us
    mul x1, other arithmetic, per_device(): kernel = jax.vmap(wendland)(points, others) * present[:, :, None, None]  27.8 us
    ppermute x9, starting transfers between devices, collect_halo(): lower = lax.ppermute(current, AXES, neighbour_route(shape, dim, -1))  26.7 us
    unnamed x43, local copies, waits for them, and re-layouts  14.4 us
  transfers between devices with their start and end apart: 36, of which 24 were waited for; matrix products, arithmetic and copies ran while one was open for 15% of the time, Pallas kernels for 0%

profile of v3, /device:TPU:1, one launch (start us, length us, event | category | flops | bytes accessed | tf_op | source)
XLA Modules:
  0.0 336.3 jit_solution(15515739260474423585)
XLA Ops:
  1.4 6.0 %collective-permute-start.7 = (f32[4,3,256]{2,1,0:T(4,128)S(1)}, f32[4,3,256]{2,1,0:T(4,128)S(1)}, u32[]{:S(2)}, u32[]{:S(2)}) collective-permute-start(f32[4,3,256]{2,1,0:T(4,128)S(1)} %copy.5), channel_id=1, source_target_pairs={{8,0},{9,1},{10,2},{11,3},{12,4},{13,5},{14,6},{15,7},{16,8},{17,9... | collective-permute-start | bytes 36872 | tf_op jit(solution)/shard_map/ppermute | solution.py:42
  9.3 7.8 %collective-permute-start.1 = (f32[4,32,256]{2,1,0:T(8,128)}, f32[4,32,256]{2,1,0:T(8,128)S(1)}, u32[]{:S(2)}, u32[]{:S(2)}) collective-permute-start(f32[4,32,256]{2,1,0:T(8,128)} %param.3), channel_id=1, source_target_pairs={{8,0},{9,1},{10,2},{11,3},{12,4},{13,5},{14,6},{15,7},{16,8},{17,9... | collective-permute-start | bytes 393224 | tf_op jit(solution)/shard_map/ppermute | solution.py:42
  29.5 4.0 %collective-permute-start.10 = (f32[36,3,256]{2,1,0:T(4,128)S(1)}, f32[36,3,256]{2,1,0:T(4,128)S(1)}, u32[]{:S(2)}, u32[]{:S(2)}) collective-permute-start(f32[36,3,256]{2,1,0:T(4,128)S(1)} %constant_dynamic-update-slice_fusion.18), channel_id=1, source_target_pairs={{0,32},{1,33},{2,34},{3,35},{4,36},{5,37},{6,38},{7,39},{8,40},{9,... | collective-permute-start | bytes 331784 | tf_op jit(solution)/shard_map/ppermute | solution.py:41
  35.8 4.0 %collective-permute-start.2 = (f32[12,32,256]{2,1,0:T(8,128)S(1)}, f32[12,32,256]{2,1,0:T(8,128)S(1)}, u32[]{:S(2)}, u32[]{:S(2)}) collective-permute-start(f32[12,32,256]{2,1,0:T(8,128)S(1)} %constant_dynamic-update-slice_fusion), channel_id=1, source_target_pairs={{0,1},{1,2},{2,3},{3,4},{4,5},{5,6},{6,7},{8,9},{9,10},{10,11},{11... | collective-permute-start | bytes 1179656 | tf_op jit(solution)/shard_map/ppermute | solution.py:41
  45.9 4.1 %collective-permute-start.4 = (f32[36,32,256]{2,1,0:T(8,128)S(1)}, f32[36,32,256]{2,1,0:T(8,128)S(1)}, u32[]{:S(2)}, u32[]{:S(2)}) collective-permute-start(f32[36,32,256]{2,1,0:T(8,128)S(1)} %constant_dynamic-update-slice_fusion.3), channel_id=1, source_target_pairs={{0,32},{1,33},{2,34},{3,35},{4,36},{5,37},{6,38},{7,39},{8,40},{9,... | collective-permute-start | bytes 3538952 | tf_op jit(solution)/shard_map/ppermute | solution.py:41
  50.0 27.8 %fusion.1 = f32[4,27,256,256]{3,2,1,0:T(8,128)} fusion(f32[4,27]{1,0:T(4,128)S(1)} %compare_convert_fusion, f32[4,256]{1,0:T(4,128)S(1)} %get-tuple-element.17, f32[4,27,256]{2,1,0:T(8,128)S(1)} %get-tuple-element.20, f32[4,256]{1,0:T(4,128)S(1)} %get-tuple-element.18, f32[4,27,256]{2,1,0:T(8,128)S(1)} %get-tuple-element.21, ...), kind=kLoop, calls=%fused_computation.5 | loop fusion | flops 127401984 | bytes 28656048 | tf_op jit(solution)/shard_map/mul | solution.py:95
  83.7 2.8 gather_fusion
  86.5 20.7 %fusion.3 = f32[4,32,256]{2,1,0:T(8,128)} fusion(f32[4,27,32,256]{3,2,1,0:T(8,128)S(1)} %bitcast.68, f32[4,27,256,256]{3,2,1,0:T(8,128)} %fusion.1, f32[4,32,256]{2,1,0:T(8,128)} %param.3), kind=kOutput, calls=%fused_computation.9 | convolution fusion | flops 2718007296 | bytes 32112640 | tf_op jit(solution)/shard_map/bmrj,bmji->bri/dot_general | solution.py:101
  107.2 8.9 %collective-permute-start.22 = (f32[4,32,256]{2,1,0:T(8,128)}, f32[4,32,256]{2,1,0:T(8,128)S(1)}, u32[]{:S(2)}, u32[]{:S(2)}) collective-permute-start(f32[4,32,256]{2,1,0:T(8,128)} %fusion.3), channel_id=1, source_target_pairs={{8,0},{9,1},{10,2},{11,3},{12,4},{13,5},{14,6},{15,7},{16,8},{17,9... | collective-permute-start | bytes 393224 | tf_op jit(solution)/shard_map/ppermute | solution.py:42
  118.4 6.0 %collective-permute-done.21 = f32[4,32,256]{2,1,0:T(8,128)S(1)} collective-permute-done((f32[4,32,256]{2,1,0:T(8,128)}, f32[4,32,256]{2,1,0:T(8,128)S(1)}, u32[]{:S(2)}, u32[]{:S(2)}) %collective-permute-start.21) | collective-permute-done | bytes 131104 | tf_op jit(solution)/shard_map/ppermute | solution.py:41
  125.3 4.1 %collective-permute-start.23 = (f32[12,32,256]{2,1,0:T(8,128)S(1)}, f32[12,32,256]{2,1,0:T(8,128)S(1)}, u32[]{:S(2)}, u32[]{:S(2)}) collective-permute-start(f32[12,32,256]{2,1,0:T(8,128)S(1)} %pad_maximum_fusion), channel_id=1, source_target_pairs={{0,1},{1,2},{2,3},{3,4},{4,5},{5,6},{6,7},{8,9},{9,10},{10,11},{11... | collective-permute-start | bytes 1179656 | tf_op jit(solution)/shard_map/ppermute | solution.py:41
  130.8 6.8 %collective-permute-done.23 = f32[12,32,256]{2,1,0:T(8,128)S(1)} collective-permute-done((f32[12,32,256]{2,1,0:T(8,128)S(1)}, f32[12,32,256]{2,1,0:T(8,128)S(1)}, u32[]{:S(2)}, u32[]{:S(2)}) %collective-permute-start.23) | collective-permute-done | bytes 393248 | tf_op jit(solution)/shard_map/ppermute | solution.py:41
  138.5 2.9 collective-permute-done.24
  141.4 3.5 %collective-permute-start.25 = (f32[36,32,256]{2,1,0:T(8,128)S(1)}, f32[36,32,256]{2,1,0:T(8,128)S(1)}, u32[]{:S(2)}, u32[]{:S(2)}) collective-permute-start(f32[36,32,256]{2,1,0:T(8,128)S(1)} %constant_dynamic-update-slice_fusion.30), channel_id=1, source_target_pairs={{0,32},{1,33},{2,34},{3,35},{4,36},{5,37},{6,38},{7,39},{8,40},{9,... | collective-permute-start | bytes 3538952 | tf_op jit(solution)/shard_map/ppermute | solution.py:41
  146.2 23.4 %collective-permute-done.25 = f32[36,32,256]{2,1,0:T(8,128)S(1)} collective-permute-done((f32[36,32,256]{2,1,0:T(8,128)S(1)}, f32[36,32,256]{2,1,0:T(8,128)S(1)}, u32[]{:S(2)}, u32[]{:S(2)}) %collective-permute-start.25) | collective-permute-done | bytes 1179680 | tf_op jit(solution)/shard_map/ppermute | solution.py:41
  173.0 5.1 %collective-permute-start.12 = (f32[2,32]{1,0:T(2,128)S(1)}, f32[2,32]{1,0:T(2,128)S(1)}, u32[]{:S(2)}, u32[]{:S(2)}) collective-permute-start(f32[2,32]{1,0:T(2,128)S(1)} %pad_maximum_fusion.2), channel_id=1, source_target_pairs={{0,1},{1,0},{2,3},{3,2},{4,5},{5,4},{6,7},{7,6},{8,9},{9,8},{10,11... | collective-permute-start | bytes 776 | tf_op jit(solution)/shard_map/ppermute | solution.py:76
  179.1 9.7 %collective-permute-start.13 = (f32[2,32]{1,0:T(2,128)S(1)}, f32[2,32]{1,0:T(2,128)S(1)}, u32[]{:S(2)}, u32[]{:S(2)}) collective-permute-start(f32[2,32]{1,0:T(2,128)S(1)} %fusion.27), channel_id=1, source_target_pairs={{0,2},{1,3},{2,0},{3,1},{4,6},{5,7},{6,4},{7,5},{8,10},{9,11},{10,... | collective-permute-start | bytes 776 | tf_op jit(solution)/shard_map/ppermute | solution.py:76
  196.0 3.9 %collective-permute-done.15 = f32[2,32]{1,0:T(2,128)S(1)} collective-permute-done((f32[2,32]{1,0:T(2,128)S(1)}, f32[2,32]{1,0:T(2,128)S(1)}, u32[]{:S(2)}, u32[]{:S(2)}) %collective-permute-start.15) | collective-permute-done | bytes 288 | tf_op jit(solution)/shard_map/ppermute | solution.py:76
  199.9 7.2 %collective-permute-start.16 = (f32[2,32]{1,0:T(2,128)S(1)}, f32[2,32]{1,0:T(2,128)S(1)}, u32[]{:S(2)}, u32[]{:S(2)}) collective-permute-start(f32[2,32]{1,0:T(2,128)S(1)} %add.174), channel_id=1, source_target_pairs={{0,16},{1,17},{2,18},{3,19},{4,20},{5,21},{6,22},{7,23},{8,24},{9,... | collective-permute-start | bytes 776 | tf_op jit(solution)/shard_map/ppermute | solution.py:76
  207.9 4.7 %collective-permute-start.17 = (f32[2,32]{1,0:T(2,128)S(1)}, f32[2,32]{1,0:T(2,128)S(1)}, u32[]{:S(2)}, u32[]{:S(2)}) collective-permute-start(f32[2,32]{1,0:T(2,128)S(1)} %add.175), channel_id=1, source_target_pairs={{0,32},{1,33},{2,34},{3,35},{4,36},{5,37},{6,38},{7,39},{8,40},{9,... | collective-permute-start | bytes 776 | tf_op jit(solution)/shard_map/ppermute | solution.py:76
  213.5 6.8 %collective-permute-start.18 = (f32[2,32]{1,0:T(2,128)S(1)}, f32[2,32]{1,0:T(2,128)S(1)}, u32[]{:S(2)}, u32[]{:S(2)}) collective-permute-start(f32[2,32]{1,0:T(2,128)S(1)} %add.176), channel_id=1, source_target_pairs={{0,64},{1,65},{2,66},{3,67},{4,68},{5,69},{6,70},{7,71},{8,72},{9,... | collective-permute-start | bytes 776 | tf_op jit(solution)/shard_map/ppermute | solution.py:76
  221.3 8.8 %collective-permute-start.19 = (f32[2,32]{1,0:T(2,128)S(1)}, f32[2,32]{1,0:T(2,128)S(1)}, u32[]{:S(2)}, u32[]{:S(2)}) collective-permute-start(f32[2,32]{1,0:T(2,128)S(1)} %add.177), channel_id=1, source_target_pairs={{0,128},{1,129},{2,130},{3,131},{4,132},{5,133},{6,134},{7,135},{8... | collective-permute-start | bytes 776 | tf_op jit(solution)/shard_map/ppermute | solution.py:76
  231.0 12.0 %collective-permute-start.20 = (f32[2,32]{1,0:T(2,128)S(1)}, f32[2,32]{1,0:T(2,128)S(1)}, u32[]{:S(2)}, u32[]{:S(2)}) collective-permute-start(f32[2,32]{1,0:T(2,128)S(1)} %add.178), channel_id=1, source_target_pairs={{0,256},{1,257},{2,258},{3,259},{4,260},{5,261},{6,262},{7,263},{8... | collective-permute-start | bytes 776 | tf_op jit(solution)/shard_map/ppermute | solution.py:76
  247.6 21.5 %multiply_reduce_fusion.3 = (f32[32]{0:T(128)S(1)}, f32[32]{0:T(128)S(1)}, f32[32]{0:T(128)S(1)}, f32[32]{0:T(128)}, f32[4,32,256]{2,1,0:T(8,128)}) fusion(f32[4,32,256]{2,1,0:T(8,128)} %param.3, f32[4,32,256]{2,1,0:T(8,128)} %fusion.3, f32[32]{0:T(128)S(1)} %bitcast_divide_fusion.1, f32[4,27,32,256]{3,2,1,0:T(8,128)S(1)} %bitcast.67, ...), kind=kOutput, calls=%fused_computation.23 | convolution fusion | flops 2718400512 | bytes 32244352 | tf_op jit(solution)/shard_map/bmrj,bmji->bri/dot_general | solution.py:101
  269.8 3.0 collective-permute-start.27
  274.8 5.4 %collective-permute-start.28 = (f32[4,32]{1,0:T(4,128)S(1)}, f32[4,32]{1,0:T(4,128)S(1)}, u32[]{:S(2)}, u32[]{:S(2)}) collective-permute-start(f32[4,32]{1,0:T(4,128)S(1)} %fusion.28), channel_id=1, source_target_pairs={{0,2},{1,3},{2,0},{3,1},{4,6},{5,7},{6,4},{7,5},{8,10},{9,11},{10,... | collective-permute-start | bytes 1544 | tf_op jit(solution)/shard_map/ppermute | solution.py:76
  288.4 3.9 %collective-permute-done.30 = f32[4,32]{1,0:T(4,128)S(1)} collective-permute-done((f32[4,32]{1,0:T(4,128)S(1)}, f32[4,32]{1,0:T(4,128)S(1)}, u32[]{:S(2)}, u32[]{:S(2)}) %collective-permute-start.30) | collective-permute-done | bytes 544 | tf_op jit(solution)/shard_map/ppermute | solution.py:76
  292.3 9.7 %collective-permute-start.31 = (f32[4,32]{1,0:T(4,128)S(1)}, f32[4,32]{1,0:T(4,128)S(1)}, u32[]{:S(2)}, u32[]{:S(2)}) collective-permute-start(f32[4,32]{1,0:T(4,128)S(1)} %add.184), channel_id=1, source_target_pairs={{0,16},{1,17},{2,18},{3,19},{4,20},{5,21},{6,22},{7,23},{8,24},{9,... | collective-permute-start | bytes 1544 | tf_op jit(solution)/shard_map/ppermute | solution.py:76
  307.2 3.6 %collective-permute-start.33 = (f32[4,32]{1,0:T(4,128)S(1)}, f32[4,32]{1,0:T(4,128)S(1)}, u32[]{:S(2)}, u32[]{:S(2)}) collective-permute-start(f32[4,32]{1,0:T(4,128)S(1)} %add.186), channel_id=1, source_target_pairs={{0,64},{1,65},{2,66},{3,67},{4,68},{5,69},{6,70},{7,71},{8,72},{9,... | collective-permute-start | bytes 1544 | tf_op jit(solution)/shard_map/ppermute | solution.py:76
  312.4 5.7 %collective-permute-start.34 = (f32[4,32]{1,0:T(4,128)S(1)}, f32[4,32]{1,0:T(4,128)S(1)}, u32[]{:S(2)}, u32[]{:S(2)}) collective-permute-start(f32[4,32]{1,0:T(4,128)S(1)} %add.187), channel_id=1, source_target_pairs={{0,128},{1,129},{2,130},{3,131},{4,132},{5,133},{6,134},{7,135},{8... | collective-permute-start | bytes 1544 | tf_op jit(solution)/shard_map/ppermute | solution.py:76
  320.6 9.8 %collective-permute-start.35 = (f32[4,32]{1,0:T(4,128)S(1)}, f32[4,32]{1,0:T(4,128)S(1)}, u32[]{:S(2)}, u32[]{:S(2)}) collective-permute-start(f32[4,32]{1,0:T(4,128)S(1)} %add.188), channel_id=1, source_target_pairs={{0,256},{1,257},{2,258},{3,259},{4,260},{5,261},{6,262},{7,263},{8... | collective-permute-start | bytes 1544 | tf_op jit(solution)/shard_map/ppermute | solution.py:76
  330.4 3.3 collective-permute-done.35
  (129 shorter events, 78.3 us)
Async XLA Ops:
  1.4 20.6 %collective-permute-start.7 = (f32[4,3,256]{2,1,0:T(4,128)S(1)}, f32[4,3,256]{2,1,0:T(4,128)S(1)}, u32[]{:S(2)}, u32[]{:S(2)}) collective-permute-start(f32[4,3,256]{2,1,0:T(4,128)S(1)} %copy.5), channel_id=1, source_target_pairs={{8,0},{9,1},{10,2},{11,3},{12,4},{13,5},{14,6},{15,7},{16,8},{17,9... | collective-permute-start | bytes 36872 | tf_op jit(solution)/shard_map/ppermute | solution.py:42
  7.4 13.9 %collective-permute-start.6 = (f32[4,3,256]{2,1,0:T(4,128)S(1)}, f32[4,3,256]{2,1,0:T(4,128)S(1)}, u32[]{:S(2)}, u32[]{:S(2)}) collective-permute-start(f32[4,3,256]{2,1,0:T(4,128)S(1)} %copy.5), channel_id=1, source_target_pairs={{0,8},{1,9},{2,10},{3,11},{4,12},{5,13},{6,14},{7,15},{8,16},{9,17... | collective-permute-start | bytes 36872 | tf_op jit(solution)/shard_map/ppermute | solution.py:41
  9.3 25.1 %collective-permute-start.1 = (f32[4,32,256]{2,1,0:T(8,128)}, f32[4,32,256]{2,1,0:T(8,128)S(1)}, u32[]{:S(2)}, u32[]{:S(2)}) collective-permute-start(f32[4,32,256]{2,1,0:T(8,128)} %param.3), channel_id=1, source_target_pairs={{8,0},{9,1},{10,2},{11,3},{12,4},{13,5},{14,6},{15,7},{16,8},{17,9... | collective-permute-start | bytes 393224 | tf_op jit(solution)/shard_map/ppermute | solution.py:42
  17.1 16.4 %collective-permute-start = (f32[4,32,256]{2,1,0:T(8,128)}, f32[4,32,256]{2,1,0:T(8,128)S(1)}, u32[]{:S(2)}, u32[]{:S(2)}) collective-permute-start(f32[4,32,256]{2,1,0:T(8,128)} %param.3), channel_id=1, source_target_pairs={{0,8},{1,9},{2,10},{3,11},{4,12},{5,13},{6,14},{7,15},{8,16},{9,17... | collective-permute-start | bytes 393224 | tf_op jit(solution)/shard_map/ppermute | solution.py:41
  23.3 4.8 %collective-permute-start.9 = (f32[12,3,256]{2,1,0:T(4,128)S(1)}, f32[12,3,256]{2,1,0:T(4,128)S(1)}, u32[]{:S(2)}, u32[]{:S(2)}) collective-permute-start(f32[12,3,256]{2,1,0:T(4,128)S(1)} %constant_dynamic-update-slice_fusion.15), channel_id=1, source_target_pairs={{1,0},{2,1},{3,2},{4,3},{5,4},{6,5},{7,6},{9,8},{10,9},{11,10},{12... | collective-permute-start | bytes 110600 | tf_op jit(solution)/shard_map/ppermute | solution.py:42
  28.2 12.4 %collective-permute-start.11 = (f32[36,3,256]{2,1,0:T(4,128)S(1)}, f32[36,3,256]{2,1,0:T(4,128)S(1)}, u32[]{:S(2)}, u32[]{:S(2)}) collective-permute-start(f32[36,3,256]{2,1,0:T(4,128)S(1)} %constant_dynamic-update-slice_fusion.18), channel_id=1, source_target_pairs={{32,0},{33,1},{34,2},{35,3},{36,4},{37,5},{38,6},{39,7},{40,8},{41... | collective-permute-start | bytes 331784 | tf_op jit(solution)/shard_map/ppermute | solution.py:42
  29.5 10.3 %collective-permute-start.10 = (f32[36,3,256]{2,1,0:T(4,128)S(1)}, f32[36,3,256]{2,1,0:T(4,128)S(1)}, u32[]{:S(2)}, u32[]{:S(2)}) collective-permute-start(f32[36,3,256]{2,1,0:T(4,128)S(1)} %constant_dynamic-update-slice_fusion.18), channel_id=1, source_target_pairs={{0,32},{1,33},{2,34},{3,35},{4,36},{5,37},{6,38},{7,39},{8,40},{9,... | collective-permute-start | bytes 331784 | tf_op jit(solution)/shard_map/ppermute | solution.py:41
  34.5 10.1 %collective-permute-start.3 = (f32[12,32,256]{2,1,0:T(8,128)S(1)}, f32[12,32,256]{2,1,0:T(8,128)S(1)}, u32[]{:S(2)}, u32[]{:S(2)}) collective-permute-start(f32[12,32,256]{2,1,0:T(8,128)S(1)} %constant_dynamic-update-slice_fusion), channel_id=1, source_target_pairs={{1,0},{2,1},{3,2},{4,3},{5,4},{6,5},{7,6},{9,8},{10,9},{11,10},{12... | collective-permute-start | bytes 1179656 | tf_op jit(solution)/shard_map/ppermute | solution.py:42
  35.8 8.7 %collective-permute-start.2 = (f32[12,32,256]{2,1,0:T(8,128)S(1)}, f32[12,32,256]{2,1,0:T(8,128)S(1)}, u32[]{:S(2)}, u32[]{:S(2)}) collective-permute-start(f32[12,32,256]{2,1,0:T(8,128)S(1)} %constant_dynamic-update-slice_fusion), channel_id=1, source_target_pairs={{0,1},{1,2},{2,3},{3,4},{4,5},{5,6},{6,7},{8,9},{9,10},{10,11},{11... | collective-permute-start | bytes 1179656 | tf_op jit(solution)/shard_map/ppermute | solution.py:41
  44.6 37.9 %collective-permute-start.5 = (f32[36,32,256]{2,1,0:T(8,128)S(1)}, f32[36,32,256]{2,1,0:T(8,128)S(1)}, u32[]{:S(2)}, u32[]{:S(2)}) collective-permute-start(f32[36,32,256]{2,1,0:T(8,128)S(1)} %constant_dynamic-update-slice_fusion.3), channel_id=1, source_target_pairs={{32,0},{33,1},{34,2},{35,3},{36,4},{37,5},{38,6},{39,7},{40,8},{41... | collective-permute-start | bytes 3538952 | tf_op jit(solution)/shard_map/ppermute | solution.py:42
  45.9 31.8 %collective-permute-start.4 = (f32[36,32,256]{2,1,0:T(8,128)S(1)}, f32[36,32,256]{2,1,0:T(8,128)S(1)}, u32[]{:S(2)}, u32[]{:S(2)}) collective-permute-start(f32[36,32,256]{2,1,0:T(8,128)S(1)} %constant_dynamic-update-slice_fusion.3), channel_id=1, source_target_pairs={{0,32},{1,33},{2,34},{3,35},{4,36},{5,37},{6,38},{7,39},{8,40},{9,... | collective-permute-start | bytes 3538952 | tf_op jit(solution)/shard_map/ppermute | solution.py:41
  107.2 11.2 %collective-permute-start.22 = (f32[4,32,256]{2,1,0:T(8,128)}, f32[4,32,256]{2,1,0:T(8,128)S(1)}, u32[]{:S(2)}, u32[]{:S(2)}) collective-permute-start(f32[4,32,256]{2,1,0:T(8,128)} %fusion.3), channel_id=1, source_target_pairs={{8,0},{9,1},{10,2},{11,3},{12,4},{13,5},{14,6},{15,7},{16,8},{17,9... | collective-permute-start | bytes 393224 | tf_op jit(solution)/shard_map/ppermute | solution.py:42
  116.1 8.3 %collective-permute-start.21 = (f32[4,32,256]{2,1,0:T(8,128)}, f32[4,32,256]{2,1,0:T(8,128)S(1)}, u32[]{:S(2)}, u32[]{:S(2)}) collective-permute-start(f32[4,32,256]{2,1,0:T(8,128)} %fusion.3), channel_id=1, source_target_pairs={{0,8},{1,9},{2,10},{3,11},{4,12},{5,13},{6,14},{7,15},{8,16},{9,17... | collective-permute-start | bytes 393224 | tf_op jit(solution)/shard_map/ppermute | solution.py:41
  125.3 12.2 %collective-permute-start.23 = (f32[12,32,256]{2,1,0:T(8,128)S(1)}, f32[12,32,256]{2,1,0:T(8,128)S(1)}, u32[]{:S(2)}, u32[]{:S(2)}) collective-permute-start(f32[12,32,256]{2,1,0:T(8,128)S(1)} %pad_maximum_fusion), channel_id=1, source_target_pairs={{0,1},{1,2},{2,3},{3,4},{4,5},{5,6},{6,7},{8,9},{9,10},{10,11},{11... | collective-permute-start | bytes 1179656 | tf_op jit(solution)/shard_map/ppermute | solution.py:41
  129.5 11.9 %collective-permute-start.24 = (f32[12,32,256]{2,1,0:T(8,128)S(1)}, f32[12,32,256]{2,1,0:T(8,128)S(1)}, u32[]{:S(2)}, u32[]{:S(2)}) collective-permute-start(f32[12,32,256]{2,1,0:T(8,128)S(1)} %pad_maximum_fusion), channel_id=1, source_target_pairs={{1,0},{2,1},{3,2},{4,3},{5,4},{6,5},{7,6},{9,8},{10,9},{11,10},{12... | collective-permute-start | bytes 1179656 | tf_op jit(solution)/shard_map/ppermute | solution.py:42
  141.4 28.1 %collective-permute-start.25 = (f32[36,32,256]{2,1,0:T(8,128)S(1)}, f32[36,32,256]{2,1,0:T(8,128)S(1)}, u32[]{:S(2)}, u32[]{:S(2)}) collective-permute-start(f32[36,32,256]{2,1,0:T(8,128)S(1)} %constant_dynamic-update-slice_fusion.30), channel_id=1, source_target_pairs={{0,32},{1,33},{2,34},{3,35},{4,36},{5,37},{6,38},{7,39},{8,40},{9,... | collective-permute-start | bytes 3538952 | tf_op jit(solution)/shard_map/ppermute | solution.py:41
  144.9 98.2 %collective-permute-start.26 = (f32[36,32,256]{2,1,0:T(8,128)S(1)}, f32[36,32,256]{2,1,0:T(8,128)S(1)}, u32[]{:S(2)}, u32[]{:S(2)}) collective-permute-start(f32[36,32,256]{2,1,0:T(8,128)S(1)} %constant_dynamic-update-slice_fusion.30), channel_id=1, source_target_pairs={{32,0},{33,1},{34,2},{35,3},{36,4},{37,5},{38,6},{39,7},{40,8},{41... | collective-permute-start | bytes 3538952 | tf_op jit(solution)/shard_map/ppermute | solution.py:42
  173.0 6.1 %collective-permute-start.12 = (f32[2,32]{1,0:T(2,128)S(1)}, f32[2,32]{1,0:T(2,128)S(1)}, u32[]{:S(2)}, u32[]{:S(2)}) collective-permute-start(f32[2,32]{1,0:T(2,128)S(1)} %pad_maximum_fusion.2), channel_id=1, source_target_pairs={{0,1},{1,0},{2,3},{3,2},{4,5},{5,4},{6,7},{7,6},{8,9},{9,8},{10,11... | collective-permute-start | bytes 776 | tf_op jit(solution)/shard_map/ppermute | solution.py:76
  179.1 10.7 %collective-permute-start.13 = (f32[2,32]{1,0:T(2,128)S(1)}, f32[2,32]{1,0:T(2,128)S(1)}, u32[]{:S(2)}, u32[]{:S(2)}) collective-permute-start(f32[2,32]{1,0:T(2,128)S(1)} %fusion.27), channel_id=1, source_target_pairs={{0,2},{1,3},{2,0},{3,1},{4,6},{5,7},{6,4},{7,5},{8,10},{9,11},{10,... | collective-permute-start | bytes 776 | tf_op jit(solution)/shard_map/ppermute | solution.py:76
  194.1 5.8 %collective-permute-start.15 = (f32[2,32]{1,0:T(2,128)S(1)}, f32[2,32]{1,0:T(2,128)S(1)}, u32[]{:S(2)}, u32[]{:S(2)}) collective-permute-start(f32[2,32]{1,0:T(2,128)S(1)} %add.173), channel_id=1, source_target_pairs={{0,8},{1,9},{2,10},{3,11},{4,12},{5,13},{6,14},{7,15},{8,0},{9,1},... | collective-permute-start | bytes 776 | tf_op jit(solution)/shard_map/ppermute | solution.py:76
  199.9 8.0 %collective-permute-start.16 = (f32[2,32]{1,0:T(2,128)S(1)}, f32[2,32]{1,0:T(2,128)S(1)}, u32[]{:S(2)}, u32[]{:S(2)}) collective-permute-start(f32[2,32]{1,0:T(2,128)S(1)} %add.174), channel_id=1, source_target_pairs={{0,16},{1,17},{2,18},{3,19},{4,20},{5,21},{6,22},{7,23},{8,24},{9,... | collective-permute-start | bytes 776 | tf_op jit(solution)/shard_map/ppermute | solution.py:76
  207.9 5.6 %collective-permute-start.17 = (f32[2,32]{1,0:T(2,128)S(1)}, f32[2,32]{1,0:T(2,128)S(1)}, u32[]{:S(2)}, u32[]{:S(2)}) collective-permute-start(f32[2,32]{1,0:T(2,128)S(1)} %add.175), channel_id=1, source_target_pairs={{0,32},{1,33},{2,34},{3,35},{4,36},{5,37},{6,38},{7,39},{8,40},{9,... | collective-permute-start | bytes 776 | tf_op jit(solution)/shard_map/ppermute | solution.py:76
  213.5 7.7 %collective-permute-start.18 = (f32[2,32]{1,0:T(2,128)S(1)}, f32[2,32]{1,0:T(2,128)S(1)}, u32[]{:S(2)}, u32[]{:S(2)}) collective-permute-start(f32[2,32]{1,0:T(2,128)S(1)} %add.176), channel_id=1, source_target_pairs={{0,64},{1,65},{2,66},{3,67},{4,68},{5,69},{6,70},{7,71},{8,72},{9,... | collective-permute-start | bytes 776 | tf_op jit(solution)/shard_map/ppermute | solution.py:76
  221.3 9.8 %collective-permute-start.19 = (f32[2,32]{1,0:T(2,128)S(1)}, f32[2,32]{1,0:T(2,128)S(1)}, u32[]{:S(2)}, u32[]{:S(2)}) collective-permute-start(f32[2,32]{1,0:T(2,128)S(1)} %add.177), channel_id=1, source_target_pairs={{0,128},{1,129},{2,130},{3,131},{4,132},{5,133},{6,134},{7,135},{8... | collective-permute-start | bytes 776 | tf_op jit(solution)/shard_map/ppermute | solution.py:76
  231.0 16.0 %collective-permute-start.20 = (f32[2,32]{1,0:T(2,128)S(1)}, f32[2,32]{1,0:T(2,128)S(1)}, u32[]{:S(2)}, u32[]{:S(2)}) collective-permute-start(f32[2,32]{1,0:T(2,128)S(1)} %add.178), channel_id=1, source_target_pairs={{0,256},{1,257},{2,258},{3,259},{4,260},{5,261},{6,262},{7,263},{8... | collective-permute-start | bytes 776 | tf_op jit(solution)/shard_map/ppermute | solution.py:76
  274.8 6.4 %collective-permute-start.28 = (f32[4,32]{1,0:T(4,128)S(1)}, f32[4,32]{1,0:T(4,128)S(1)}, u32[]{:S(2)}, u32[]{:S(2)}) collective-permute-start(f32[4,32]{1,0:T(4,128)S(1)} %fusion.28), channel_id=1, source_target_pairs={{0,2},{1,3},{2,0},{3,1},{4,6},{5,7},{6,4},{7,5},{8,10},{9,11},{10,... | collective-permute-start | bytes 1544 | tf_op jit(solution)/shard_map/ppermute | solution.py:76
  281.9 4.6 %collective-permute-start.29 = (f32[4,32]{1,0:T(4,128)S(1)}, f32[4,32]{1,0:T(4,128)S(1)}, u32[]{:S(2)}, u32[]{:S(2)}) collective-permute-start(f32[4,32]{1,0:T(4,128)S(1)} %fusion.34), channel_id=1, source_target_pairs={{0,4},{1,5},{2,6},{3,7},{4,0},{5,1},{6,2},{7,3},{8,12},{9,13},{10,... | collective-permute-start | bytes 1544 | tf_op jit(solution)/shard_map/ppermute | solution.py:76
  286.5 5.8 %collective-permute-start.30 = (f32[4,32]{1,0:T(4,128)S(1)}, f32[4,32]{1,0:T(4,128)S(1)}, u32[]{:S(2)}, u32[]{:S(2)}) collective-permute-start(f32[4,32]{1,0:T(4,128)S(1)} %add.183), channel_id=1, source_target_pairs={{0,8},{1,9},{2,10},{3,11},{4,12},{5,13},{6,14},{7,15},{8,0},{9,1},... | collective-permute-start | bytes 1544 | tf_op jit(solution)/shard_map/ppermute | solution.py:76
  292.3 10.5 %collective-permute-start.31 = (f32[4,32]{1,0:T(4,128)S(1)}, f32[4,32]{1,0:T(4,128)S(1)}, u32[]{:S(2)}, u32[]{:S(2)}) collective-permute-start(f32[4,32]{1,0:T(4,128)S(1)} %add.184), channel_id=1, source_target_pairs={{0,16},{1,17},{2,18},{3,19},{4,20},{5,21},{6,22},{7,23},{8,24},{9,... | collective-permute-start | bytes 1544 | tf_op jit(solution)/shard_map/ppermute | solution.py:76
  307.2 5.2 %collective-permute-start.33 = (f32[4,32]{1,0:T(4,128)S(1)}, f32[4,32]{1,0:T(4,128)S(1)}, u32[]{:S(2)}, u32[]{:S(2)}) collective-permute-start(f32[4,32]{1,0:T(4,128)S(1)} %add.186), channel_id=1, source_target_pairs={{0,64},{1,65},{2,66},{3,67},{4,68},{5,69},{6,70},{7,71},{8,72},{9,... | collective-permute-start | bytes 1544 | tf_op jit(solution)/shard_map/ppermute | solution.py:76
  312.4 8.2 %collective-permute-start.34 = (f32[4,32]{1,0:T(4,128)S(1)}, f32[4,32]{1,0:T(4,128)S(1)}, u32[]{:S(2)}, u32[]{:S(2)}) collective-permute-start(f32[4,32]{1,0:T(4,128)S(1)} %add.187), channel_id=1, source_target_pairs={{0,128},{1,129},{2,130},{3,131},{4,132},{5,133},{6,134},{7,135},{8... | collective-permute-start | bytes 1544 | tf_op jit(solution)/shard_map/ppermute | solution.py:76
  320.6 13.0 %collective-permute-start.35 = (f32[4,32]{1,0:T(4,128)S(1)}, f32[4,32]{1,0:T(4,128)S(1)}, u32[]{:S(2)}, u32[]{:S(2)}) collective-permute-start(f32[4,32]{1,0:T(4,128)S(1)} %add.188), channel_id=1, source_target_pairs={{0,256},{1,257},{2,258},{3,259},{4,260},{5,261},{6,262},{7,263},{8... | collective-permute-start | bytes 1544 | tf_op jit(solution)/shard_map/ppermute | solution.py:76
  (8 other events, 190.2 us)

commit v4 on v3

--- a/solution.py
+++ b/solution.py
@@ -110,33 +110,65 @@
     residual0 = right_side
     direction0 = right_side
     image0 = operate(direction0)
-    first = all_sum(
-        jnp.stack([column_sums(residual0, residual0), column_sums(direction0, image0)])
-    )
     image_sq = operate(image0)
-    norm0, curve0 = first[0], first[1]
-    step0 = norm0 / curve0
-    solution_field = spread(step0) * direction0
-    residual1 = residual0 - spread(step0) * image0
-    image_res = image0 - spread(step0) * image_sq
-    second = all_sum(
+    moments = all_sum(
         jnp.stack(
             [
-                column_sums(residual1, residual1),
-                column_sums(residual1, image_res),
-                column_sums(residual1, image0),
-                column_sums(direction0, image_res),
+                column_sums(residual0, residual0),
+                column_sums(residual0, image0),
+                column_sums(image0, image0),
+                column_sums(residual0, image_sq),
+                column_sums(image0, image_sq),
             ]
         )
     )
-    norm1 = second[0]
-    ratio = norm1 / norm0
-    curve1 = second[1] + ratio * (second[2] + second[3]) + ratio * ratio * curve0
-    step1 = norm1 / curve1
-    direction1 = residual1 + spread(ratio) * direction0
-    image1 = image_res + spread(ratio) * image0
-    solution_field = solution_field + spread(step1) * direction1
-    residual2 = residual1 - spread(step1) * image1
+    norm0, curve0 = moments[0], moments[1]
+    step0 = norm0 / curve0
+    norm1_est = norm0 - 2.0 * step0 * curve0 + step0 * step0 * moments[2]
+    usable = jnp.all(jnp.isfinite(moments))
+    usable &= jnp.all(jnp.abs(moments[:3]) > 1e-30)
+    usable &= jnp.all(norm1_est >= 0.15 * norm0)
+
+    def from_moments():
+        ratio = norm1_est / norm0
+        grow = 1.0 + ratio
+        curve1 = (
+            grow * grow * curve0
+            - grow * step0 * (moments[3] + moments[2])
+            + step0 * step0 * moments[4]
+        )
+        step1 = norm1_est / curve1
+        total = step0 + step1 * grow
+        both = step1 * step0
+        solution_field = spread(total) * residual0 - spread(both) * image0
+        residual2 = residual0 - spread(total) * image0 + spread(both) * image_sq
+        return (solution_field, residual2)
+
+    def from_vectors():
+        solution_field = spread(step0) * direction0
+        residual1 = residual0 - spread(step0) * image0
+        image_res = image0 - spread(step0) * image_sq
+        second = all_sum(
+            jnp.stack(
+                [
+                    column_sums(residual1, residual1),
+                    column_sums(residual1, image_res),
+                    column_sums(residual1, image0),
+                    column_sums(direction0, image_res),
+                ]
+            )
+        )
+        norm1 = second[0]
+        ratio = norm1 / norm0
+        curve1 = second[1] + ratio * (second[2] + second[3]) + ratio * ratio * curve0
+        step1 = norm1 / curve1
+        direction1 = residual1 + spread(ratio) * direction0
+        image1 = image_res + spread(ratio) * image0
+        solution_field = solution_field + spread(step1) * direction1
+        residual2 = residual1 - spread(step1) * image1
+        return (solution_field, residual2)
+
+    solution_field, residual2 = lax.cond(usable, from_moments, from_vectors)
     return (solution_field, residual2)
 
 

time: 342 us -> 283 us (0.83)
  starting transfers between devices: 159 us -> 115 us
  waiting for transfers between devices: 73.4 us -> 57.7 us
    ppermute x18 -> x9, starting transfers between devices: 102 us -> 58.1 us  [all_sum(): lax.ppermute(value, AXES, [(i, i ^ bit) for i in range(total)])]
    ppermute x18 -> x9, waiting for transfers between devices: 28.6 us -> 12.8 us  [all_sum(): lax.ppermute(value, AXES, [(i, i ^ bit) for i in range(total)])]
    unnamed x43 -> x40, local copies, waits for them, and re-layouts: 14.4 us -> 14.6 us
  transfers between devices with their start and end apart: 36 -> 27, of which waited for: 24 -> 17; matrix products, arithmetic and copies ran while one was open for 15% -> 16% of each run, Pallas kernels for 0% -> 0%
where the time goes in v4:
time: 283 us; the launch traced here: 278 us
  starting transfers between devices  115 us (41%)
  waiting for transfers between devices  57.7 us (20%)
  matrix products  42.1 us (15%)
  other arithmetic  34 us (12%)
  local copies, waits for them, and re-layouts  25.2 us (9%)
  between operations  3.09 us (1%)
    ppermute x9, starting transfers between devices, all_sum(): lax.ppermute(value, AXES, [(i, i ^ bit) for i in range(total)])  58.1 us
    dot_general x2, matrix products, operate(): jnp.einsum('bmrj,bmji->bri', near_values, kernel, precision=lax.Precision...  42.1 us
    ppermute x9, waiting for transfers between devices, collect_halo(): lower = lax.ppermute(current, AXES, neighbour_route(shape, dim, -1))  38.7 us
    ppermute x9, starting transfers between devices, collect_halo(): upper = lax.ppermute(current, AXES, neighbour_route(shape, dim, 1))  30.7 us
    mul x1, other arithmetic, per_device(): kernel = jax.vmap(wendland)(points, others) * present[:, :, None, None]  27.8 us
    ppermute x9, starting transfers between devices, collect_halo(): lower = lax.ppermute(current, AXES, neighbour_route(shape, dim, -1))  26.7 us
    unnamed x40, local copies, waits for them, and re-layouts  14.6 us
    ppermute x9, waiting for transfers between devices, all_sum(): lax.ppermute(value, AXES, [(i, i ^ bit) for i in range(total)])  12.8 us
  transfers between devices with their start and end apart: 27, of which 17 were waited for; matrix products, arithmetic and copies ran while one was open for 16% of the time, Pallas kernels for 0%

profile of v4, /device:TPU:1, one launch (start us, length us, event | category | flops | bytes accessed | tf_op | source)
XLA Modules:
  0.0 277.5 jit_solution(12358699913395402021)
XLA Ops:
  1.4 6.0 %collective-permute-start.16 = (f32[4,3,256]{2,1,0:T(4,128)S(1)}, f32[4,3,256]{2,1,0:T(4,128)S(1)}, u32[]{:S(2)}, u32[]{:S(2)}) collective-permute-start(f32[4,3,256]{2,1,0:T(4,128)S(1)} %copy.9), channel_id=1, source_target_pairs={{8,0},{9,1},{10,2},{11,3},{12,4},{13,5},{14,6},{15,7},{16,8},{17,9... | collective-permute-start | bytes 36872 | tf_op jit(solution)/shard_map/ppermute | solution.py:42
  7.4 1.9 collective-permute-start.15
  9.3 7.8 %collective-permute-start.10 = (f32[4,32,256]{2,1,0:T(8,128)}, f32[4,32,256]{2,1,0:T(8,128)S(1)}, u32[]{:S(2)}, u32[]{:S(2)}) collective-permute-start(f32[4,32,256]{2,1,0:T(8,128)} %param.5), channel_id=1, source_target_pairs={{8,0},{9,1},{10,2},{11,3},{12,4},{13,5},{14,6},{15,7},{16,8},{17,9... | collective-permute-start | bytes 393224 | tf_op jit(solution)/shard_map/ppermute | solution.py:42
  17.1 1.9 collective-permute-start.9
  25.4 2.8 collective-permute-done.18
  29.5 4.0 %collective-permute-start.19 = (f32[36,3,256]{2,1,0:T(4,128)S(1)}, f32[36,3,256]{2,1,0:T(4,128)S(1)}, u32[]{:S(2)}, u32[]{:S(2)}) collective-permute-start(f32[36,3,256]{2,1,0:T(4,128)S(1)} %constant_dynamic-update-slice_fusion.18), channel_id=1, source_target_pairs={{0,32},{1,33},{2,34},{3,35},{4,36},{5,37},{6,38},{7,39},{8,40},{9,... | collective-permute-start | bytes 331784 | tf_op jit(solution)/shard_map/ppermute | solution.py:41
  35.8 4.0 %collective-permute-start.11 = (f32[12,32,256]{2,1,0:T(8,128)S(1)}, f32[12,32,256]{2,1,0:T(8,128)S(1)}, u32[]{:S(2)}, u32[]{:S(2)}) collective-permute-start(f32[12,32,256]{2,1,0:T(8,128)S(1)} %constant_dynamic-update-slice_fusion), channel_id=1, source_target_pairs={{0,1},{1,2},{2,3},{3,4},{4,5},{5,6},{6,7},{8,9},{9,10},{10,11},{11... | collective-permute-start | bytes 1179656 | tf_op jit(solution)/shard_map/ppermute | solution.py:41
  41.8 2.7 collective-permute-done.11
  45.9 4.1 %collective-permute-start.13 = (f32[36,32,256]{2,1,0:T(8,128)S(1)}, f32[36,32,256]{2,1,0:T(8,128)S(1)}, u32[]{:S(2)}, u32[]{:S(2)}) collective-permute-start(f32[36,32,256]{2,1,0:T(8,128)S(1)} %constant_dynamic-update-slice_fusion.3), channel_id=1, source_target_pairs={{0,32},{1,33},{2,34},{3,35},{4,36},{5,37},{6,38},{7,39},{8,40},{9,... | collective-permute-start | bytes 3538952 | tf_op jit(solution)/shard_map/ppermute | solution.py:41
  50.0 27.8 %fusion.8 = f32[4,27,256,256]{3,2,1,0:T(8,128)} fusion(f32[4,27]{1,0:T(4,128)S(1)} %compare_convert_fusion, f32[4,256]{1,0:T(4,128)S(1)} %get-tuple-element.72, f32[4,27,256]{2,1,0:T(8,128)S(1)} %get-tuple-element.77, f32[4,256]{1,0:T(4,128)S(1)} %get-tuple-element.73, f32[4,27,256]{2,1,0:T(8,128)S(1)} %get-tuple-element.78, ...), kind=kLoop, calls=%fused_computation.29 | loop fusion | flops 127401984 | bytes 28656048 | tf_op jit(solution)/shard_map/mul | solution.py:95
  83.8 2.8 gather_fusion
  86.6 20.7 %fusion.10 = f32[4,32,256]{2,1,0:T(8,128)} fusion(f32[4,27,32,256]{3,2,1,0:T(8,128)S(1)} %bitcast.95, f32[4,27,256,256]{3,2,1,0:T(8,128)} %fusion.8, f32[4,32,256]{2,1,0:T(8,128)} %param.5), kind=kOutput, calls=%fused_computation.33 | convolution fusion | flops 2718007296 | bytes 32112640 | tf_op jit(solution)/shard_map/bmrj,bmji->bri/dot_general | solution.py:101
  107.2 8.9 %collective-permute-start.22 = (f32[4,32,256]{2,1,0:T(8,128)}, f32[4,32,256]{2,1,0:T(8,128)S(1)}, u32[]{:S(2)}, u32[]{:S(2)}) collective-permute-start(f32[4,32,256]{2,1,0:T(8,128)} %fusion.10), channel_id=1, source_target_pairs={{8,0},{9,1},{10,2},{11,3},{12,4},{13,5},{14,6},{15,7},{16,8},{17,9... | collective-permute-start | bytes 393224 | tf_op jit(solution)/shard_map/ppermute | solution.py:42
  116.2 1.9 collective-permute-start.21
  118.4 6.0 %collective-permute-done.21 = f32[4,32,256]{2,1,0:T(8,128)S(1)} collective-permute-done((f32[4,32,256]{2,1,0:T(8,128)}, f32[4,32,256]{2,1,0:T(8,128)S(1)}, u32[]{:S(2)}, u32[]{:S(2)}) %collective-permute-start.21) | collective-permute-done | bytes 131104 | tf_op jit(solution)/shard_map/ppermute | solution.py:41
  125.4 4.1 %collective-permute-start.23 = (f32[12,32,256]{2,1,0:T(8,128)S(1)}, f32[12,32,256]{2,1,0:T(8,128)S(1)}, u32[]{:S(2)}, u32[]{:S(2)}) collective-permute-start(f32[12,32,256]{2,1,0:T(8,128)S(1)} %pad_maximum_fusion.1), channel_id=1, source_target_pairs={{0,1},{1,2},{2,3},{3,4},{4,5},{5,6},{6,7},{8,9},{9,10},{10,11},{11... | collective-permute-start | bytes 1179656 | tf_op jit(solution)/shard_map/ppermute | solution.py:41
  130.9 6.8 %collective-permute-done.23 = f32[12,32,256]{2,1,0:T(8,128)S(1)} collective-permute-done((f32[12,32,256]{2,1,0:T(8,128)S(1)}, f32[12,32,256]{2,1,0:T(8,128)S(1)}, u32[]{:S(2)}, u32[]{:S(2)}) %collective-permute-start.23) | collective-permute-done | bytes 393248 | tf_op jit(solution)/shard_map/ppermute | solution.py:41
  138.6 2.9 %collective-permute-done.24 = f32[12,32,256]{2,1,0:T(8,128)S(1)} collective-permute-done((f32[12,32,256]{2,1,0:T(8,128)S(1)}, f32[12,32,256]{2,1,0:T(8,128)S(1)}, u32[]{:S(2)}, u32[]{:S(2)}) %collective-permute-start.24) | collective-permute-done | bytes 393248 | tf_op jit(solution)/shard_map/ppermute | solution.py:42
  141.5 3.5 %collective-permute-start.25 = (f32[36,32,256]{2,1,0:T(8,128)S(1)}, f32[36,32,256]{2,1,0:T(8,128)S(1)}, u32[]{:S(2)}, u32[]{:S(2)}) collective-permute-start(f32[36,32,256]{2,1,0:T(8,128)S(1)} %constant_dynamic-update-slice_fusion.30), channel_id=1, source_target_pairs={{0,32},{1,33},{2,34},{3,35},{4,36},{5,37},{6,38},{7,39},{8,40},{9,... | collective-permute-start | bytes 3538952 | tf_op jit(solution)/shard_map/ppermute | solution.py:41
  146.5 23.2 %collective-permute-done.25 = f32[36,32,256]{2,1,0:T(8,128)S(1)} collective-permute-done((f32[36,32,256]{2,1,0:T(8,128)S(1)}, f32[36,32,256]{2,1,0:T(8,128)S(1)}, u32[]{:S(2)}, u32[]{:S(2)}) %collective-permute-start.25) | collective-permute-done | bytes 1179680 | tf_op jit(solution)/shard_map/ppermute | solution.py:41
  175.8 2.8 gather_fusion.2
  178.6 21.4 %multiply_reduce_fusion.4 = (f32[32]{0:T(128)S(1)}, f32[32]{0:T(128)S(1)}, f32[32]{0:T(128)S(1)}, f32[32]{0:T(128)S(1)}, f32[32]{0:T(128)}, /*index=5*/f32[4,32,256]{2,1,0:T(8,128)}) fusion(f32[4,32,256]{2,1,0:T(8,128)} %fusion.10, f32[4,32,256]{2,1,0:T(8,128)} %param.5, f32[4,27,32,256]{3,2,1,0:T(8,128)S(1)} %bitcast.94, f32[4,27,256,256]{3,2,1,0:T(8,128)} %fusion.8), kind=kOutput, calls=%fused_computation.40 | convolution fusion | flops 2718334720 | bytes 32244352 | tf_op jit(solution)/shard_map/bmrj,bmji->bri/dot_general | solution.py:101
  200.7 5.5 %collective-permute-start.27 = (f32[5,32]{1,0:T(8,128)S(1)}, f32[5,32]{1,0:T(8,128)S(1)}, u32[]{:S(2)}, u32[]{:S(2)}) collective-permute-start(f32[5,32]{1,0:T(8,128)S(1)} %stack.38), channel_id=1, source_target_pairs={{0,1},{1,0},{2,3},{3,2},{4,5},{5,4},{6,7},{7,6},{8,9},{9,8},{10,11... | collective-permute-start | bytes 1928 | tf_op jit(solution)/shard_map/ppermute | solution.py:76
  207.2 9.7 %collective-permute-start.28 = (f32[5,32]{1,0:T(8,128)S(1)}, f32[5,32]{1,0:T(8,128)S(1)}, u32[]{:S(2)}, u32[]{:S(2)}) collective-permute-start(f32[5,32]{1,0:T(8,128)S(1)} %add.181), channel_id=1, source_target_pairs={{0,2},{1,3},{2,0},{3,1},{4,6},{5,7},{6,4},{7,5},{8,10},{9,11},{10,... | collective-permute-start | bytes 1928 | tf_op jit(solution)/shard_map/ppermute | solution.py:76
  217.9 2.3 collective-permute-start.29
  220.3 2.0 collective-permute-done.29
  224.2 3.9 %collective-permute-done.30 = f32[5,32]{1,0:T(8,128)S(1)} collective-permute-done((f32[5,32]{1,0:T(8,128)S(1)}, f32[5,32]{1,0:T(8,128)S(1)}, u32[]{:S(2)}, u32[]{:S(2)}) %collective-permute-start.30) | collective-permute-done | bytes 672 | tf_op jit(solution)/shard_map/ppermute | solution.py:76
  228.1 7.2 %collective-permute-start.31 = (f32[5,32]{1,0:T(8,128)S(1)}, f32[5,32]{1,0:T(8,128)S(1)}, u32[]{:S(2)}, u32[]{:S(2)}) collective-permute-start(f32[5,32]{1,0:T(8,128)S(1)} %add.184), channel_id=1, source_target_pairs={{0,16},{1,17},{2,18},{3,19},{4,20},{5,21},{6,22},{7,23},{8,24},{9,... | collective-permute-start | bytes 1928 | tf_op jit(solution)/shard_map/ppermute | solution.py:76
  236.1 4.8 %collective-permute-start.32 = (f32[5,32]{1,0:T(8,128)S(1)}, f32[5,32]{1,0:T(8,128)S(1)}, u32[]{:S(2)}, u32[]{:S(2)}) collective-permute-start(f32[5,32]{1,0:T(8,128)S(1)} %add.185), channel_id=1, source_target_pairs={{0,32},{1,33},{2,34},{3,35},{4,36},{5,37},{6,38},{7,39},{8,40},{9,... | collective-permute-start | bytes 1928 | tf_op jit(solution)/shard_map/ppermute | solution.py:76
  242.0 5.9 %collective-permute-start.33 = (f32[5,32]{1,0:T(8,128)S(1)}, f32[5,32]{1,0:T(8,128)S(1)}, u32[]{:S(2)}, u32[]{:S(2)}) collective-permute-start(f32[5,32]{1,0:T(8,128)S(1)} %add.186), channel_id=1, source_target_pairs={{0,64},{1,65},{2,66},{3,67},{4,68},{5,69},{6,70},{7,71},{8,72},{9,... | collective-permute-start | bytes 1928 | tf_op jit(solution)/shard_map/ppermute | solution.py:76
  248.9 8.8 %collective-permute-start.34 = (f32[5,32]{1,0:T(8,128)S(1)}, f32[5,32]{1,0:T(8,128)S(1)}, u32[]{:S(2)}, u32[]{:S(2)}) collective-permute-start(f32[5,32]{1,0:T(8,128)S(1)} %add.187), channel_id=1, source_target_pairs={{0,128},{1,129},{2,130},{3,131},{4,132},{5,133},{6,134},{7,135},{8... | collective-permute-start | bytes 1928 | tf_op jit(solution)/shard_map/ppermute | solution.py:76
  258.7 11.8 %collective-permute-start.35 = (f32[5,32]{1,0:T(8,128)S(1)}, f32[5,32]{1,0:T(8,128)S(1)}, u32[]{:S(2)}, u32[]{:S(2)}) collective-permute-start(f32[5,32]{1,0:T(8,128)S(1)} %add.188), channel_id=1, source_target_pairs={{0,256},{1,257},{2,258},{3,259},{4,260},{5,261},{6,262},{7,263},{8... | collective-permute-start | bytes 1928 | tf_op jit(solution)/shard_map/ppermute | solution.py:76
  (101 shorter events, 46.3 us)
Async XLA Ops:
  0.6 43.9 %copy-start = (f32[4,32,256]{2,1,0:T(8,128)S(1)}, f32[4,32,256]{2,1,0:T(8,128)}, u32[]{:S(2)}) copy-start(f32[4,32,256]{2,1,0:T(8,128)} %param.5) | copy-start | bytes 393220
  1.4 20.6 %collective-permute-start.16 = (f32[4,3,256]{2,1,0:T(4,128)S(1)}, f32[4,3,256]{2,1,0:T(4,128)S(1)}, u32[]{:S(2)}, u32[]{:S(2)}) collective-permute-start(f32[4,3,256]{2,1,0:T(4,128)S(1)} %copy.9), channel_id=1, source_target_pairs={{8,0},{9,1},{10,2},{11,3},{12,4},{13,5},{14,6},{15,7},{16,8},{17,9... | collective-permute-start | bytes 36872 | tf_op jit(solution)/shard_map/ppermute | solution.py:42
  7.4 13.9 %collective-permute-start.15 = (f32[4,3,256]{2,1,0:T(4,128)S(1)}, f32[4,3,256]{2,1,0:T(4,128)S(1)}, u32[]{:S(2)}, u32[]{:S(2)}) collective-permute-start(f32[4,3,256]{2,1,0:T(4,128)S(1)} %copy.9), channel_id=1, source_target_pairs={{0,8},{1,9},{2,10},{3,11},{4,12},{5,13},{6,14},{7,15},{8,16},{9,17... | collective-permute-start | bytes 36872 | tf_op jit(solution)/shard_map/ppermute | solution.py:41
  9.3 25.1 %collective-permute-start.10 = (f32[4,32,256]{2,1,0:T(8,128)}, f32[4,32,256]{2,1,0:T(8,128)S(1)}, u32[]{:S(2)}, u32[]{:S(2)}) collective-permute-start(f32[4,32,256]{2,1,0:T(8,128)} %param.5), channel_id=1, source_target_pairs={{8,0},{9,1},{10,2},{11,3},{12,4},{13,5},{14,6},{15,7},{16,8},{17,9... | collective-permute-start | bytes 393224 | tf_op jit(solution)/shard_map/ppermute | solution.py:42
  17.1 16.4 %collective-permute-start.9 = (f32[4,32,256]{2,1,0:T(8,128)}, f32[4,32,256]{2,1,0:T(8,128)S(1)}, u32[]{:S(2)}, u32[]{:S(2)}) collective-permute-start(f32[4,32,256]{2,1,0:T(8,128)} %param.5), channel_id=1, source_target_pairs={{0,8},{1,9},{2,10},{3,11},{4,12},{5,13},{6,14},{7,15},{8,16},{9,17... | collective-permute-start | bytes 393224 | tf_op jit(solution)/shard_map/ppermute | solution.py:41
  22.0 2.6 collective-permute-start.17
  23.3 4.8 %collective-permute-start.18 = (f32[12,3,256]{2,1,0:T(4,128)S(1)}, f32[12,3,256]{2,1,0:T(4,128)S(1)}, u32[]{:S(2)}, u32[]{:S(2)}) collective-permute-start(f32[12,3,256]{2,1,0:T(4,128)S(1)} %constant_dynamic-update-slice_fusion.15), channel_id=1, source_target_pairs={{1,0},{2,1},{3,2},{4,3},{5,4},{6,5},{7,6},{9,8},{10,9},{11,10},{12... | collective-permute-start | bytes 110600 | tf_op jit(solution)/shard_map/ppermute | solution.py:42
  28.2 12.4 %collective-permute-start.20 = (f32[36,3,256]{2,1,0:T(4,128)S(1)}, f32[36,3,256]{2,1,0:T(4,128)S(1)}, u32[]{:S(2)}, u32[]{:S(2)}) collective-permute-start(f32[36,3,256]{2,1,0:T(4,128)S(1)} %constant_dynamic-update-slice_fusion.18), channel_id=1, source_target_pairs={{32,0},{33,1},{34,2},{35,3},{36,4},{37,5},{38,6},{39,7},{40,8},{41... | collective-permute-start | bytes 331784 | tf_op jit(solution)/shard_map/ppermute | solution.py:42
  29.5 10.3 %collective-permute-start.19 = (f32[36,3,256]{2,1,0:T(4,128)S(1)}, f32[36,3,256]{2,1,0:T(4,128)S(1)}, u32[]{:S(2)}, u32[]{:S(2)}) collective-permute-start(f32[36,3,256]{2,1,0:T(4,128)S(1)} %constant_dynamic-update-slice_fusion.18), channel_id=1, source_target_pairs={{0,32},{1,33},{2,34},{3,35},{4,36},{5,37},{6,38},{7,39},{8,40},{9,... | collective-permute-start | bytes 331784 | tf_op jit(solution)/shard_map/ppermute | solution.py:41
  34.5 10.1 %collective-permute-start.12 = (f32[12,32,256]{2,1,0:T(8,128)S(1)}, f32[12,32,256]{2,1,0:T(8,128)S(1)}, u32[]{:S(2)}, u32[]{:S(2)}) collective-permute-start(f32[12,32,256]{2,1,0:T(8,128)S(1)} %constant_dynamic-update-slice_fusion), channel_id=1, source_target_pairs={{1,0},{2,1},{3,2},{4,3},{5,4},{6,5},{7,6},{9,8},{10,9},{11,10},{12... | collective-permute-start | bytes 1179656 | tf_op jit(solution)/shard_map/ppermute | solution.py:42
  35.8 8.7 %collective-permute-start.11 = (f32[12,32,256]{2,1,0:T(8,128)S(1)}, f32[12,32,256]{2,1,0:T(8,128)S(1)}, u32[]{:S(2)}, u32[]{:S(2)}) collective-permute-start(f32[12,32,256]{2,1,0:T(8,128)S(1)} %constant_dynamic-update-slice_fusion), channel_id=1, source_target_pairs={{0,1},{1,2},{2,3},{3,4},{4,5},{5,6},{6,7},{8,9},{9,10},{10,11},{11... | collective-permute-start | bytes 1179656 | tf_op jit(solution)/shard_map/ppermute | solution.py:41
  44.6 38.0 %collective-permute-start.14 = (f32[36,32,256]{2,1,0:T(8,128)S(1)}, f32[36,32,256]{2,1,0:T(8,128)S(1)}, u32[]{:S(2)}, u32[]{:S(2)}) collective-permute-start(f32[36,32,256]{2,1,0:T(8,128)S(1)} %constant_dynamic-update-slice_fusion.3), channel_id=1, source_target_pairs={{32,0},{33,1},{34,2},{35,3},{36,4},{37,5},{38,6},{39,7},{40,8},{41... | collective-permute-start | bytes 3538952 | tf_op jit(solution)/shard_map/ppermute | solution.py:42
  45.9 31.9 %collective-permute-start.13 = (f32[36,32,256]{2,1,0:T(8,128)S(1)}, f32[36,32,256]{2,1,0:T(8,128)S(1)}, u32[]{:S(2)}, u32[]{:S(2)}) collective-permute-start(f32[36,32,256]{2,1,0:T(8,128)S(1)} %constant_dynamic-update-slice_fusion.3), channel_id=1, source_target_pairs={{0,32},{1,33},{2,34},{3,35},{4,36},{5,37},{6,38},{7,39},{8,40},{9,... | collective-permute-start | bytes 3538952 | tf_op jit(solution)/shard_map/ppermute | solution.py:41
  107.2 65.1 %copy-start.1 = (f32[4,32,256]{2,1,0:T(8,128)S(1)}, f32[4,32,256]{2,1,0:T(8,128)}, u32[]{:S(2)}) copy-start(f32[4,32,256]{2,1,0:T(8,128)} %fusion.10) | copy-start | bytes 393220
  107.2 11.2 %collective-permute-start.22 = (f32[4,32,256]{2,1,0:T(8,128)}, f32[4,32,256]{2,1,0:T(8,128)S(1)}, u32[]{:S(2)}, u32[]{:S(2)}) collective-permute-start(f32[4,32,256]{2,1,0:T(8,128)} %fusion.10), channel_id=1, source_target_pairs={{8,0},{9,1},{10,2},{11,3},{12,4},{13,5},{14,6},{15,7},{16,8},{17,9... | collective-permute-start | bytes 393224 | tf_op jit(solution)/shard_map/ppermute | solution.py:42
  116.2 8.3 %collective-permute-start.21 = (f32[4,32,256]{2,1,0:T(8,128)}, f32[4,32,256]{2,1,0:T(8,128)S(1)}, u32[]{:S(2)}, u32[]{:S(2)}) collective-permute-start(f32[4,32,256]{2,1,0:T(8,128)} %fusion.10), channel_id=1, source_target_pairs={{0,8},{1,9},{2,10},{3,11},{4,12},{5,13},{6,14},{7,15},{8,16},{9,17... | collective-permute-start | bytes 393224 | tf_op jit(solution)/shard_map/ppermute | solution.py:41
  125.4 12.2 %collective-permute-start.23 = (f32[12,32,256]{2,1,0:T(8,128)S(1)}, f32[12,32,256]{2,1,0:T(8,128)S(1)}, u32[]{:S(2)}, u32[]{:S(2)}) collective-permute-start(f32[12,32,256]{2,1,0:T(8,128)S(1)} %pad_maximum_fusion.1), channel_id=1, source_target_pairs={{0,1},{1,2},{2,3},{3,4},{4,5},{5,6},{6,7},{8,9},{9,10},{10,11},{11... | collective-permute-start | bytes 1179656 | tf_op jit(solution)/shard_map/ppermute | solution.py:41
  129.6 11.9 %collective-permute-start.24 = (f32[12,32,256]{2,1,0:T(8,128)S(1)}, f32[12,32,256]{2,1,0:T(8,128)S(1)}, u32[]{:S(2)}, u32[]{:S(2)}) collective-permute-start(f32[12,32,256]{2,1,0:T(8,128)S(1)} %pad_maximum_fusion.1), channel_id=1, source_target_pairs={{1,0},{2,1},{3,2},{4,3},{5,4},{6,5},{7,6},{9,8},{10,9},{11,10},{12... | collective-permute-start | bytes 1179656 | tf_op jit(solution)/shard_map/ppermute | solution.py:42
  141.5 28.1 %collective-permute-start.25 = (f32[36,32,256]{2,1,0:T(8,128)S(1)}, f32[36,32,256]{2,1,0:T(8,128)S(1)}, u32[]{:S(2)}, u32[]{:S(2)}) collective-permute-start(f32[36,32,256]{2,1,0:T(8,128)S(1)} %constant_dynamic-update-slice_fusion.30), channel_id=1, source_target_pairs={{0,32},{1,33},{2,34},{3,35},{4,36},{5,37},{6,38},{7,39},{8,40},{9,... | collective-permute-start | bytes 3538952 | tf_op jit(solution)/shard_map/ppermute | solution.py:41
  145.0 29.7 %collective-permute-start.26 = (f32[36,32,256]{2,1,0:T(8,128)S(1)}, f32[36,32,256]{2,1,0:T(8,128)S(1)}, u32[]{:S(2)}, u32[]{:S(2)}) collective-permute-start(f32[36,32,256]{2,1,0:T(8,128)S(1)} %constant_dynamic-update-slice_fusion.30), channel_id=1, source_target_pairs={{32,0},{33,1},{34,2},{35,3},{36,4},{37,5},{38,6},{39,7},{40,8},{41... | collective-permute-start | bytes 3538952 | tf_op jit(solution)/shard_map/ppermute | solution.py:42
  200.7 6.5 %collective-permute-start.27 = (f32[5,32]{1,0:T(8,128)S(1)}, f32[5,32]{1,0:T(8,128)S(1)}, u32[]{:S(2)}, u32[]{:S(2)}) collective-permute-start(f32[5,32]{1,0:T(8,128)S(1)} %stack.38), channel_id=1, source_target_pairs={{0,1},{1,0},{2,3},{3,2},{4,5},{5,4},{6,7},{7,6},{8,9},{9,8},{10,11... | collective-permute-start | bytes 1928 | tf_op jit(solution)/shard_map/ppermute | solution.py:76
  207.2 10.7 %collective-permute-start.28 = (f32[5,32]{1,0:T(8,128)S(1)}, f32[5,32]{1,0:T(8,128)S(1)}, u32[]{:S(2)}, u32[]{:S(2)}) collective-permute-start(f32[5,32]{1,0:T(8,128)S(1)} %add.181), channel_id=1, source_target_pairs={{0,2},{1,3},{2,0},{3,1},{4,6},{5,7},{6,4},{7,5},{8,10},{9,11},{10,... | collective-permute-start | bytes 1928 | tf_op jit(solution)/shard_map/ppermute | solution.py:76
  217.9 4.3 %collective-permute-start.29 = (f32[5,32]{1,0:T(8,128)S(1)}, f32[5,32]{1,0:T(8,128)S(1)}, u32[]{:S(2)}, u32[]{:S(2)}) collective-permute-start(f32[5,32]{1,0:T(8,128)S(1)} %add.182), channel_id=1, source_target_pairs={{0,4},{1,5},{2,6},{3,7},{4,0},{5,1},{6,2},{7,3},{8,12},{9,13},{10,... | collective-permute-start | bytes 1928 | tf_op jit(solution)/shard_map/ppermute | solution.py:76
  222.3 5.8 %collective-permute-start.30 = (f32[5,32]{1,0:T(8,128)S(1)}, f32[5,32]{1,0:T(8,128)S(1)}, u32[]{:S(2)}, u32[]{:S(2)}) collective-permute-start(f32[5,32]{1,0:T(8,128)S(1)} %add.183), channel_id=1, source_target_pairs={{0,8},{1,9},{2,10},{3,11},{4,12},{5,13},{6,14},{7,15},{8,0},{9,1},... | collective-permute-start | bytes 1928 | tf_op jit(solution)/shard_map/ppermute | solution.py:76
  228.1 8.0 %collective-permute-start.31 = (f32[5,32]{1,0:T(8,128)S(1)}, f32[5,32]{1,0:T(8,128)S(1)}, u32[]{:S(2)}, u32[]{:S(2)}) collective-permute-start(f32[5,32]{1,0:T(8,128)S(1)} %add.184), channel_id=1, source_target_pairs={{0,16},{1,17},{2,18},{3,19},{4,20},{5,21},{6,22},{7,23},{8,24},{9,... | collective-permute-start | bytes 1928 | tf_op jit(solution)/shard_map/ppermute | solution.py:76
  236.1 5.8 %collective-permute-start.32 = (f32[5,32]{1,0:T(8,128)S(1)}, f32[5,32]{1,0:T(8,128)S(1)}, u32[]{:S(2)}, u32[]{:S(2)}) collective-permute-start(f32[5,32]{1,0:T(8,128)S(1)} %add.185), channel_id=1, source_target_pairs={{0,32},{1,33},{2,34},{3,35},{4,36},{5,37},{6,38},{7,39},{8,40},{9,... | collective-permute-start | bytes 1928 | tf_op jit(solution)/shard_map/ppermute | solution.py:76
  242.0 6.9 %collective-permute-start.33 = (f32[5,32]{1,0:T(8,128)S(1)}, f32[5,32]{1,0:T(8,128)S(1)}, u32[]{:S(2)}, u32[]{:S(2)}) collective-permute-start(f32[5,32]{1,0:T(8,128)S(1)} %add.186), channel_id=1, source_target_pairs={{0,64},{1,65},{2,66},{3,67},{4,68},{5,69},{6,70},{7,71},{8,72},{9,... | collective-permute-start | bytes 1928 | tf_op jit(solution)/shard_map/ppermute | solution.py:76
  248.9 9.8 %collective-permute-start.34 = (f32[5,32]{1,0:T(8,128)S(1)}, f32[5,32]{1,0:T(8,128)S(1)}, u32[]{:S(2)}, u32[]{:S(2)}) collective-permute-start(f32[5,32]{1,0:T(8,128)S(1)} %add.187), channel_id=1, source_target_pairs={{0,128},{1,129},{2,130},{3,131},{4,132},{5,133},{6,134},{7,135},{8... | collective-permute-start | bytes 1928 | tf_op jit(solution)/shard_map/ppermute | solution.py:76
  258.7 13.1 %collective-permute-start.35 = (f32[5,32]{1,0:T(8,128)S(1)}, f32[5,32]{1,0:T(8,128)S(1)}, u32[]{:S(2)}, u32[]{:S(2)}) collective-permute-start(f32[5,32]{1,0:T(8,128)S(1)} %add.188), channel_id=1, source_target_pairs={{0,256},{1,257},{2,258},{3,259},{4,260},{5,261},{6,262},{7,263},{8... | collective-permute-start | bytes 1928 | tf_op jit(solution)/shard_map/ppermute | solution.py:76

commit v5 on v4

--- a/solution.py
+++ b/solution.py
@@ -90,13 +90,16 @@
     shape = grid_shape()
     per_dev = points.shape[0]
     positions, present = locate(near_boxes, per_dev, shape)
-    point_tiles = collect_halo(points, shape)
+    joined_tiles = collect_halo(jnp.concatenate([points, right_side], axis=1), shape)
+    point_tiles = joined_tiles[:, : points.shape[1]]
+    first_tiles = joined_tiles[:, points.shape[1] :]
     others = point_tiles[positions]
     kernel = jax.vmap(wendland)(points, others) * present[:, :, None, None]
     kernel = lax.optimization_barrier(kernel)
 
-    def operate(values):
-        gathered = collect_halo(values, shape)
+    def operate(values, gathered=None):
+        if gathered is None:
+            gathered = collect_halo(values, shape)
         near_values = gathered[positions]
         products = jnp.einsum(
             "bmrj,bmji->bri",
@@ -109,7 +112,7 @@
 
     residual0 = right_side
     direction0 = right_side
-    image0 = operate(direction0)
+    image0 = operate(direction0, first_tiles)
     image_sq = operate(image0)
     moments = all_sum(
         jnp.stack(

time: 283 us -> 293 us (1.035)
  waiting for transfers between devices: 57.7 us -> 102 us
  starting transfers between devices: 115 us -> 84.2 us
  local copies, waits for them, and re-layouts: 25.2 us -> 20.1 us
  other arithmetic: 34 us -> 37.3 us
    ppermute x9 -> x6, waiting for transfers between devices: 38.7 us -> 77.9 us  [collect_halo(): lower = lax.ppermute(current, AXES, neighbour_route(shape, dim, -1))]
    ppermute x9 -> x6, starting transfers between devices: 30.7 us -> 13.9 us  [collect_halo(): upper = lax.ppermute(current, AXES, neighbour_route(shape, dim, 1))]
    ppermute x9 -> x6, starting transfers between devices: 26.7 us -> 16.7 us  [collect_halo(): lower = lax.ppermute(current, AXES, neighbour_route(shape, dim, -1))]
    unnamed x40 -> x30, local copies, waits for them, and re-layouts: 14.6 us -> 8.38 us
    ppermute x9, starting transfers between devices: 58.1 us -> 53.6 us  [all_sum(): lax.ppermute(value, AXES, [(i, i ^ bit) for i in range(total)])]
    ppermute x9 -> x6, waiting for transfers between devices: 6.18 us -> 10.3 us  [collect_halo(): upper = lax.ppermute(current, AXES, neighbour_route(shape, dim, 1))]
  transfers between devices with their start and end apart: 27 -> 21, of which waited for: 17 -> 21; matrix products, arithmetic and copies ran while one was open for 16% -> 3% of each run, Pallas kernels for 0% -> 0%
where the time goes in v5:
time: 293 us; the launch traced here: 288 us
  waiting for transfers between devices  102 us (35%)
  starting transfers between devices  84.2 us (29%)
  matrix products  42.1 us (14%)
  other arithmetic  37.3 us (13%)
  local copies, waits for them, and re-layouts  20.1 us (7%)
    ppermute x6, waiting for transfers between devices, collect_halo(): lower = lax.ppermute(current, AXES, neighbour_route(shape, dim, -1))  77.9 us
    ppermute x9, starting transfers between devices, all_sum(): lax.ppermute(value, AXES, [(i, i ^ bit) for i in range(total)])  53.6 us
    dot_general x2, matrix products, operate(): jnp.einsum('bmrj,bmji->bri', near_values, kernel, precision=lax.Precision...  42.1 us
    mul x1, other arithmetic, per_device(): kernel = jax.vmap(wendland)(points, others) * present[:, :, None, None]  29.2 us
    ppermute x6, starting transfers between devices, collect_halo(): lower = lax.ppermute(current, AXES, neighbour_route(shape, dim, -1))  16.7 us
    ppermute x6, starting transfers between devices, collect_halo(): upper = lax.ppermute(current, AXES, neighbour_route(shape, dim, 1))  13.9 us
    ppermute x9, waiting for transfers between devices, all_sum(): lax.ppermute(value, AXES, [(i, i ^ bit) for i in range(total)])  13.4 us
    ppermute x6, waiting for transfers between devices, collect_halo(): upper = lax.ppermute(current, AXES, neighbour_route(shape, dim, 1))  10.3 us
  transfers between devices with their start and end apart: 21, of which 21 were waited for; matrix products, arithmetic and copies ran while one was open for 3% of the time, Pallas kernels for 0%

profile of v5, /device:TPU:1, one launch (start us, length us, event | category | flops | bytes accessed | tf_op | source)
XLA Modules:
  0.0 288.3 jit_solution(1936221095922278695)
XLA Ops:
  2.3 6.0 %collective-permute-start.10 = (f32[4,35,256]{2,1,0:T(8,128)S(1)}, f32[4,35,256]{2,1,0:T(8,128)S(1)}, u32[]{:S(2)}, u32[]{:S(2)}) collective-permute-start(f32[4,35,256]{2,1,0:T(8,128)S(1)} %pad_maximum_fusion.3), channel_id=1, source_target_pairs={{8,0},{9,1},{10,2},{11,3},{12,4},{13,5},{14,6},{15,7},{16,8},{17,9... | collective-permute-start | bytes 430088 | tf_op jit(solution)/shard_map/ppermute | solution.py:42
  8.3 1.9 collective-permute-start.9
  10.6 8.5 %collective-permute-done.9 = f32[4,35,256]{2,1,0:T(8,128)S(1)} collective-permute-done((f32[4,35,256]{2,1,0:T(8,128)S(1)}, f32[4,35,256]{2,1,0:T(8,128)S(1)}, u32[]{:S(2)}, u32[]{:S(2)}) %collective-permute-start.9) | collective-permute-done | bytes 143392 | tf_op jit(solution)/shard_map/ppermute | solution.py:41
  22.7 9.3 %collective-permute-done.11 = f32[12,35,256]{2,1,0:T(8,128)S(1)} collective-permute-done((f32[12,35,256]{2,1,0:T(8,128)S(1)}, f32[12,35,256]{2,1,0:T(8,128)S(1)}, u32[]{:S(2)}, u32[]{:S(2)}) %collective-permute-start.11) | collective-permute-done | bytes 430112 | tf_op jit(solution)/shard_map/ppermute | solution.py:41
  33.0 2.9 collective-permute-done.12
  36.3 3.3 %collective-permute-start.13 = (f32[36,35,256]{2,0,1:T(8,128)S(1)}, f32[36,35,256]{2,0,1:T(8,128)}, u32[]{:S(2)}, u32[]{:S(2)}) collective-permute-start(f32[36,35,256]{2,0,1:T(8,128)S(1)} %copy.26), channel_id=1, source_target_pairs={{0,32},{1,33},{2,34},{3,35},{4,36},{5,37},{6,38},{7,39},{8,40},{9,... | collective-permute-start | bytes 3870728 | tf_op jit(solution)/shard_map/ppermute | solution.py:41
  41.6 27.7 %collective-permute-done.13 = f32[36,35,256]{2,0,1:T(8,128)} collective-permute-done((f32[36,35,256]{2,0,1:T(8,128)S(1)}, f32[36,35,256]{2,0,1:T(8,128)}, u32[]{:S(2)}, u32[]{:S(2)}) %collective-permute-start.13) | collective-permute-done | bytes 1290272 | tf_op jit(solution)/shard_map/ppermute | solution.py:41
  71.2 3.1 %collective-permute-done.14 = f32[36,35,256]{2,0,1:T(8,128)S(1)} collective-permute-done((f32[36,35,256]{2,0,1:T(8,128)S(1)}, f32[36,35,256]{2,0,1:T(8,128)S(1)}, u32[]{:S(2)}, u32[]{:S(2)}) %collective-permute-start.14) | collective-permute-done | bytes 1290272 | tf_op jit(solution)/shard_map/ppermute | solution.py:42
  76.2 2.6 gather_fusion
  81.0 29.2 %fusion.8 = f32[4,27,256,256]{3,2,1,0:T(8,128)} fusion(f32[4,27]{1,0:T(4,128)} %compare_convert_fusion, f32[4,256]{1,0:T(4,128)S(1)} %get-tuple-element.72, f32[4,27,256]{2,1,0:T(8,128)S(1)} %get-tuple-element.77, f32[4,256]{1,0:T(4,128)S(1)} %get-tuple-element.73, f32[4,27,256]{2,1,0:T(8,128)S(1)} %get-tuple-element.78, f32[4,256]{1,0:T(4,128)S(1)} %get-tuple-element.71, ...), kind=kLoop, calls=%fused_computation.29 | loop fusion | flops 127401984 | bytes 28656048 | tf_op jit(solution)/shard_map/mul | solution.py:97
  110.1 20.7 %fusion.10 = f32[4,32,256]{2,1,0:T(8,128)} fusion(f32[4,27,32,256]{3,2,1,0:T(8,128)S(1)} %bitcast.95, f32[4,27,256,256]{3,2,1,0:T(8,128)} %fusion.8, f32[4,32,256]{2,1,0:T(8,128)} %param.5), kind=kOutput, calls=%fused_computation.35 | convolution fusion | flops 2718007296 | bytes 32112640 | tf_op jit(solution)/shard_map/bmrj,bmji->bri/dot_general | solution.py:104
  130.8 2.6 collective-permute-start.16
  133.4 4.3 %collective-permute-start.15 = (f32[4,32,256]{2,1,0:T(8,128)}, f32[4,32,256]{2,1,0:T(8,128)S(1)}, u32[]{:S(2)}, u32[]{:S(2)}) collective-permute-start(f32[4,32,256]{2,1,0:T(8,128)} %fusion.10), channel_id=1, source_target_pairs={{0,8},{1,9},{2,10},{3,11},{4,12},{5,13},{6,14},{7,15},{8,16},{9,17... | collective-permute-start | bytes 393224 | tf_op jit(solution)/shard_map/ppermute | solution.py:41
  138.4 3.5 %collective-permute-done.15 = f32[4,32,256]{2,1,0:T(8,128)S(1)} collective-permute-done((f32[4,32,256]{2,1,0:T(8,128)}, f32[4,32,256]{2,1,0:T(8,128)S(1)}, u32[]{:S(2)}, u32[]{:S(2)}) %collective-permute-start.15) | collective-permute-done | bytes 131104 | tf_op jit(solution)/shard_map/ppermute | solution.py:41
  142.8 3.2 %collective-permute-start.17 = (f32[12,32,256]{2,1,0:T(8,128)S(1)}, f32[12,32,256]{2,1,0:T(8,128)S(1)}, u32[]{:S(2)}, u32[]{:S(2)}) collective-permute-start(f32[12,32,256]{2,1,0:T(8,128)S(1)} %pad_maximum_fusion.2), channel_id=1, source_target_pairs={{0,1},{1,2},{2,3},{3,4},{4,5},{5,6},{6,7},{8,9},{9,10},{10,11},{11... | collective-permute-start | bytes 1179656 | tf_op jit(solution)/shard_map/ppermute | solution.py:41
  147.3 6.8 %collective-permute-done.17 = f32[12,32,256]{2,1,0:T(8,128)S(1)} collective-permute-done((f32[12,32,256]{2,1,0:T(8,128)S(1)}, f32[12,32,256]{2,1,0:T(8,128)S(1)}, u32[]{:S(2)}, u32[]{:S(2)}) %collective-permute-start.17) | collective-permute-done | bytes 393248 | tf_op jit(solution)/shard_map/ppermute | solution.py:41
  155.0 2.9 collective-permute-done.18
  157.9 2.7 collective-permute-start.19
  162.1 22.2 %collective-permute-done.19 = f32[36,32,256]{2,1,0:T(8,128)S(1)} collective-permute-done((f32[36,32,256]{2,1,0:T(8,128)S(1)}, f32[36,32,256]{2,1,0:T(8,128)S(1)}, u32[]{:S(2)}, u32[]{:S(2)}) %collective-permute-start.19) | collective-permute-done | bytes 1179680 | tf_op jit(solution)/shard_map/ppermute | solution.py:41
  190.7 2.8 gather_fusion.2
  193.5 21.4 %multiply_reduce_fusion.4 = (f32[32]{0:T(128)S(1)}, f32[32]{0:T(128)S(1)}, f32[32]{0:T(128)S(1)}, f32[32]{0:T(128)S(1)}, f32[32]{0:T(128)}, /*index=5*/f32[4,32,256]{2,1,0:T(8,128)}) fusion(f32[4,32,256]{2,1,0:T(8,128)} %fusion.10, f32[4,32,256]{2,1,0:T(8,128)} %param.5, f32[4,27,32,256]{3,2,1,0:T(8,128)S(1)} %bitcast.94, f32[4,27,256,256]{3,2,1,0:T(8,128)} %fusion.8), kind=kOutput, calls=%fused_computation.44 | convolution fusion | flops 2718334720 | bytes 32244352 | tf_op jit(solution)/shard_map/bmrj,bmji->bri/dot_general | solution.py:104
  215.6 5.0 %collective-permute-start.21 = (f32[5,32]{1,0:T(8,128)S(1)}, f32[5,32]{1,0:T(8,128)S(1)}, u32[]{:S(2)}, u32[]{:S(2)}) collective-permute-start(f32[5,32]{1,0:T(8,128)S(1)} %stack.38), channel_id=1, source_target_pairs={{0,1},{1,0},{2,3},{3,2},{4,5},{5,4},{6,7},{7,6},{8,9},{9,8},{10,11... | collective-permute-start | bytes 1928 | tf_op jit(solution)/shard_map/ppermute | solution.py:76
  221.5 5.8 %collective-permute-start.22 = (f32[5,32]{1,0:T(8,128)S(1)}, f32[5,32]{1,0:T(8,128)S(1)}, u32[]{:S(2)}, u32[]{:S(2)}) collective-permute-start(f32[5,32]{1,0:T(8,128)S(1)} %add.181), channel_id=1, source_target_pairs={{0,2},{1,3},{2,0},{3,1},{4,6},{5,7},{6,4},{7,5},{8,10},{9,11},{10,... | collective-permute-start | bytes 1928 | tf_op jit(solution)/shard_map/ppermute | solution.py:76
  228.3 2.2 collective-permute-start.23
  230.5 2.1 collective-permute-done.23
  232.7 1.9 collective-permute-start.24
  234.6 3.9 %collective-permute-done.24 = f32[5,32]{1,0:T(8,128)S(1)} collective-permute-done((f32[5,32]{1,0:T(8,128)S(1)}, f32[5,32]{1,0:T(8,128)S(1)}, u32[]{:S(2)}, u32[]{:S(2)}) %collective-permute-start.24) | collective-permute-done | bytes 672 | tf_op jit(solution)/shard_map/ppermute | solution.py:76
  238.5 8.0 %collective-permute-start.25 = (f32[5,32]{1,0:T(8,128)S(1)}, f32[5,32]{1,0:T(8,128)S(1)}, u32[]{:S(2)}, u32[]{:S(2)}) collective-permute-start(f32[5,32]{1,0:T(8,128)S(1)} %add.184), channel_id=1, source_target_pairs={{0,16},{1,17},{2,18},{3,19},{4,20},{5,21},{6,22},{7,23},{8,24},{9,... | collective-permute-start | bytes 1928 | tf_op jit(solution)/shard_map/ppermute | solution.py:76
  247.3 4.6 %collective-permute-start.26 = (f32[5,32]{1,0:T(8,128)S(1)}, f32[5,32]{1,0:T(8,128)S(1)}, u32[]{:S(2)}, u32[]{:S(2)}) collective-permute-start(f32[5,32]{1,0:T(8,128)S(1)} %add.185), channel_id=1, source_target_pairs={{0,32},{1,33},{2,34},{3,35},{4,36},{5,37},{6,38},{7,39},{8,40},{9,... | collective-permute-start | bytes 1928 | tf_op jit(solution)/shard_map/ppermute | solution.py:76
  252.9 5.9 %collective-permute-start.27 = (f32[5,32]{1,0:T(8,128)S(1)}, f32[5,32]{1,0:T(8,128)S(1)}, u32[]{:S(2)}, u32[]{:S(2)}) collective-permute-start(f32[5,32]{1,0:T(8,128)S(1)} %add.186), channel_id=1, source_target_pairs={{0,64},{1,65},{2,66},{3,67},{4,68},{5,69},{6,70},{7,71},{8,72},{9,... | collective-permute-start | bytes 1928 | tf_op jit(solution)/shard_map/ppermute | solution.py:76
  259.8 8.8 %collective-permute-start.28 = (f32[5,32]{1,0:T(8,128)S(1)}, f32[5,32]{1,0:T(8,128)S(1)}, u32[]{:S(2)}, u32[]{:S(2)}) collective-permute-start(f32[5,32]{1,0:T(8,128)S(1)} %add.187), channel_id=1, source_target_pairs={{0,128},{1,129},{2,130},{3,131},{4,132},{5,133},{6,134},{7,135},{8... | collective-permute-start | bytes 1928 | tf_op jit(solution)/shard_map/ppermute | solution.py:76
  269.6 11.4 %collective-permute-start.29 = (f32[5,32]{1,0:T(8,128)S(1)}, f32[5,32]{1,0:T(8,128)S(1)}, u32[]{:S(2)}, u32[]{:S(2)}) collective-permute-start(f32[5,32]{1,0:T(8,128)S(1)} %add.188), channel_id=1, source_target_pairs={{0,256},{1,257},{2,258},{3,259},{4,260},{5,261},{6,262},{7,263},{8... | collective-permute-start | bytes 1928 | tf_op jit(solution)/shard_map/ppermute | solution.py:76
  (82 shorter events, 40.3 us)
Async XLA Ops:
  1.3 38.2 %copy-start.4 = (s32[4,27]{1,0:T(4,128)S(1)}, s32[4,27]{1,0:T(4,128)}, u32[]{:S(2)}) copy-start(s32[4,27]{1,0:T(4,128)} %param.7) | copy-start | bytes 1300
  1.3 40.2 %copy-start.3 = (f32[4,3,256]{2,0,1:T(4,128)S(1)}, f32[4,3,256]{2,0,1:T(4,128)}, u32[]{:S(2)}) copy-start(f32[4,3,256]{2,0,1:T(4,128)} %param.6) | copy-start | bytes 36868
  2.3 8.3 %collective-permute-start.10 = (f32[4,35,256]{2,1,0:T(8,128)S(1)}, f32[4,35,256]{2,1,0:T(8,128)S(1)}, u32[]{:S(2)}, u32[]{:S(2)}) collective-permute-start(f32[4,35,256]{2,1,0:T(8,128)S(1)} %pad_maximum_fusion.3), channel_id=1, source_target_pairs={{8,0},{9,1},{10,2},{11,3},{12,4},{13,5},{14,6},{15,7},{16,8},{17,9... | collective-permute-start | bytes 430088 | tf_op jit(solution)/shard_map/ppermute | solution.py:42
  8.3 10.8 %collective-permute-start.9 = (f32[4,35,256]{2,1,0:T(8,128)S(1)}, f32[4,35,256]{2,1,0:T(8,128)S(1)}, u32[]{:S(2)}, u32[]{:S(2)}) collective-permute-start(f32[4,35,256]{2,1,0:T(8,128)S(1)} %pad_maximum_fusion.3), channel_id=1, source_target_pairs={{0,8},{1,9},{2,10},{3,11},{4,12},{5,13},{6,14},{7,15},{8,16},{9,17... | collective-permute-start | bytes 430088 | tf_op jit(solution)/shard_map/ppermute | solution.py:41
  20.0 11.9 %collective-permute-start.11 = (f32[12,35,256]{2,1,0:T(8,128)S(1)}, f32[12,35,256]{2,1,0:T(8,128)S(1)}, u32[]{:S(2)}, u32[]{:S(2)}) collective-permute-start(f32[12,35,256]{2,1,0:T(8,128)S(1)} %pad_maximum_fusion.1), channel_id=1, source_target_pairs={{0,1},{1,2},{2,3},{3,4},{4,5},{5,6},{6,7},{8,9},{9,10},{10,11},{11... | collective-permute-start | bytes 1290248 | tf_op jit(solution)/shard_map/ppermute | solution.py:41
  21.4 14.4 %collective-permute-start.12 = (f32[12,35,256]{2,1,0:T(8,128)S(1)}, f32[12,35,256]{2,1,0:T(8,128)S(1)}, u32[]{:S(2)}, u32[]{:S(2)}) collective-permute-start(f32[12,35,256]{2,1,0:T(8,128)S(1)} %pad_maximum_fusion.1), channel_id=1, source_target_pairs={{1,0},{2,1},{3,2},{4,3},{5,4},{6,5},{7,6},{9,8},{10,9},{11,10},{12... | collective-permute-start | bytes 1290248 | tf_op jit(solution)/shard_map/ppermute | solution.py:42
  35.9 35.3 %copy-start.1 = (f32[4,32,256]{2,1,0:T(8,128)S(1)}, f32[4,32,256]{2,1,0:T(8,128)}, u32[]{:S(2)}) copy-start(f32[4,32,256]{2,1,0:T(8,128)} %param.5) | copy-start | bytes 393220
  36.3 33.0 %collective-permute-start.13 = (f32[36,35,256]{2,0,1:T(8,128)S(1)}, f32[36,35,256]{2,0,1:T(8,128)}, u32[]{:S(2)}, u32[]{:S(2)}) collective-permute-start(f32[36,35,256]{2,0,1:T(8,128)S(1)} %copy.26), channel_id=1, source_target_pairs={{0,32},{1,33},{2,34},{3,35},{4,36},{5,37},{6,38},{7,39},{8,40},{9,... | collective-permute-start | bytes 3870728 | tf_op jit(solution)/shard_map/ppermute | solution.py:41
  39.7 34.6 %collective-permute-start.14 = (f32[36,35,256]{2,0,1:T(8,128)S(1)}, f32[36,35,256]{2,0,1:T(8,128)S(1)}, u32[]{:S(2)}, u32[]{:S(2)}) collective-permute-start(f32[36,35,256]{2,0,1:T(8,128)S(1)} %copy.26), channel_id=1, source_target_pairs={{32,0},{33,1},{34,2},{35,3},{36,4},{37,5},{38,6},{39,7},{40,8},{41... | collective-permute-start | bytes 3870728 | tf_op jit(solution)/shard_map/ppermute | solution.py:42
  81.0 29.2 %copy-start = (f32[108,32,256]{2,1,0:T(8,128)S(1)}, f32[108,32,256]{2,1,0:T(8,128)}, u32[]{:S(2)}) copy-start(f32[108,32,256]{2,1,0:T(8,128)} %gather_fusion) | copy-start | bytes 10616836
  130.8 56.1 %copy-start.2 = (f32[4,32,256]{2,1,0:T(8,128)S(1)}, f32[4,32,256]{2,1,0:T(8,128)}, u32[]{:S(2)}) copy-start(f32[4,32,256]{2,1,0:T(8,128)} %fusion.10) | copy-start | bytes 393220
  130.8 7.5 %collective-permute-start.16 = (f32[4,32,256]{2,1,0:T(8,128)}, f32[4,32,256]{2,1,0:T(8,128)S(1)}, u32[]{:S(2)}, u32[]{:S(2)}) collective-permute-start(f32[4,32,256]{2,1,0:T(8,128)} %fusion.10), channel_id=1, source_target_pairs={{8,0},{9,1},{10,2},{11,3},{12,4},{13,5},{14,6},{15,7},{16,8},{17,9... | collective-permute-start | bytes 393224 | tf_op jit(solution)/shard_map/ppermute | solution.py:42
  133.4 8.4 %collective-permute-start.15 = (f32[4,32,256]{2,1,0:T(8,128)}, f32[4,32,256]{2,1,0:T(8,128)S(1)}, u32[]{:S(2)}, u32[]{:S(2)}) collective-permute-start(f32[4,32,256]{2,1,0:T(8,128)} %fusion.10), channel_id=1, source_target_pairs={{0,8},{1,9},{2,10},{3,11},{4,12},{5,13},{6,14},{7,15},{8,16},{9,17... | collective-permute-start | bytes 393224 | tf_op jit(solution)/shard_map/ppermute | solution.py:41
  142.8 11.3 %collective-permute-start.17 = (f32[12,32,256]{2,1,0:T(8,128)S(1)}, f32[12,32,256]{2,1,0:T(8,128)S(1)}, u32[]{:S(2)}, u32[]{:S(2)}) collective-permute-start(f32[12,32,256]{2,1,0:T(8,128)S(1)} %pad_maximum_fusion.2), channel_id=1, source_target_pairs={{0,1},{1,2},{2,3},{3,4},{4,5},{5,6},{6,7},{8,9},{9,10},{10,11},{11... | collective-permute-start | bytes 1179656 | tf_op jit(solution)/shard_map/ppermute | solution.py:41
  146.0 11.9 %collective-permute-start.18 = (f32[12,32,256]{2,1,0:T(8,128)S(1)}, f32[12,32,256]{2,1,0:T(8,128)S(1)}, u32[]{:S(2)}, u32[]{:S(2)}) collective-permute-start(f32[12,32,256]{2,1,0:T(8,128)S(1)} %pad_maximum_fusion.2), channel_id=1, source_target_pairs={{1,0},{2,1},{3,2},{4,3},{5,4},{6,5},{7,6},{9,8},{10,9},{11,10},{12... | collective-permute-start | bytes 1179656 | tf_op jit(solution)/shard_map/ppermute | solution.py:42
  157.9 26.3 %collective-permute-start.19 = (f32[36,32,256]{2,1,0:T(8,128)S(1)}, f32[36,32,256]{2,1,0:T(8,128)S(1)}, u32[]{:S(2)}, u32[]{:S(2)}) collective-permute-start(f32[36,32,256]{2,1,0:T(8,128)S(1)} %constant_dynamic-update-slice_fusion.10), channel_id=1, source_target_pairs={{0,32},{1,33},{2,34},{3,35},{4,36},{5,37},{6,38},{7,39},{8,40},{9,... | collective-permute-start | bytes 3538952 | tf_op jit(solution)/shard_map/ppermute | solution.py:41
  160.6 28.9 %collective-permute-start.20 = (f32[36,32,256]{2,1,0:T(8,128)S(1)}, f32[36,32,256]{2,1,0:T(8,128)S(1)}, u32[]{:S(2)}, u32[]{:S(2)}) collective-permute-start(f32[36,32,256]{2,1,0:T(8,128)S(1)} %constant_dynamic-update-slice_fusion.10), channel_id=1, source_target_pairs={{32,0},{33,1},{34,2},{35,3},{36,4},{37,5},{38,6},{39,7},{40,8},{41... | collective-permute-start | bytes 3538952 | tf_op jit(solution)/shard_map/ppermute | solution.py:42
  215.6 6.0 %collective-permute-start.21 = (f32[5,32]{1,0:T(8,128)S(1)}, f32[5,32]{1,0:T(8,128)S(1)}, u32[]{:S(2)}, u32[]{:S(2)}) collective-permute-start(f32[5,32]{1,0:T(8,128)S(1)} %stack.38), channel_id=1, source_target_pairs={{0,1},{1,0},{2,3},{3,2},{4,5},{5,4},{6,7},{7,6},{8,9},{9,8},{10,11... | collective-permute-start | bytes 1928 | tf_op jit(solution)/shard_map/ppermute | solution.py:76
  221.5 6.8 %collective-permute-start.22 = (f32[5,32]{1,0:T(8,128)S(1)}, f32[5,32]{1,0:T(8,128)S(1)}, u32[]{:S(2)}, u32[]{:S(2)}) collective-permute-start(f32[5,32]{1,0:T(8,128)S(1)} %add.181), channel_id=1, source_target_pairs={{0,2},{1,3},{2,0},{3,1},{4,6},{5,7},{6,4},{7,5},{8,10},{9,11},{10,... | collective-permute-start | bytes 1928 | tf_op jit(solution)/shard_map/ppermute | solution.py:76
  228.3 4.3 %collective-permute-start.23 = (f32[5,32]{1,0:T(8,128)S(1)}, f32[5,32]{1,0:T(8,128)S(1)}, u32[]{:S(2)}, u32[]{:S(2)}) collective-permute-start(f32[5,32]{1,0:T(8,128)S(1)} %add.182), channel_id=1, source_target_pairs={{0,4},{1,5},{2,6},{3,7},{4,0},{5,1},{6,2},{7,3},{8,12},{9,13},{10,... | collective-permute-start | bytes 1928 | tf_op jit(solution)/shard_map/ppermute | solution.py:76
  232.7 5.8 %collective-permute-start.24 = (f32[5,32]{1,0:T(8,128)S(1)}, f32[5,32]{1,0:T(8,128)S(1)}, u32[]{:S(2)}, u32[]{:S(2)}) collective-permute-start(f32[5,32]{1,0:T(8,128)S(1)} %add.183), channel_id=1, source_target_pairs={{0,8},{1,9},{2,10},{3,11},{4,12},{5,13},{6,14},{7,15},{8,0},{9,1},... | collective-permute-start | bytes 1928 | tf_op jit(solution)/shard_map/ppermute | solution.py:76
  238.5 8.8 %collective-permute-start.25 = (f32[5,32]{1,0:T(8,128)S(1)}, f32[5,32]{1,0:T(8,128)S(1)}, u32[]{:S(2)}, u32[]{:S(2)}) collective-permute-start(f32[5,32]{1,0:T(8,128)S(1)} %add.184), channel_id=1, source_target_pairs={{0,16},{1,17},{2,18},{3,19},{4,20},{5,21},{6,22},{7,23},{8,24},{9,... | collective-permute-start | bytes 1928 | tf_op jit(solution)/shard_map/ppermute | solution.py:76
  247.3 5.6 %collective-permute-start.26 = (f32[5,32]{1,0:T(8,128)S(1)}, f32[5,32]{1,0:T(8,128)S(1)}, u32[]{:S(2)}, u32[]{:S(2)}) collective-permute-start(f32[5,32]{1,0:T(8,128)S(1)} %add.185), channel_id=1, source_target_pairs={{0,32},{1,33},{2,34},{3,35},{4,36},{5,37},{6,38},{7,39},{8,40},{9,... | collective-permute-start | bytes 1928 | tf_op jit(solution)/shard_map/ppermute | solution.py:76
  252.9 6.9 %collective-permute-start.27 = (f32[5,32]{1,0:T(8,128)S(1)}, f32[5,32]{1,0:T(8,128)S(1)}, u32[]{:S(2)}, u32[]{:S(2)}) collective-permute-start(f32[5,32]{1,0:T(8,128)S(1)} %add.186), channel_id=1, source_target_pairs={{0,64},{1,65},{2,66},{3,67},{4,68},{5,69},{6,70},{7,71},{8,72},{9,... | collective-permute-start | bytes 1928 | tf_op jit(solution)/shard_map/ppermute | solution.py:76
  259.8 9.8 %collective-permute-start.28 = (f32[5,32]{1,0:T(8,128)S(1)}, f32[5,32]{1,0:T(8,128)S(1)}, u32[]{:S(2)}, u32[]{:S(2)}) collective-permute-start(f32[5,32]{1,0:T(8,128)S(1)} %add.187), channel_id=1, source_target_pairs={{0,128},{1,129},{2,130},{3,131},{4,132},{5,133},{6,134},{7,135},{8... | collective-permute-start | bytes 1928 | tf_op jit(solution)/shard_map/ppermute | solution.py:76
  269.6 13.1 %collective-permute-start.29 = (f32[5,32]{1,0:T(8,128)S(1)}, f32[5,32]{1,0:T(8,128)S(1)}, u32[]{:S(2)}, u32[]{:S(2)}) collective-permute-start(f32[5,32]{1,0:T(8,128)S(1)} %add.188), channel_id=1, source_target_pairs={{0,256},{1,257},{2,258},{3,259},{4,260},{5,261},{6,262},{7,263},{8... | collective-permute-start | bytes 1928 | tf_op jit(solution)/shard_map/ppermute | solution.py:76

commit v6 on v4

--- a/solution.py
+++ b/solution.py
@@ -70,11 +70,10 @@
 
 
 def all_sum(value):
-    total = lax.axis_size("leaf") * lax.axis_size("sub")
-    bit = 1
-    while bit < total:
-        value = value + lax.ppermute(value, AXES, [(i, i ^ bit) for i in range(total)])
-        bit *= 2
+    for axis in ("sub", "leaf"):
+        size = lax.axis_size(axis)
+        copies = jnp.broadcast_to(value[None], (size,) + value.shape)
+        value = jnp.sum(lax.all_to_all(copies, axis, 0, 0, tiled=False), axis=0)
     return value
 
 

time: 283 us -> 250 us (0.88); the launches traced: 278 us -> 249 us
  starting transfers between devices: 115 us -> 54 us
  blocking collectives: 0 us -> 50.6 us
  waiting for transfers between devices: 57.7 us -> 38.2 us
    ppermute x9 -> x0, starting transfers between devices: 58.1 us -> none  [all_sum(): lax.ppermute(value, AXES, [(i, i ^ bit) for i in range(total)])]
    all_to_all x0 -> x2, blocking collectives: none -> 50.6 us  [all_sum(): value = jnp.sum(lax.all_to_all(copies, axis, 0, 0, tiled=False), axis=0)]
    ppermute x9 -> x0, waiting for transfers between devices: 12.8 us -> none  [all_sum(): lax.ppermute(value, AXES, [(i, i ^ bit) for i in range(total)])]
    ppermute x9, waiting for transfers between devices: 38.7 us -> 27 us  [collect_halo(): lower = lax.ppermute(current, AXES, neighbour_route(shape, dim, -1))]
    ppermute x9, starting transfers between devices: 30.7 us -> 21.3 us  [collect_halo(): upper = lax.ppermute(current, AXES, neighbour_route(shape, dim, 1))]
    ppermute x9, starting transfers between devices: 26.7 us -> 32.7 us  [collect_halo(): lower = lax.ppermute(current, AXES, neighbour_route(shape, dim, -1))]
    ppermute x9, waiting for transfers between devices: 6.18 us -> 11.2 us  [collect_halo(): upper = lax.ppermute(current, AXES, neighbour_route(shape, dim, 1))]
    unnamed x40 -> x44, local copies, waits for them, and re-layouts: 14.6 us -> 14.8 us
  transfers between devices with their start and end apart: 27 -> 18, of which waited for: 17 -> 9; matrix products, arithmetic and copies ran while one was open for 16% -> 18% of each run, Pallas kernels for 0% -> 0%
where the time goes in v6:
time: 250 us; the launch traced here: 249 us
  starting transfers between devices  54 us (22%)
  blocking collectives  50.6 us (20%)
  matrix products  42.1 us (17%)
  waiting for transfers between devices  38.2 us (15%)
  other arithmetic  35.5 us (14%)
  local copies, waits for them, and re-layouts  25.9 us (10%)
  between operations  3.1 us (1%)
    all_to_all x2, blocking collectives, all_sum(): value = jnp.sum(lax.all_to_all(copies, axis, 0, 0, tiled=False), axis=0)  50.6 us
    dot_general x2, matrix products, operate(): jnp.einsum('bmrj,bmji->bri', near_values, kernel, precision=lax.Precision...  42.1 us
    ppermute x9, starting transfers between devices, collect_halo(): lower = lax.ppermute(current, AXES, neighbour_route(shape, dim, -1))  32.7 us
    mul x1, other arithmetic, per_device(): kernel = jax.vmap(wendland)(points, others) * present[:, :, None, None]  27.8 us
    ppermute x9, waiting for transfers between devices, collect_halo(): lower = lax.ppermute(current, AXES, neighbour_route(shape, dim, -1))  27 us
    ppermute x9, starting transfers between devices, collect_halo(): upper = lax.ppermute(current, AXES, neighbour_route(shape, dim, 1))  21.3 us
    unnamed x44, local copies, waits for them, and re-layouts  14.8 us
    ppermute x9, waiting for transfers between devices, collect_halo(): upper = lax.ppermute(current, AXES, neighbour_route(shape, dim, 1))  11.2 us
  transfers between devices with their start and end apart: 18, of which 9 were waited for; matrix products, arithmetic and copies ran while one was open for 18% of the time, Pallas kernels for 0%

profile of v6, /device:TPU:1, one launch (start us, length us, event | category | flops | bytes accessed | tf_op | source)
XLA Modules:
  0.0 249.4 jit_solution(85414664831601465)
XLA Ops:
  1.4 5.5 %collective-permute-start.6 = (f32[4,3,256]{2,1,0:T(4,128)S(1)}, f32[4,3,256]{2,1,0:T(4,128)S(1)}, u32[]{:S(2)}, u32[]{:S(2)}) collective-permute-start(f32[4,3,256]{2,1,0:T(4,128)S(1)} %copy.23), channel_id=1, source_target_pairs={{0,8},{1,9},{2,10},{3,11},{4,12},{5,13},{6,14},{7,15},{8,16},{9,17... | collective-permute-start | bytes 36872 | tf_op jit(solution)/shard_map/ppermute | solution.py:41
  6.9 2.5 collective-permute-start.7
  9.3 4.3 %collective-permute-start = (f32[4,32,256]{2,1,0:T(8,128)}, f32[4,32,256]{2,1,0:T(8,128)S(1)}, u32[]{:S(2)}, u32[]{:S(2)}) collective-permute-start(f32[4,32,256]{2,1,0:T(8,128)} %param.5), channel_id=1, source_target_pairs={{0,8},{1,9},{2,10},{3,11},{4,12},{5,13},{6,14},{7,15},{8,16},{9,17... | collective-permute-start | bytes 393224 | tf_op jit(solution)/shard_map/ppermute | solution.py:41
  13.7 4.8 %collective-permute-start.1 = (f32[4,32,256]{2,1,0:T(8,128)}, f32[4,32,256]{2,1,0:T(8,128)S(1)}, u32[]{:S(2)}, u32[]{:S(2)}) collective-permute-start(f32[4,32,256]{2,1,0:T(8,128)} %param.5), channel_id=1, source_target_pairs={{8,0},{9,1},{10,2},{11,3},{12,4},{13,5},{14,6},{15,7},{16,8},{17,9... | collective-permute-start | bytes 393224 | tf_op jit(solution)/shard_map/ppermute | solution.py:42
  21.4 1.5 collective-permute-start.8
  22.9 1.3 collective-permute-start.9
  25.0 3.1 %collective-permute-done.9 = f32[12,3,256]{2,1,0:T(4,128)S(1)} collective-permute-done((f32[12,3,256]{2,1,0:T(4,128)S(1)}, f32[12,3,256]{2,1,0:T(4,128)S(1)}, u32[]{:S(2)}, u32[]{:S(2)}) %collective-permute-start.9) | collective-permute-done | bytes 36896 | tf_op jit(solution)/shard_map/ppermute | solution.py:42
  28.1 3.5 %collective-permute-start.10 = (f32[36,3,256]{2,1,0:T(4,128)S(1)}, f32[36,3,256]{2,1,0:T(4,128)S(1)}, u32[]{:S(2)}, u32[]{:S(2)}) collective-permute-start(f32[36,3,256]{2,1,0:T(4,128)S(1)} %constant_dynamic-update-slice_fusion.18), channel_id=1, source_target_pairs={{0,32},{1,33},{2,34},{3,35},{4,36},{5,37},{6,38},{7,39},{8,40},{9,... | collective-permute-start | bytes 331784 | tf_op jit(solution)/shard_map/ppermute | solution.py:41
  31.6 1.3 collective-permute-start.11
  33.9 3.2 %collective-permute-start.2 = (f32[12,32,256]{2,1,0:T(8,128)S(1)}, f32[12,32,256]{2,1,0:T(8,128)S(1)}, u32[]{:S(2)}, u32[]{:S(2)}) collective-permute-start(f32[12,32,256]{2,1,0:T(8,128)S(1)} %constant_dynamic-update-slice_fusion), channel_id=1, source_target_pairs={{0,1},{1,2},{2,3},{3,4},{4,5},{5,6},{6,7},{8,9},{9,10},{10,11},{11... | collective-permute-start | bytes 1179656 | tf_op jit(solution)/shard_map/ppermute | solution.py:41
  40.5 3.9 %collective-permute-done.2 = f32[12,32,256]{2,1,0:T(8,128)S(1)} collective-permute-done((f32[12,32,256]{2,1,0:T(8,128)S(1)}, f32[12,32,256]{2,1,0:T(8,128)S(1)}, u32[]{:S(2)}, u32[]{:S(2)}) %collective-permute-start.2) | collective-permute-done | bytes 393248 | tf_op jit(solution)/shard_map/ppermute | solution.py:41
  44.5 3.8 %collective-permute-done.3 = f32[12,32,256]{2,1,0:T(8,128)S(1)} collective-permute-done((f32[12,32,256]{2,1,0:T(8,128)S(1)}, f32[12,32,256]{2,1,0:T(8,128)S(1)}, u32[]{:S(2)}, u32[]{:S(2)}) %collective-permute-start.3) | collective-permute-done | bytes 393248 | tf_op jit(solution)/shard_map/ppermute | solution.py:42
  48.3 4.1 %collective-permute-start.4 = (f32[36,32,256]{2,1,0:T(8,128)S(1)}, f32[36,32,256]{2,1,0:T(8,128)S(1)}, u32[]{:S(2)}, u32[]{:S(2)}) collective-permute-start(f32[36,32,256]{2,1,0:T(8,128)S(1)} %constant_dynamic-update-slice_fusion.3), channel_id=1, source_target_pairs={{0,32},{1,33},{2,34},{3,35},{4,36},{5,37},{6,38},{7,39},{8,40},{9,... | collective-permute-start | bytes 3538952 | tf_op jit(solution)/shard_map/ppermute | solution.py:41
  52.4 1.3 collective-permute-start.5
  53.7 27.8 %fusion.7 = f32[4,27,256,256]{3,2,1,0:T(8,128)} fusion(f32[4,27]{1,0:T(4,128)S(1)} %compare_convert_fusion, f32[4,256]{1,0:T(4,128)S(1)} %get-tuple-element.70, f32[4,27,256]{2,1,0:T(8,128)S(1)} %get-tuple-element.75, f32[4,256]{1,0:T(4,128)S(1)} %get-tuple-element.71, f32[4,27,256]{2,1,0:T(8,128)S(1)} %get-tuple-element.76, ...), kind=kLoop, calls=%fused_computation.28 | loop fusion | flops 127401984 | bytes 28656048 | tf_op jit(solution)/shard_map/mul | solution.py:94
  87.5 2.8 %gather_fusion = f32[108,32,256]{2,1,0:T(8,128)S(1)} fusion(f32[108,32,256]{2,1,0:T(8,128)} %constant_dynamic-update-slice_fusion.8, s32[1024]{0:T(1024)S(1)} %pad_clamp_fusion), kind=kCustom, calls=%fused_computation | custom fusion | bytes 7078320 | tf_op jit(solution)/shard_map/gather | solution.py:99
  90.2 20.7 %fusion.9 = f32[4,32,256]{2,1,0:T(8,128)} fusion(f32[4,27,32,256]{3,2,1,0:T(8,128)S(1)} %bitcast.95, f32[4,27,256,256]{3,2,1,0:T(8,128)} %fusion.7, f32[4,32,256]{2,1,0:T(8,128)} %param.5), kind=kOutput, calls=%fused_computation.32 | convolution fusion | flops 2718007296 | bytes 32112640 | tf_op jit(solution)/shard_map/bmrj,bmji->bri/dot_general | solution.py:100
  110.9 2.0 collective-permute-start.12
  113.0 6.2 %collective-permute-start.13 = (f32[4,32,256]{2,1,0:T(8,128)}, f32[4,32,256]{2,1,0:T(8,128)S(1)}, u32[]{:S(2)}, u32[]{:S(2)}) collective-permute-start(f32[4,32,256]{2,1,0:T(8,128)} %fusion.9), channel_id=1, source_target_pairs={{8,0},{9,1},{10,2},{11,3},{12,4},{13,5},{14,6},{15,7},{16,8},{17,9... | collective-permute-start | bytes 393224 | tf_op jit(solution)/shard_map/ppermute | solution.py:42
  119.1 2.0 collective-permute-done.12
  122.4 4.3 %collective-permute-start.14 = (f32[12,32,256]{2,1,0:T(8,128)S(1)}, f32[12,32,256]{2,1,0:T(8,128)S(1)}, u32[]{:S(2)}, u32[]{:S(2)}) collective-permute-start(f32[12,32,256]{2,1,0:T(8,128)S(1)} %pad_maximum_fusion.1), channel_id=1, source_target_pairs={{0,1},{1,2},{2,3},{3,4},{4,5},{5,6},{6,7},{8,9},{9,10},{10,11},{11... | collective-permute-start | bytes 1179656 | tf_op jit(solution)/shard_map/ppermute | solution.py:41
  128.0 3.4 %collective-permute-done.14 = f32[12,32,256]{2,1,0:T(8,128)S(1)} collective-permute-done((f32[12,32,256]{2,1,0:T(8,128)S(1)}, f32[12,32,256]{2,1,0:T(8,128)S(1)}, u32[]{:S(2)}, u32[]{:S(2)}) %collective-permute-start.14) | collective-permute-done | bytes 393248 | tf_op jit(solution)/shard_map/ppermute | solution.py:41
  132.4 2.9 %collective-permute-done.15 = f32[12,32,256]{2,1,0:T(8,128)S(1)} collective-permute-done((f32[12,32,256]{2,1,0:T(8,128)S(1)}, f32[12,32,256]{2,1,0:T(8,128)S(1)}, u32[]{:S(2)}, u32[]{:S(2)}) %collective-permute-start.15) | collective-permute-done | bytes 393248 | tf_op jit(solution)/shard_map/ppermute | solution.py:42
  135.3 4.2 %collective-permute-start.16 = (f32[36,32,256]{2,1,0:T(8,128)S(1)}, f32[36,32,256]{2,1,0:T(8,128)S(1)}, u32[]{:S(2)}, u32[]{:S(2)}) collective-permute-start(f32[36,32,256]{2,1,0:T(8,128)S(1)} %constant_dynamic-update-slice_fusion.30), channel_id=1, source_target_pairs={{0,32},{1,33},{2,34},{3,35},{4,36},{5,37},{6,38},{7,39},{8,40},{9,... | collective-permute-start | bytes 3538952 | tf_op jit(solution)/shard_map/ppermute | solution.py:41
  139.4 1.5 collective-permute-start.17
  140.9 17.7 %collective-permute-done.16 = f32[36,32,256]{2,1,0:T(8,128)S(1)} collective-permute-done((f32[36,32,256]{2,1,0:T(8,128)S(1)}, f32[36,32,256]{2,1,0:T(8,128)S(1)}, u32[]{:S(2)}, u32[]{:S(2)}) %collective-permute-start.16) | collective-permute-done | bytes 1179680 | tf_op jit(solution)/shard_map/ppermute | solution.py:41
  165.7 2.8 %gather_fusion.2 = f32[108,32,256]{2,1,0:T(8,128)S(1)} fusion(f32[108,32,256]{2,1,0:T(8,128)} %constant_dynamic-update-slice_fusion.35, s32[1024]{0:T(1024)S(1)} %pad_clamp_fusion), kind=kCustom, calls=%fused_computation.2 | custom fusion | bytes 7078320 | tf_op jit(solution)/shard_map/gather | solution.py:99
  168.4 21.4 %multiply_reduce_fusion.4 = (f32[32]{0:T(128)S(1)}, f32[32]{0:T(128)S(1)}, f32[32]{0:T(128)S(1)}, f32[32]{0:T(128)S(1)}, f32[32]{0:T(128)}, /*index=5*/f32[4,32,256]{2,1,0:T(8,128)}) fusion(f32[4,32,256]{2,1,0:T(8,128)} %fusion.9, f32[4,32,256]{2,1,0:T(8,128)} %param.5, f32[4,27,32,256]{3,2,1,0:T(8,128)S(1)} %bitcast.94, f32[4,27,256,256]{3,2,1,0:T(8,128)} %fusion.7), kind=kOutput, calls=%fused_computation.39 | convolution fusion | flops 2718334720 | bytes 32244352 | tf_op jit(solution)/shard_map/bmrj,bmji->bri/dot_general | solution.py:100
  190.6 12.5 %all_to_all.20 = f32[16,1,160]{2,1,0:T(1,128)S(1)} all-to-all(f32[16,1,160]{2,1,0:T(1,128)S(1)} %reshape.58), channel_id=1, replica_groups=mesh['leaf'=32,'sub'=16] {'sub'}, dimensions={0} | all-to-all | bytes 20480 | tf_op jit(solution)/shard_map/all_to_all | solution.py:76
  204.6 38.1 %all_to_all.21 = f32[32,1,160]{2,1,0:T(1,128)S(1)} all-to-all(f32[32,1,160]{2,1,0:T(1,128)S(1)} %reshape.60), channel_id=1, replica_groups=mesh['leaf'=32,'sub'=16] {'leaf'}, dimensions={0} | all-to-all | bytes 40960 | tf_op jit(solution)/shard_map/all_to_all | solution.py:76
  247.5 1.9 conditional.1
  247.5 1.8 multiply_add_fusion.1
  (88 shorter events, 30.3 us)
Async XLA Ops:
  0.6 43.8 %copy-start = (f32[4,32,256]{2,1,0:T(8,128)S(1)}, f32[4,32,256]{2,1,0:T(8,128)}, u32[]{:S(2)}) copy-start(f32[4,32,256]{2,1,0:T(8,128)} %param.5) | copy-start | bytes 393220
  1.4 19.3 %collective-permute-start.6 = (f32[4,3,256]{2,1,0:T(4,128)S(1)}, f32[4,3,256]{2,1,0:T(4,128)S(1)}, u32[]{:S(2)}, u32[]{:S(2)}) collective-permute-start(f32[4,3,256]{2,1,0:T(4,128)S(1)} %copy.23), channel_id=1, source_target_pairs={{0,8},{1,9},{2,10},{3,11},{4,12},{5,13},{6,14},{7,15},{8,16},{9,17... | collective-permute-start | bytes 36872 | tf_op jit(solution)/shard_map/ppermute | solution.py:41
  6.9 14.5 %collective-permute-start.7 = (f32[4,3,256]{2,1,0:T(4,128)S(1)}, f32[4,3,256]{2,1,0:T(4,128)S(1)}, u32[]{:S(2)}, u32[]{:S(2)}) collective-permute-start(f32[4,3,256]{2,1,0:T(4,128)S(1)} %copy.23), channel_id=1, source_target_pairs={{8,0},{9,1},{10,2},{11,3},{12,4},{13,5},{14,6},{15,7},{16,8},{17,9... | collective-permute-start | bytes 36872 | tf_op jit(solution)/shard_map/ppermute | solution.py:42
  9.3 23.6 %collective-permute-start = (f32[4,32,256]{2,1,0:T(8,128)}, f32[4,32,256]{2,1,0:T(8,128)S(1)}, u32[]{:S(2)}, u32[]{:S(2)}) collective-permute-start(f32[4,32,256]{2,1,0:T(8,128)} %param.5), channel_id=1, source_target_pairs={{0,8},{1,9},{2,10},{3,11},{4,12},{5,13},{6,14},{7,15},{8,16},{9,17... | collective-permute-start | bytes 393224 | tf_op jit(solution)/shard_map/ppermute | solution.py:41
  13.7 20.2 %collective-permute-start.1 = (f32[4,32,256]{2,1,0:T(8,128)}, f32[4,32,256]{2,1,0:T(8,128)S(1)}, u32[]{:S(2)}, u32[]{:S(2)}) collective-permute-start(f32[4,32,256]{2,1,0:T(8,128)} %param.5), channel_id=1, source_target_pairs={{8,0},{9,1},{10,2},{11,3},{12,4},{13,5},{14,6},{15,7},{16,8},{17,9... | collective-permute-start | bytes 393224 | tf_op jit(solution)/shard_map/ppermute | solution.py:42
  21.4 2.8 %collective-permute-start.8 = (f32[12,3,256]{2,1,0:T(4,128)S(1)}, f32[12,3,256]{2,1,0:T(4,128)S(1)}, u32[]{:S(2)}, u32[]{:S(2)}) collective-permute-start(f32[12,3,256]{2,1,0:T(4,128)S(1)} %constant_dynamic-update-slice_fusion.15), channel_id=1, source_target_pairs={{0,1},{1,2},{2,3},{3,4},{4,5},{5,6},{6,7},{8,9},{9,10},{10,11},{11... | collective-permute-start | bytes 110600 | tf_op jit(solution)/shard_map/ppermute | solution.py:41
  22.9 5.1 %collective-permute-start.9 = (f32[12,3,256]{2,1,0:T(4,128)S(1)}, f32[12,3,256]{2,1,0:T(4,128)S(1)}, u32[]{:S(2)}, u32[]{:S(2)}) collective-permute-start(f32[12,3,256]{2,1,0:T(4,128)S(1)} %constant_dynamic-update-slice_fusion.15), channel_id=1, source_target_pairs={{1,0},{2,1},{3,2},{4,3},{5,4},{6,5},{7,6},{9,8},{10,9},{11,10},{12... | collective-permute-start | bytes 110600 | tf_op jit(solution)/shard_map/ppermute | solution.py:42
  28.1 10.4 %collective-permute-start.10 = (f32[36,3,256]{2,1,0:T(4,128)S(1)}, f32[36,3,256]{2,1,0:T(4,128)S(1)}, u32[]{:S(2)}, u32[]{:S(2)}) collective-permute-start(f32[36,3,256]{2,1,0:T(4,128)S(1)} %constant_dynamic-update-slice_fusion.18), channel_id=1, source_target_pairs={{0,32},{1,33},{2,34},{3,35},{4,36},{5,37},{6,38},{7,39},{8,40},{9,... | collective-permute-start | bytes 331784 | tf_op jit(solution)/shard_map/ppermute | solution.py:41
  31.6 7.7 %collective-permute-start.11 = (f32[36,3,256]{2,1,0:T(4,128)S(1)}, f32[36,3,256]{2,1,0:T(4,128)S(1)}, u32[]{:S(2)}, u32[]{:S(2)}) collective-permute-start(f32[36,3,256]{2,1,0:T(4,128)S(1)} %constant_dynamic-update-slice_fusion.18), channel_id=1, source_target_pairs={{32,0},{33,1},{34,2},{35,3},{36,4},{37,5},{38,6},{39,7},{40,8},{41... | collective-permute-start | bytes 331784 | tf_op jit(solution)/shard_map/ppermute | solution.py:42
  33.9 10.5 %collective-permute-start.2 = (f32[12,32,256]{2,1,0:T(8,128)S(1)}, f32[12,32,256]{2,1,0:T(8,128)S(1)}, u32[]{:S(2)}, u32[]{:S(2)}) collective-permute-start(f32[12,32,256]{2,1,0:T(8,128)S(1)} %constant_dynamic-update-slice_fusion), channel_id=1, source_target_pairs={{0,1},{1,2},{2,3},{3,4},{4,5},{5,6},{6,7},{8,9},{9,10},{10,11},{11... | collective-permute-start | bytes 1179656 | tf_op jit(solution)/shard_map/ppermute | solution.py:41
  37.2 11.1 %collective-permute-start.3 = (f32[12,32,256]{2,1,0:T(8,128)S(1)}, f32[12,32,256]{2,1,0:T(8,128)S(1)}, u32[]{:S(2)}, u32[]{:S(2)}) collective-permute-start(f32[12,32,256]{2,1,0:T(8,128)S(1)} %constant_dynamic-update-slice_fusion), channel_id=1, source_target_pairs={{1,0},{2,1},{3,2},{4,3},{5,4},{6,5},{7,6},{9,8},{10,9},{11,10},{12... | collective-permute-start | bytes 1179656 | tf_op jit(solution)/shard_map/ppermute | solution.py:42
  48.3 33.3 %collective-permute-start.4 = (f32[36,32,256]{2,1,0:T(8,128)S(1)}, f32[36,32,256]{2,1,0:T(8,128)S(1)}, u32[]{:S(2)}, u32[]{:S(2)}) collective-permute-start(f32[36,32,256]{2,1,0:T(8,128)S(1)} %constant_dynamic-update-slice_fusion.3), channel_id=1, source_target_pairs={{0,32},{1,33},{2,34},{3,35},{4,36},{5,37},{6,38},{7,39},{8,40},{9,... | collective-permute-start | bytes 3538952 | tf_op jit(solution)/shard_map/ppermute | solution.py:41
  52.4 33.9 %collective-permute-start.5 = (f32[36,32,256]{2,1,0:T(8,128)S(1)}, f32[36,32,256]{2,1,0:T(8,128)S(1)}, u32[]{:S(2)}, u32[]{:S(2)}) collective-permute-start(f32[36,32,256]{2,1,0:T(8,128)S(1)} %constant_dynamic-update-slice_fusion.3), channel_id=1, source_target_pairs={{32,0},{33,1},{34,2},{35,3},{36,4},{37,5},{38,6},{39,7},{40,8},{41... | collective-permute-start | bytes 3538952 | tf_op jit(solution)/shard_map/ppermute | solution.py:42
  110.9 50.3 %copy-start.1 = (f32[4,32,256]{2,1,0:T(8,128)S(1)}, f32[4,32,256]{2,1,0:T(8,128)}, u32[]{:S(2)}) copy-start(f32[4,32,256]{2,1,0:T(8,128)} %fusion.9) | copy-start | bytes 393220
  110.9 10.2 %collective-permute-start.12 = (f32[4,32,256]{2,1,0:T(8,128)}, f32[4,32,256]{2,1,0:T(8,128)S(1)}, u32[]{:S(2)}, u32[]{:S(2)}) collective-permute-start(f32[4,32,256]{2,1,0:T(8,128)} %fusion.9), channel_id=1, source_target_pairs={{0,8},{1,9},{2,10},{3,11},{4,12},{5,13},{6,14},{7,15},{8,16},{9,17... | collective-permute-start | bytes 393224 | tf_op jit(solution)/shard_map/ppermute | solution.py:41
  113.0 8.5 %collective-permute-start.13 = (f32[4,32,256]{2,1,0:T(8,128)}, f32[4,32,256]{2,1,0:T(8,128)S(1)}, u32[]{:S(2)}, u32[]{:S(2)}) collective-permute-start(f32[4,32,256]{2,1,0:T(8,128)} %fusion.9), channel_id=1, source_target_pairs={{8,0},{9,1},{10,2},{11,3},{12,4},{13,5},{14,6},{15,7},{16,8},{17,9... | collective-permute-start | bytes 393224 | tf_op jit(solution)/shard_map/ppermute | solution.py:42
  122.4 9.0 %collective-permute-start.14 = (f32[12,32,256]{2,1,0:T(8,128)S(1)}, f32[12,32,256]{2,1,0:T(8,128)S(1)}, u32[]{:S(2)}, u32[]{:S(2)}) collective-permute-start(f32[12,32,256]{2,1,0:T(8,128)S(1)} %pad_maximum_fusion.1), channel_id=1, source_target_pairs={{0,1},{1,2},{2,3},{3,4},{4,5},{5,6},{6,7},{8,9},{9,10},{10,11},{11... | collective-permute-start | bytes 1179656 | tf_op jit(solution)/shard_map/ppermute | solution.py:41
  126.7 8.5 %collective-permute-start.15 = (f32[12,32,256]{2,1,0:T(8,128)S(1)}, f32[12,32,256]{2,1,0:T(8,128)S(1)}, u32[]{:S(2)}, u32[]{:S(2)}) collective-permute-start(f32[12,32,256]{2,1,0:T(8,128)S(1)} %pad_maximum_fusion.1), channel_id=1, source_target_pairs={{1,0},{2,1},{3,2},{4,3},{5,4},{6,5},{7,6},{9,8},{10,9},{11,10},{12... | collective-permute-start | bytes 1179656 | tf_op jit(solution)/shard_map/ppermute | solution.py:42
  135.3 23.4 %collective-permute-start.16 = (f32[36,32,256]{2,1,0:T(8,128)S(1)}, f32[36,32,256]{2,1,0:T(8,128)S(1)}, u32[]{:S(2)}, u32[]{:S(2)}) collective-permute-start(f32[36,32,256]{2,1,0:T(8,128)S(1)} %constant_dynamic-update-slice_fusion.30), channel_id=1, source_target_pairs={{0,32},{1,33},{2,34},{3,35},{4,36},{5,37},{6,38},{7,39},{8,40},{9,... | collective-permute-start | bytes 3538952 | tf_op jit(solution)/shard_map/ppermute | solution.py:41
  139.4 25.1 %collective-permute-start.17 = (f32[36,32,256]{2,1,0:T(8,128)S(1)}, f32[36,32,256]{2,1,0:T(8,128)S(1)}, u32[]{:S(2)}, u32[]{:S(2)}) collective-permute-start(f32[36,32,256]{2,1,0:T(8,128)S(1)} %constant_dynamic-update-slice_fusion.30), channel_id=1, source_target_pairs={{32,0},{33,1},{34,2},{35,3},{36,4},{37,5},{38,6},{39,7},{40,8},{41... | collective-permute-start | bytes 3538952 | tf_op jit(solution)/shard_map/ppermute | solution.py:42

commit v7 on v6

--- a/solution.py
+++ b/solution.py
@@ -101,7 +101,7 @@
             "bmrj,bmji->bri",
             near_values,
             kernel,
-            precision=lax.Precision.HIGHEST,
+            precision=lax.Precision.HIGH,
             preferred_element_type=jnp.float32,
         )
         return KERNEL_SCALE * products + NOISE_LEVEL * values

time: 250 us -> 237 us (0.948)
  matrix products: 42.1 us -> 28.1 us
    dot_general x2, matrix products: 42.1 us -> 28.1 us  [operate(): jnp.einsum('bmrj,bmji->bri', near_values, kernel, precision=lax.Precision...]
  transfers between devices with their start and end apart: 18 -> 18, of which waited for: 9 -> 9; matrix products, arithmetic and copies ran while one was open for 18% -> 19% of each run, Pallas kernels for 0% -> 0%
where the time goes in v7:
time: 237 us; the launch traced here: 235 us
  starting transfers between devices  53.8 us (23%)
  blocking collectives  50.6 us (21%)
  waiting for transfers between devices  38.4 us (16%)
  other arithmetic  35.5 us (15%)
  matrix products  28.1 us (12%)
  local copies, waits for them, and re-layouts  25.9 us (11%)
  between operations  3.1 us (1%)
    all_to_all x2, blocking collectives, all_sum(): value = jnp.sum(lax.all_to_all(copies, axis, 0, 0, tiled=False), axis=0)  50.6 us
    ppermute x9, starting transfers between devices, collect_halo(): lower = lax.ppermute(current, AXES, neighbour_route(shape, dim, -1))  32.7 us
    dot_general x2, matrix products, operate(): jnp.einsum('bmrj,bmji->bri', near_values, kernel, precision=lax.Precision...  28.1 us
    mul x1, other arithmetic, per_device(): kernel = jax.vmap(wendland)(points, others) * present[:, :, None, None]  27.8 us
    ppermute x9, waiting for transfers between devices, collect_halo(): lower = lax.ppermute(current, AXES, neighbour_route(shape, dim, -1))  27.2 us
    ppermute x9, starting transfers between devices, collect_halo(): upper = lax.ppermute(current, AXES, neighbour_route(shape, dim, 1))  21.2 us
    unnamed x44, local copies, waits for them, and re-layouts  14.8 us
    ppermute x9, waiting for transfers between devices, collect_halo(): upper = lax.ppermute(current, AXES, neighbour_route(shape, dim, 1))  11.2 us
  transfers between devices with their start and end apart: 18, of which 9 were waited for; matrix products, arithmetic and copies ran while one was open for 19% of the time, Pallas kernels for 0%

profile of v7, /device:TPU:1, one launch (start us, length us, event | category | flops | bytes accessed | tf_op | source)
XLA Modules:
  0.0 235.4 jit_solution(14784421386291354374)
XLA Ops:
  1.4 5.5 %collective-permute-start.6 = (f32[4,3,256]{2,1,0:T(4,128)S(1)}, f32[4,3,256]{2,1,0:T(4,128)S(1)}, u32[]{:S(2)}, u32[]{:S(2)}) collective-permute-start(f32[4,3,256]{2,1,0:T(4,128)S(1)} %copy.23), channel_id=1, source_target_pairs={{0,8},{1,9},{2,10},{3,11},{4,12},{5,13},{6,14},{7,15},{8,16},{9,17... | collective-permute-start | bytes 36872 | tf_op jit(solution)/shard_map/ppermute | solution.py:41
  6.9 2.5 %collective-permute-start.7 = (f32[4,3,256]{2,1,0:T(4,128)S(1)}, f32[4,3,256]{2,1,0:T(4,128)S(1)}, u32[]{:S(2)}, u32[]{:S(2)}) collective-permute-start(f32[4,3,256]{2,1,0:T(4,128)S(1)} %copy.23), channel_id=1, source_target_pairs={{8,0},{9,1},{10,2},{11,3},{12,4},{13,5},{14,6},{15,7},{16,8},{17,9... | collective-permute-start | bytes 36872 | tf_op jit(solution)/shard_map/ppermute | solution.py:42
  9.3 4.3 %collective-permute-start = (f32[4,32,256]{2,1,0:T(8,128)}, f32[4,32,256]{2,1,0:T(8,128)S(1)}, u32[]{:S(2)}, u32[]{:S(2)}) collective-permute-start(f32[4,32,256]{2,1,0:T(8,128)} %param.5), channel_id=1, source_target_pairs={{0,8},{1,9},{2,10},{3,11},{4,12},{5,13},{6,14},{7,15},{8,16},{9,17... | collective-permute-start | bytes 393224 | tf_op jit(solution)/shard_map/ppermute | solution.py:41
  13.7 4.8 %collective-permute-start.1 = (f32[4,32,256]{2,1,0:T(8,128)}, f32[4,32,256]{2,1,0:T(8,128)S(1)}, u32[]{:S(2)}, u32[]{:S(2)}) collective-permute-start(f32[4,32,256]{2,1,0:T(8,128)} %param.5), channel_id=1, source_target_pairs={{8,0},{9,1},{10,2},{11,3},{12,4},{13,5},{14,6},{15,7},{16,8},{17,9... | collective-permute-start | bytes 393224 | tf_op jit(solution)/shard_map/ppermute | solution.py:42
  21.4 1.5 collective-permute-start.8
  22.9 1.3 collective-permute-start.9
  25.0 3.1 %collective-permute-done.9 = f32[12,3,256]{2,1,0:T(4,128)S(1)} collective-permute-done((f32[12,3,256]{2,1,0:T(4,128)S(1)}, f32[12,3,256]{2,1,0:T(4,128)S(1)}, u32[]{:S(2)}, u32[]{:S(2)}) %collective-permute-start.9) | collective-permute-done | bytes 36896 | tf_op jit(solution)/shard_map/ppermute | solution.py:42
  28.1 3.5 %collective-permute-start.10 = (f32[36,3,256]{2,1,0:T(4,128)S(1)}, f32[36,3,256]{2,1,0:T(4,128)S(1)}, u32[]{:S(2)}, u32[]{:S(2)}) collective-permute-start(f32[36,3,256]{2,1,0:T(4,128)S(1)} %constant_dynamic-update-slice_fusion.18), channel_id=1, source_target_pairs={{0,32},{1,33},{2,34},{3,35},{4,36},{5,37},{6,38},{7,39},{8,40},{9,... | collective-permute-start | bytes 331784 | tf_op jit(solution)/shard_map/ppermute | solution.py:41
  31.6 1.3 collective-permute-start.11
  33.9 3.2 %collective-permute-start.2 = (f32[12,32,256]{2,1,0:T(8,128)S(1)}, f32[12,32,256]{2,1,0:T(8,128)S(1)}, u32[]{:S(2)}, u32[]{:S(2)}) collective-permute-start(f32[12,32,256]{2,1,0:T(8,128)S(1)} %constant_dynamic-update-slice_fusion), channel_id=1, source_target_pairs={{0,1},{1,2},{2,3},{3,4},{4,5},{5,6},{6,7},{8,9},{9,10},{10,11},{11... | collective-permute-start | bytes 1179656 | tf_op jit(solution)/shard_map/ppermute | solution.py:41
  37.2 1.3 collective-permute-start.3
  40.5 3.9 %collective-permute-done.2 = f32[12,32,256]{2,1,0:T(8,128)S(1)} collective-permute-done((f32[12,32,256]{2,1,0:T(8,128)S(1)}, f32[12,32,256]{2,1,0:T(8,128)S(1)}, u32[]{:S(2)}, u32[]{:S(2)}) %collective-permute-start.2) | collective-permute-done | bytes 393248 | tf_op jit(solution)/shard_map/ppermute | solution.py:41
  44.5 3.8 %collective-permute-done.3 = f32[12,32,256]{2,1,0:T(8,128)S(1)} collective-permute-done((f32[12,32,256]{2,1,0:T(8,128)S(1)}, f32[12,32,256]{2,1,0:T(8,128)S(1)}, u32[]{:S(2)}, u32[]{:S(2)}) %collective-permute-start.3) | collective-permute-done | bytes 393248 | tf_op jit(solution)/shard_map/ppermute | solution.py:42
  48.3 4.1 %collective-permute-start.4 = (f32[36,32,256]{2,1,0:T(8,128)S(1)}, f32[36,32,256]{2,1,0:T(8,128)S(1)}, u32[]{:S(2)}, u32[]{:S(2)}) collective-permute-start(f32[36,32,256]{2,1,0:T(8,128)S(1)} %constant_dynamic-update-slice_fusion.3), channel_id=1, source_target_pairs={{0,32},{1,33},{2,34},{3,35},{4,36},{5,37},{6,38},{7,39},{8,40},{9,... | collective-permute-start | bytes 3538952 | tf_op jit(solution)/shard_map/ppermute | solution.py:41
  52.4 1.3 collective-permute-start.5
  53.7 27.8 %fusion.7 = f32[4,27,256,256]{3,2,1,0:T(8,128)} fusion(f32[4,27]{1,0:T(4,128)S(1)} %compare_convert_fusion, f32[4,256]{1,0:T(4,128)S(1)} %get-tuple-element.70, f32[4,27,256]{2,1,0:T(8,128)S(1)} %get-tuple-element.75, f32[4,256]{1,0:T(4,128)S(1)} %get-tuple-element.71, f32[4,27,256]{2,1,0:T(8,128)S(1)} %get-tuple-element.76, ...), kind=kLoop, calls=%fused_computation.28 | loop fusion | flops 127401984 | bytes 28656048 | tf_op jit(solution)/shard_map/mul | solution.py:94
  87.5 2.8 %gather_fusion = f32[108,32,256]{2,1,0:T(8,128)S(1)} fusion(f32[108,32,256]{2,1,0:T(8,128)} %constant_dynamic-update-slice_fusion.8, s32[1024]{0:T(1024)S(1)} %pad_clamp_fusion), kind=kCustom, calls=%fused_computation | custom fusion | bytes 7078320 | tf_op jit(solution)/shard_map/gather | solution.py:99
  90.2 13.7 %fusion.9 = f32[4,32,256]{2,1,0:T(8,128)} fusion(f32[4,27,32,256]{3,2,1,0:T(8,128)S(1)} %bitcast.95, f32[4,27,256,256]{3,2,1,0:T(8,128)} %fusion.7, f32[4,32,256]{2,1,0:T(8,128)} %param.5), kind=kOutput, calls=%fused_computation.32 | convolution fusion | flops 1359052800 | bytes 32112640 | tf_op jit(solution)/shard_map/bmrj,bmji->bri/dot_general | solution.py:100
  104.0 2.0 collective-permute-start.12
  106.0 6.2 %collective-permute-start.13 = (f32[4,32,256]{2,1,0:T(8,128)}, f32[4,32,256]{2,1,0:T(8,128)S(1)}, u32[]{:S(2)}, u32[]{:S(2)}) collective-permute-start(f32[4,32,256]{2,1,0:T(8,128)} %fusion.9), channel_id=1, source_target_pairs={{8,0},{9,1},{10,2},{11,3},{12,4},{13,5},{14,6},{15,7},{16,8},{17,9... | collective-permute-start | bytes 393224 | tf_op jit(solution)/shard_map/ppermute | solution.py:42
  112.2 2.0 collective-permute-done.12
  115.4 4.3 %collective-permute-start.14 = (f32[12,32,256]{2,1,0:T(8,128)S(1)}, f32[12,32,256]{2,1,0:T(8,128)S(1)}, u32[]{:S(2)}, u32[]{:S(2)}) collective-permute-start(f32[12,32,256]{2,1,0:T(8,128)S(1)} %pad_maximum_fusion.1), channel_id=1, source_target_pairs={{0,1},{1,2},{2,3},{3,4},{4,5},{5,6},{6,7},{8,9},{9,10},{10,11},{11... | collective-permute-start | bytes 1179656 | tf_op jit(solution)/shard_map/ppermute | solution.py:41
  121.0 3.4 %collective-permute-done.14 = f32[12,32,256]{2,1,0:T(8,128)S(1)} collective-permute-done((f32[12,32,256]{2,1,0:T(8,128)S(1)}, f32[12,32,256]{2,1,0:T(8,128)S(1)}, u32[]{:S(2)}, u32[]{:S(2)}) %collective-permute-start.14) | collective-permute-done | bytes 393248 | tf_op jit(solution)/shard_map/ppermute | solution.py:41
  125.4 2.9 %collective-permute-done.15 = f32[12,32,256]{2,1,0:T(8,128)S(1)} collective-permute-done((f32[12,32,256]{2,1,0:T(8,128)S(1)}, f32[12,32,256]{2,1,0:T(8,128)S(1)}, u32[]{:S(2)}, u32[]{:S(2)}) %collective-permute-start.15) | collective-permute-done | bytes 393248 | tf_op jit(solution)/shard_map/ppermute | solution.py:42
  128.3 4.2 %collective-permute-start.16 = (f32[36,32,256]{2,1,0:T(8,128)S(1)}, f32[36,32,256]{2,1,0:T(8,128)S(1)}, u32[]{:S(2)}, u32[]{:S(2)}) collective-permute-start(f32[36,32,256]{2,1,0:T(8,128)S(1)} %constant_dynamic-update-slice_fusion.30), channel_id=1, source_target_pairs={{0,32},{1,33},{2,34},{3,35},{4,36},{5,37},{6,38},{7,39},{8,40},{9,... | collective-permute-start | bytes 3538952 | tf_op jit(solution)/shard_map/ppermute | solution.py:41
  133.8 17.9 %collective-permute-done.16 = f32[36,32,256]{2,1,0:T(8,128)S(1)} collective-permute-done((f32[36,32,256]{2,1,0:T(8,128)S(1)}, f32[36,32,256]{2,1,0:T(8,128)S(1)}, u32[]{:S(2)}, u32[]{:S(2)}) %collective-permute-start.16) | collective-permute-done | bytes 1179680 | tf_op jit(solution)/shard_map/ppermute | solution.py:41
  158.7 2.8 %gather_fusion.2 = f32[108,32,256]{2,1,0:T(8,128)S(1)} fusion(f32[108,32,256]{2,1,0:T(8,128)} %constant_dynamic-update-slice_fusion.35, s32[1024]{0:T(1024)S(1)} %pad_clamp_fusion), kind=kCustom, calls=%fused_computation.2 | custom fusion | bytes 7078320 | tf_op jit(solution)/shard_map/gather | solution.py:99
  161.5 14.4 %multiply_reduce_fusion.4 = (f32[32]{0:T(128)S(1)}, f32[32]{0:T(128)S(1)}, f32[32]{0:T(128)S(1)}, f32[32]{0:T(128)S(1)}, f32[32]{0:T(128)}, /*index=5*/f32[4,32,256]{2,1,0:T(8,128)}) fusion(f32[4,32,256]{2,1,0:T(8,128)} %fusion.9, f32[4,32,256]{2,1,0:T(8,128)} %param.5, f32[4,27,32,256]{3,2,1,0:T(8,128)S(1)} %bitcast.94, f32[4,27,256,256]{3,2,1,0:T(8,128)} %fusion.7), kind=kOutput, calls=%fused_computation.39 | convolution fusion | flops 1359380352 | bytes 32244352 | tf_op jit(solution)/shard_map/bmrj,bmji->bri/dot_general | solution.py:100
  176.7 12.5 %all_to_all.20 = f32[16,1,160]{2,1,0:T(1,128)S(1)} all-to-all(f32[16,1,160]{2,1,0:T(1,128)S(1)} %reshape.58), channel_id=1, replica_groups=mesh['leaf'=32,'sub'=16] {'sub'}, dimensions={0} | all-to-all | bytes 20480 | tf_op jit(solution)/shard_map/all_to_all | solution.py:76
  190.6 38.1 %all_to_all.21 = f32[32,1,160]{2,1,0:T(1,128)S(1)} all-to-all(f32[32,1,160]{2,1,0:T(1,128)S(1)} %reshape.60), channel_id=1, replica_groups=mesh['leaf'=32,'sub'=16] {'leaf'}, dimensions={0} | all-to-all | bytes 40960 | tf_op jit(solution)/shard_map/all_to_all | solution.py:76
  233.5 1.9 conditional.1
  233.6 1.8 multiply_add_fusion.1
  (88 shorter events, 30.3 us)
Async XLA Ops:
  0.6 43.8 %copy-start = (f32[4,32,256]{2,1,0:T(8,128)S(1)}, f32[4,32,256]{2,1,0:T(8,128)}, u32[]{:S(2)}) copy-start(f32[4,32,256]{2,1,0:T(8,128)} %param.5) | copy-start | bytes 393220
  1.4 19.3 %collective-permute-start.6 = (f32[4,3,256]{2,1,0:T(4,128)S(1)}, f32[4,3,256]{2,1,0:T(4,128)S(1)}, u32[]{:S(2)}, u32[]{:S(2)}) collective-permute-start(f32[4,3,256]{2,1,0:T(4,128)S(1)} %copy.23), channel_id=1, source_target_pairs={{0,8},{1,9},{2,10},{3,11},{4,12},{5,13},{6,14},{7,15},{8,16},{9,17... | collective-permute-start | bytes 36872 | tf_op jit(solution)/shard_map/ppermute | solution.py:41
  6.9 14.5 %collective-permute-start.7 = (f32[4,3,256]{2,1,0:T(4,128)S(1)}, f32[4,3,256]{2,1,0:T(4,128)S(1)}, u32[]{:S(2)}, u32[]{:S(2)}) collective-permute-start(f32[4,3,256]{2,1,0:T(4,128)S(1)} %copy.23), channel_id=1, source_target_pairs={{8,0},{9,1},{10,2},{11,3},{12,4},{13,5},{14,6},{15,7},{16,8},{17,9... | collective-permute-start | bytes 36872 | tf_op jit(solution)/shard_map/ppermute | solution.py:42
  9.3 23.6 %collective-permute-start = (f32[4,32,256]{2,1,0:T(8,128)}, f32[4,32,256]{2,1,0:T(8,128)S(1)}, u32[]{:S(2)}, u32[]{:S(2)}) collective-permute-start(f32[4,32,256]{2,1,0:T(8,128)} %param.5), channel_id=1, source_target_pairs={{0,8},{1,9},{2,10},{3,11},{4,12},{5,13},{6,14},{7,15},{8,16},{9,17... | collective-permute-start | bytes 393224 | tf_op jit(solution)/shard_map/ppermute | solution.py:41
  13.7 20.2 %collective-permute-start.1 = (f32[4,32,256]{2,1,0:T(8,128)}, f32[4,32,256]{2,1,0:T(8,128)S(1)}, u32[]{:S(2)}, u32[]{:S(2)}) collective-permute-start(f32[4,32,256]{2,1,0:T(8,128)} %param.5), channel_id=1, source_target_pairs={{8,0},{9,1},{10,2},{11,3},{12,4},{13,5},{14,6},{15,7},{16,8},{17,9... | collective-permute-start | bytes 393224 | tf_op jit(solution)/shard_map/ppermute | solution.py:42
  21.4 2.8 %collective-permute-start.8 = (f32[12,3,256]{2,1,0:T(4,128)S(1)}, f32[12,3,256]{2,1,0:T(4,128)S(1)}, u32[]{:S(2)}, u32[]{:S(2)}) collective-permute-start(f32[12,3,256]{2,1,0:T(4,128)S(1)} %constant_dynamic-update-slice_fusion.15), channel_id=1, source_target_pairs={{0,1},{1,2},{2,3},{3,4},{4,5},{5,6},{6,7},{8,9},{9,10},{10,11},{11... | collective-permute-start | bytes 110600 | tf_op jit(solution)/shard_map/ppermute | solution.py:41
  22.9 5.1 %collective-permute-start.9 = (f32[12,3,256]{2,1,0:T(4,128)S(1)}, f32[12,3,256]{2,1,0:T(4,128)S(1)}, u32[]{:S(2)}, u32[]{:S(2)}) collective-permute-start(f32[12,3,256]{2,1,0:T(4,128)S(1)} %constant_dynamic-update-slice_fusion.15), channel_id=1, source_target_pairs={{1,0},{2,1},{3,2},{4,3},{5,4},{6,5},{7,6},{9,8},{10,9},{11,10},{12... | collective-permute-start | bytes 110600 | tf_op jit(solution)/shard_map/ppermute | solution.py:42
  28.1 10.4 %collective-permute-start.10 = (f32[36,3,256]{2,1,0:T(4,128)S(1)}, f32[36,3,256]{2,1,0:T(4,128)S(1)}, u32[]{:S(2)}, u32[]{:S(2)}) collective-permute-start(f32[36,3,256]{2,1,0:T(4,128)S(1)} %constant_dynamic-update-slice_fusion.18), channel_id=1, source_target_pairs={{0,32},{1,33},{2,34},{3,35},{4,36},{5,37},{6,38},{7,39},{8,40},{9,... | collective-permute-start | bytes 331784 | tf_op jit(solution)/shard_map/ppermute | solution.py:41
  31.6 7.7 %collective-permute-start.11 = (f32[36,3,256]{2,1,0:T(4,128)S(1)}, f32[36,3,256]{2,1,0:T(4,128)S(1)}, u32[]{:S(2)}, u32[]{:S(2)}) collective-permute-start(f32[36,3,256]{2,1,0:T(4,128)S(1)} %constant_dynamic-update-slice_fusion.18), channel_id=1, source_target_pairs={{32,0},{33,1},{34,2},{35,3},{36,4},{37,5},{38,6},{39,7},{40,8},{41... | collective-permute-start | bytes 331784 | tf_op jit(solution)/shard_map/ppermute | solution.py:42
  33.9 10.5 %collective-permute-start.2 = (f32[12,32,256]{2,1,0:T(8,128)S(1)}, f32[12,32,256]{2,1,0:T(8,128)S(1)}, u32[]{:S(2)}, u32[]{:S(2)}) collective-permute-start(f32[12,32,256]{2,1,0:T(8,128)S(1)} %constant_dynamic-update-slice_fusion), channel_id=1, source_target_pairs={{0,1},{1,2},{2,3},{3,4},{4,5},{5,6},{6,7},{8,9},{9,10},{10,11},{11... | collective-permute-start | bytes 1179656 | tf_op jit(solution)/shard_map/ppermute | solution.py:41
  37.2 11.1 %collective-permute-start.3 = (f32[12,32,256]{2,1,0:T(8,128)S(1)}, f32[12,32,256]{2,1,0:T(8,128)S(1)}, u32[]{:S(2)}, u32[]{:S(2)}) collective-permute-start(f32[12,32,256]{2,1,0:T(8,128)S(1)} %constant_dynamic-update-slice_fusion), channel_id=1, source_target_pairs={{1,0},{2,1},{3,2},{4,3},{5,4},{6,5},{7,6},{9,8},{10,9},{11,10},{12... | collective-permute-start | bytes 1179656 | tf_op jit(solution)/shard_map/ppermute | solution.py:42
  48.3 33.3 %collective-permute-start.4 = (f32[36,32,256]{2,1,0:T(8,128)S(1)}, f32[36,32,256]{2,1,0:T(8,128)S(1)}, u32[]{:S(2)}, u32[]{:S(2)}) collective-permute-start(f32[36,32,256]{2,1,0:T(8,128)S(1)} %constant_dynamic-update-slice_fusion.3), channel_id=1, source_target_pairs={{0,32},{1,33},{2,34},{3,35},{4,36},{5,37},{6,38},{7,39},{8,40},{9,... | collective-permute-start | bytes 3538952 | tf_op jit(solution)/shard_map/ppermute | solution.py:41
  52.4 33.9 %collective-permute-start.5 = (f32[36,32,256]{2,1,0:T(8,128)S(1)}, f32[36,32,256]{2,1,0:T(8,128)S(1)}, u32[]{:S(2)}, u32[]{:S(2)}) collective-permute-start(f32[36,32,256]{2,1,0:T(8,128)S(1)} %constant_dynamic-update-slice_fusion.3), channel_id=1, source_target_pairs={{32,0},{33,1},{34,2},{35,3},{36,4},{37,5},{38,6},{39,7},{40,8},{41... | collective-permute-start | bytes 3538952 | tf_op jit(solution)/shard_map/ppermute | solution.py:42
  104.0 50.3 %copy-start.1 = (f32[4,32,256]{2,1,0:T(8,128)S(1)}, f32[4,32,256]{2,1,0:T(8,128)}, u32[]{:S(2)}) copy-start(f32[4,32,256]{2,1,0:T(8,128)} %fusion.9) | copy-start | bytes 393220
  104.0 10.2 %collective-permute-start.12 = (f32[4,32,256]{2,1,0:T(8,128)}, f32[4,32,256]{2,1,0:T(8,128)S(1)}, u32[]{:S(2)}, u32[]{:S(2)}) collective-permute-start(f32[4,32,256]{2,1,0:T(8,128)} %fusion.9), channel_id=1, source_target_pairs={{0,8},{1,9},{2,10},{3,11},{4,12},{5,13},{6,14},{7,15},{8,16},{9,17... | collective-permute-start | bytes 393224 | tf_op jit(solution)/shard_map/ppermute | solution.py:41
  106.0 8.5 %collective-permute-start.13 = (f32[4,32,256]{2,1,0:T(8,128)}, f32[4,32,256]{2,1,0:T(8,128)S(1)}, u32[]{:S(2)}, u32[]{:S(2)}) collective-permute-start(f32[4,32,256]{2,1,0:T(8,128)} %fusion.9), channel_id=1, source_target_pairs={{8,0},{9,1},{10,2},{11,3},{12,4},{13,5},{14,6},{15,7},{16,8},{17,9... | collective-permute-start | bytes 393224 | tf_op jit(solution)/shard_map/ppermute | solution.py:42
  115.4 9.0 %collective-permute-start.14 = (f32[12,32,256]{2,1,0:T(8,128)S(1)}, f32[12,32,256]{2,1,0:T(8,128)S(1)}, u32[]{:S(2)}, u32[]{:S(2)}) collective-permute-start(f32[12,32,256]{2,1,0:T(8,128)S(1)} %pad_maximum_fusion.1), channel_id=1, source_target_pairs={{0,1},{1,2},{2,3},{3,4},{4,5},{5,6},{6,7},{8,9},{9,10},{10,11},{11... | collective-permute-start | bytes 1179656 | tf_op jit(solution)/shard_map/ppermute | solution.py:41
  119.7 8.5 %collective-permute-start.15 = (f32[12,32,256]{2,1,0:T(8,128)S(1)}, f32[12,32,256]{2,1,0:T(8,128)S(1)}, u32[]{:S(2)}, u32[]{:S(2)}) collective-permute-start(f32[12,32,256]{2,1,0:T(8,128)S(1)} %pad_maximum_fusion.1), channel_id=1, source_target_pairs={{1,0},{2,1},{3,2},{4,3},{5,4},{6,5},{7,6},{9,8},{10,9},{11,10},{12... | collective-permute-start | bytes 1179656 | tf_op jit(solution)/shard_map/ppermute | solution.py:42
  128.3 23.4 %collective-permute-start.16 = (f32[36,32,256]{2,1,0:T(8,128)S(1)}, f32[36,32,256]{2,1,0:T(8,128)S(1)}, u32[]{:S(2)}, u32[]{:S(2)}) collective-permute-start(f32[36,32,256]{2,1,0:T(8,128)S(1)} %constant_dynamic-update-slice_fusion.30), channel_id=1, source_target_pairs={{0,32},{1,33},{2,34},{3,35},{4,36},{5,37},{6,38},{7,39},{8,40},{9,... | collective-permute-start | bytes 3538952 | tf_op jit(solution)/shard_map/ppermute | solution.py:41
  132.5 25.1 %collective-permute-start.17 = (f32[36,32,256]{2,1,0:T(8,128)S(1)}, f32[36,32,256]{2,1,0:T(8,128)S(1)}, u32[]{:S(2)}, u32[]{:S(2)}) collective-permute-start(f32[36,32,256]{2,1,0:T(8,128)S(1)} %constant_dynamic-update-slice_fusion.30), channel_id=1, source_target_pairs={{32,0},{33,1},{34,2},{35,3},{36,4},{37,5},{38,6},{39,7},{40,8},{41... | collective-permute-start | bytes 3538952 | tf_op jit(solution)/shard_map/ppermute | solution.py:42

commit v8 on v7

--- a/solution.py
+++ b/solution.py
@@ -32,7 +32,7 @@
     return route
 
 
-HALO_ORDER = (1, 2, 0)
+HALO_ORDER = (2, 1, 0)
 
 
 def collect_halo(tile_in, shape):
@@ -64,7 +64,7 @@
     step_x = owner_dev // plane - own_dev // plane
     step_y = owner_dev // count_low % count_mid - own_dev // count_low % count_mid
     step_z = owner_dev % count_low - own_dev % count_low
-    positions = (((step_x + 1) * 3 + step_z + 1) * 3 + step_y + 1) * per_dev + clamped % per_dev
+    positions = (((step_x + 1) * 3 + step_y + 1) * 3 + step_z + 1) * per_dev + clamped % per_dev
     positions = jnp.clip(positions, 0, 27 * per_dev - 1)
     return (positions, present)
 

time: 237 us -> 244 us (1.030)
  waiting for transfers between devices: 38.4 us -> 41.8 us
    ppermute x9, waiting for transfers between devices: 27.2 us -> 32.6 us  [collect_halo(): lower = lax.ppermute(current, AXES, neighbour_route(shape, dim, -1))]
  transfers between devices with their start and end apart: 18 -> 18, of which waited for: 9 -> 8; matrix products, arithmetic and copies ran while one was open for 19% -> 19% of each run, Pallas kernels for 0% -> 0%
where the time goes in v8:
time: 244 us; the launch traced here: 242 us
  starting transfers between devices  55.3 us (23%)
  blocking collectives  52.6 us (22%)
  waiting for transfers between devices  41.8 us (17%)
  other arithmetic  35.5 us (15%)
  matrix products  28.1 us (12%)
  local copies, waits for them, and re-layouts  25.9 us (11%)
  between operations  3.11 us (1%)
    all_to_all x2, blocking collectives, all_sum(): value = jnp.sum(lax.all_to_all(copies, axis, 0, 0, tiled=False), axis=0)  52.6 us
    ppermute x9, starting transfers between devices, collect_halo(): lower = lax.ppermute(current, AXES, neighbour_route(shape, dim, -1))  32.9 us
    ppermute x9, waiting for transfers between devices, collect_halo(): lower = lax.ppermute(current, AXES, neighbour_route(shape, dim, -1))  32.6 us
    dot_general x2, matrix products, operate(): jnp.einsum('bmrj,bmji->bri', near_values, kernel, precision=lax.Precision...  28.1 us
    mul x1, other arithmetic, per_device(): kernel = jax.vmap(wendland)(points, others) * present[:, :, None, None]  27.8 us
    ppermute x9, starting transfers between devices, collect_halo(): upper = lax.ppermute(current, AXES, neighbour_route(shape, dim, 1))  22.4 us
    unnamed x44, local copies, waits for them, and re-layouts  14.8 us
    ppermute x9, waiting for transfers between devices, collect_halo(): upper = lax.ppermute(current, AXES, neighbour_route(shape, dim, 1))  9.13 us
  transfers between devices with their start and end apart: 18, of which 8 were waited for; matrix products, arithmetic and copies ran while one was open for 19% of the time, Pallas kernels for 0%

profile of v8, /device:TPU:1, one launch (start us, length us, event | category | flops | bytes accessed | tf_op | source)
XLA Modules:
  0.0 242.3 jit_solution(15295920050879343488)
XLA Ops:
  1.4 4.0 %collective-permute-start.6 = (f32[4,3,256]{2,1,0:T(4,128)S(1)}, f32[4,3,256]{2,1,0:T(4,128)S(1)}, u32[]{:S(2)}, u32[]{:S(2)}) collective-permute-start(f32[4,3,256]{2,1,0:T(4,128)S(1)} %copy.23), channel_id=1, source_target_pairs={{0,1},{1,2},{2,3},{3,4},{4,5},{5,6},{6,7},{8,9},{9,10},{10,11},{11... | collective-permute-start | bytes 36872 | tf_op jit(solution)/shard_map/ppermute | solution.py:41
  5.4 1.3 collective-permute-start.7
  6.7 4.0 %collective-permute-start = (f32[4,32,256]{2,1,0:T(8,128)}, f32[4,32,256]{2,1,0:T(8,128)S(1)}, u32[]{:S(2)}, u32[]{:S(2)}) collective-permute-start(f32[4,32,256]{2,1,0:T(8,128)} %param.5), channel_id=1, source_target_pairs={{0,1},{1,2},{2,3},{3,4},{4,5},{5,6},{6,7},{8,9},{9,10},{10,11},{11... | collective-permute-start | bytes 393224 | tf_op jit(solution)/shard_map/ppermute | solution.py:41
  10.7 1.3 collective-permute-start.1
  15.0 4.7 %collective-permute-start.8 = (f32[12,3,256]{2,1,0:T(4,128)S(1)}, f32[12,3,256]{2,1,0:T(4,128)S(1)}, u32[]{:S(2)}, u32[]{:S(2)}) collective-permute-start(f32[12,3,256]{2,1,0:T(4,128)S(1)} %constant_dynamic-update-slice_fusion.15), channel_id=1, source_target_pairs={{0,8},{1,9},{2,10},{3,11},{4,12},{5,13},{6,14},{7,15},{8,16},{9,17... | collective-permute-start | bytes 110600 | tf_op jit(solution)/shard_map/ppermute | solution.py:41
  19.7 3.3 %collective-permute-start.9 = (f32[12,3,256]{2,1,0:T(4,128)S(1)}, f32[12,3,256]{2,1,0:T(4,128)S(1)}, u32[]{:S(2)}, u32[]{:S(2)}) collective-permute-start(f32[12,3,256]{2,1,0:T(4,128)S(1)} %constant_dynamic-update-slice_fusion.15), channel_id=1, source_target_pairs={{8,0},{9,1},{10,2},{11,3},{12,4},{13,5},{14,6},{15,7},{16,8},{17,9... | collective-permute-start | bytes 110600 | tf_op jit(solution)/shard_map/ppermute | solution.py:42
  23.8 2.2 collective-permute-done.9
  26.0 3.5 %collective-permute-start.10 = (f32[36,3,256]{2,1,0:T(4,128)S(1)}, f32[36,3,256]{2,1,0:T(4,128)S(1)}, u32[]{:S(2)}, u32[]{:S(2)}) collective-permute-start(f32[36,3,256]{2,1,0:T(4,128)S(1)} %constant_dynamic-update-slice_fusion.18), channel_id=1, source_target_pairs={{0,32},{1,33},{2,34},{3,35},{4,36},{5,37},{6,38},{7,39},{8,40},{9,... | collective-permute-start | bytes 331784 | tf_op jit(solution)/shard_map/ppermute | solution.py:41
  29.6 1.3 collective-permute-start.11
  31.9 1.9 collective-permute-start.2
  33.8 5.1 %collective-permute-start.3 = (f32[12,32,256]{2,1,0:T(8,128)S(1)}, f32[12,32,256]{2,1,0:T(8,128)S(1)}, u32[]{:S(2)}, u32[]{:S(2)}) collective-permute-start(f32[12,32,256]{2,1,0:T(8,128)S(1)} %constant_dynamic-update-slice_fusion), channel_id=1, source_target_pairs={{8,0},{9,1},{10,2},{11,3},{12,4},{13,5},{14,6},{15,7},{16,8},{17,9... | collective-permute-start | bytes 1179656 | tf_op jit(solution)/shard_map/ppermute | solution.py:42
  41.0 4.4 %collective-permute-done.2 = f32[12,32,256]{2,1,0:T(8,128)S(1)} collective-permute-done((f32[12,32,256]{2,1,0:T(8,128)S(1)}, f32[12,32,256]{2,1,0:T(8,128)S(1)}, u32[]{:S(2)}, u32[]{:S(2)}) %collective-permute-start.2) | collective-permute-done | bytes 393248 | tf_op jit(solution)/shard_map/ppermute | solution.py:41
  45.4 2.9 %collective-permute-done.3 = f32[12,32,256]{2,1,0:T(8,128)S(1)} collective-permute-done((f32[12,32,256]{2,1,0:T(8,128)S(1)}, f32[12,32,256]{2,1,0:T(8,128)S(1)}, u32[]{:S(2)}, u32[]{:S(2)}) %collective-permute-start.3) | collective-permute-done | bytes 393248 | tf_op jit(solution)/shard_map/ppermute | solution.py:42
  48.4 4.2 %collective-permute-start.4 = (f32[36,32,256]{2,1,0:T(8,128)S(1)}, f32[36,32,256]{2,1,0:T(8,128)S(1)}, u32[]{:S(2)}, u32[]{:S(2)}) collective-permute-start(f32[36,32,256]{2,1,0:T(8,128)S(1)} %constant_dynamic-update-slice_fusion.3), channel_id=1, source_target_pairs={{0,32},{1,33},{2,34},{3,35},{4,36},{5,37},{6,38},{7,39},{8,40},{9,... | collective-permute-start | bytes 3538952 | tf_op jit(solution)/shard_map/ppermute | solution.py:41
  52.6 1.3 collective-permute-start.5
  53.9 27.8 %fusion.7 = f32[4,27,256,256]{3,2,1,0:T(8,128)} fusion(f32[4,27]{1,0:T(4,128)S(1)} %compare_convert_fusion, f32[4,256]{1,0:T(4,128)S(1)} %get-tuple-element.70, f32[4,27,256]{2,1,0:T(8,128)S(1)} %get-tuple-element.75, f32[4,256]{1,0:T(4,128)S(1)} %get-tuple-element.71, f32[4,27,256]{2,1,0:T(8,128)S(1)} %get-tuple-element.76, ...), kind=kLoop, calls=%fused_computation.28 | loop fusion | flops 127401984 | bytes 28656048 | tf_op jit(solution)/shard_map/mul | solution.py:94
  87.6 2.8 %gather_fusion = f32[108,32,256]{2,1,0:T(8,128)S(1)} fusion(f32[108,32,256]{2,1,0:T(8,128)} %constant_dynamic-update-slice_fusion.8, s32[1024]{0:T(1024)S(1)} %pad_clamp_fusion), kind=kCustom, calls=%fused_computation | custom fusion | bytes 7078320 | tf_op jit(solution)/shard_map/gather | solution.py:99
  90.4 13.7 %fusion.9 = f32[4,32,256]{2,1,0:T(8,128)} fusion(f32[4,27,32,256]{3,2,1,0:T(8,128)S(1)} %bitcast.95, f32[4,27,256,256]{3,2,1,0:T(8,128)} %fusion.7, f32[4,32,256]{2,1,0:T(8,128)} %param.5), kind=kOutput, calls=%fused_computation.32 | convolution fusion | flops 1359052800 | bytes 32112640 | tf_op jit(solution)/shard_map/bmrj,bmji->bri/dot_general | solution.py:100
  104.1 4.1 %collective-permute-start.12 = (f32[4,32,256]{2,1,0:T(8,128)}, f32[4,32,256]{2,1,0:T(8,128)S(1)}, u32[]{:S(2)}, u32[]{:S(2)}) collective-permute-start(f32[4,32,256]{2,1,0:T(8,128)} %fusion.9), channel_id=1, source_target_pairs={{0,1},{1,2},{2,3},{3,4},{4,5},{5,6},{6,7},{8,9},{9,10},{10,11},{11... | collective-permute-start | bytes 393224 | tf_op jit(solution)/shard_map/ppermute | solution.py:41
  108.3 1.3 collective-permute-start.13
  110.5 3.7 %collective-permute-done.13 = f32[4,32,256]{2,1,0:T(8,128)S(1)} collective-permute-done((f32[4,32,256]{2,1,0:T(8,128)}, f32[4,32,256]{2,1,0:T(8,128)S(1)}, u32[]{:S(2)}, u32[]{:S(2)}) %collective-permute-start.13) | collective-permute-done | bytes 131104 | tf_op jit(solution)/shard_map/ppermute | solution.py:42
  115.1 1.9 collective-permute-start.14
  117.0 6.2 %collective-permute-start.15 = (f32[12,32,256]{2,1,0:T(8,128)S(1)}, f32[12,32,256]{2,1,0:T(8,128)S(1)}, u32[]{:S(2)}, u32[]{:S(2)}) collective-permute-start(f32[12,32,256]{2,1,0:T(8,128)S(1)} %pad_maximum_fusion.1), channel_id=1, source_target_pairs={{8,0},{9,1},{10,2},{11,3},{12,4},{13,5},{14,6},{15,7},{16,8},{17,9... | collective-permute-start | bytes 1179656 | tf_op jit(solution)/shard_map/ppermute | solution.py:42
  123.2 7.4 %collective-permute-done.14 = f32[12,32,256]{2,1,0:T(8,128)S(1)} collective-permute-done((f32[12,32,256]{2,1,0:T(8,128)S(1)}, f32[12,32,256]{2,1,0:T(8,128)S(1)}, u32[]{:S(2)}, u32[]{:S(2)}) %collective-permute-start.14) | collective-permute-done | bytes 393248 | tf_op jit(solution)/shard_map/ppermute | solution.py:41
  131.7 4.5 %collective-permute-start.16 = (f32[36,32,256]{2,1,0:T(8,128)S(1)}, f32[36,32,256]{2,1,0:T(8,128)S(1)}, u32[]{:S(2)}, u32[]{:S(2)}) collective-permute-start(f32[36,32,256]{2,1,0:T(8,128)S(1)} %constant_dynamic-update-slice_fusion.30), channel_id=1, source_target_pairs={{0,32},{1,33},{2,34},{3,35},{4,36},{5,37},{6,38},{7,39},{8,40},{9,... | collective-permute-start | bytes 3538952 | tf_op jit(solution)/shard_map/ppermute | solution.py:41
  137.5 19.9 %collective-permute-done.16 = f32[36,32,256]{2,1,0:T(8,128)S(1)} collective-permute-done((f32[36,32,256]{2,1,0:T(8,128)S(1)}, f32[36,32,256]{2,1,0:T(8,128)S(1)}, u32[]{:S(2)}, u32[]{:S(2)}) %collective-permute-start.16) | collective-permute-done | bytes 1179680 | tf_op jit(solution)/shard_map/ppermute | solution.py:41
  163.6 2.8 %gather_fusion.2 = f32[108,32,256]{2,1,0:T(8,128)S(1)} fusion(f32[108,32,256]{2,1,0:T(8,128)} %constant_dynamic-update-slice_fusion.35, s32[1024]{0:T(1024)S(1)} %pad_clamp_fusion), kind=kCustom, calls=%fused_computation.2 | custom fusion | bytes 7078320 | tf_op jit(solution)/shard_map/gather | solution.py:99
  166.4 14.4 %multiply_reduce_fusion.4 = (f32[32]{0:T(128)S(1)}, f32[32]{0:T(128)S(1)}, f32[32]{0:T(128)S(1)}, f32[32]{0:T(128)S(1)}, f32[32]{0:T(128)}, /*index=5*/f32[4,32,256]{2,1,0:T(8,128)}) fusion(f32[4,32,256]{2,1,0:T(8,128)} %fusion.9, f32[4,32,256]{2,1,0:T(8,128)} %param.5, f32[4,27,32,256]{3,2,1,0:T(8,128)S(1)} %bitcast.94, f32[4,27,256,256]{3,2,1,0:T(8,128)} %fusion.7), kind=kOutput, calls=%fused_computation.39 | convolution fusion | flops 1359380352 | bytes 32244352 | tf_op jit(solution)/shard_map/bmrj,bmji->bri/dot_general | solution.py:100
  181.6 16.3 %all_to_all.20 = f32[16,1,160]{2,1,0:T(1,128)S(1)} all-to-all(f32[16,1,160]{2,1,0:T(1,128)S(1)} %reshape.58), channel_id=1, replica_groups=mesh['leaf'=32,'sub'=16] {'sub'}, dimensions={0} | all-to-all | bytes 20480 | tf_op jit(solution)/shard_map/all_to_all | solution.py:76
  199.3 36.3 %all_to_all.21 = f32[32,1,160]{2,1,0:T(1,128)S(1)} all-to-all(f32[32,1,160]{2,1,0:T(1,128)S(1)} %reshape.60), channel_id=1, replica_groups=mesh['leaf'=32,'sub'=16] {'leaf'}, dimensions={0} | all-to-all | bytes 40960 | tf_op jit(solution)/shard_map/all_to_all | solution.py:76
  240.5 1.9 conditional.1
  240.5 1.8 multiply_add_fusion.1
  (88 shorter events, 28.8 us)
Async XLA Ops:
  0.6 44.8 %copy-start = (f32[4,32,256]{2,1,0:T(8,128)S(1)}, f32[4,32,256]{2,1,0:T(8,128)}, u32[]{:S(2)}) copy-start(f32[4,32,256]{2,1,0:T(8,128)} %param.5) | copy-start | bytes 393220
  1.4 12.9 %collective-permute-start.6 = (f32[4,3,256]{2,1,0:T(4,128)S(1)}, f32[4,3,256]{2,1,0:T(4,128)S(1)}, u32[]{:S(2)}, u32[]{:S(2)}) collective-permute-start(f32[4,3,256]{2,1,0:T(4,128)S(1)} %copy.23), channel_id=1, source_target_pairs={{0,1},{1,2},{2,3},{3,4},{4,5},{5,6},{6,7},{8,9},{9,10},{10,11},{11... | collective-permute-start | bytes 36872 | tf_op jit(solution)/shard_map/ppermute | solution.py:41
  5.4 9.6 %collective-permute-start.7 = (f32[4,3,256]{2,1,0:T(4,128)S(1)}, f32[4,3,256]{2,1,0:T(4,128)S(1)}, u32[]{:S(2)}, u32[]{:S(2)}) collective-permute-start(f32[4,3,256]{2,1,0:T(4,128)S(1)} %copy.23), channel_id=1, source_target_pairs={{1,0},{2,1},{3,2},{4,3},{5,4},{6,5},{7,6},{9,8},{10,9},{11,10},{12... | collective-permute-start | bytes 36872 | tf_op jit(solution)/shard_map/ppermute | solution.py:42
  6.7 24.2 %collective-permute-start = (f32[4,32,256]{2,1,0:T(8,128)}, f32[4,32,256]{2,1,0:T(8,128)S(1)}, u32[]{:S(2)}, u32[]{:S(2)}) collective-permute-start(f32[4,32,256]{2,1,0:T(8,128)} %param.5), channel_id=1, source_target_pairs={{0,1},{1,2},{2,3},{3,4},{4,5},{5,6},{6,7},{8,9},{9,10},{10,11},{11... | collective-permute-start | bytes 393224 | tf_op jit(solution)/shard_map/ppermute | solution.py:41
  10.7 21.1 %collective-permute-start.1 = (f32[4,32,256]{2,1,0:T(8,128)}, f32[4,32,256]{2,1,0:T(8,128)S(1)}, u32[]{:S(2)}, u32[]{:S(2)}) collective-permute-start(f32[4,32,256]{2,1,0:T(8,128)} %param.5), channel_id=1, source_target_pairs={{1,0},{2,1},{3,2},{4,3},{5,4},{6,5},{7,6},{9,8},{10,9},{11,10},{12... | collective-permute-start | bytes 393224 | tf_op jit(solution)/shard_map/ppermute | solution.py:42
  15.0 8.0 %collective-permute-start.8 = (f32[12,3,256]{2,1,0:T(4,128)S(1)}, f32[12,3,256]{2,1,0:T(4,128)S(1)}, u32[]{:S(2)}, u32[]{:S(2)}) collective-permute-start(f32[12,3,256]{2,1,0:T(4,128)S(1)} %constant_dynamic-update-slice_fusion.15), channel_id=1, source_target_pairs={{0,8},{1,9},{2,10},{3,11},{4,12},{5,13},{6,14},{7,15},{8,16},{9,17... | collective-permute-start | bytes 110600 | tf_op jit(solution)/shard_map/ppermute | solution.py:41
  19.7 6.3 %collective-permute-start.9 = (f32[12,3,256]{2,1,0:T(4,128)S(1)}, f32[12,3,256]{2,1,0:T(4,128)S(1)}, u32[]{:S(2)}, u32[]{:S(2)}) collective-permute-start(f32[12,3,256]{2,1,0:T(4,128)S(1)} %constant_dynamic-update-slice_fusion.15), channel_id=1, source_target_pairs={{8,0},{9,1},{10,2},{11,3},{12,4},{13,5},{14,6},{15,7},{16,8},{17,9... | collective-permute-start | bytes 110600 | tf_op jit(solution)/shard_map/ppermute | solution.py:42
  26.0 12.9 %collective-permute-start.10 = (f32[36,3,256]{2,1,0:T(4,128)S(1)}, f32[36,3,256]{2,1,0:T(4,128)S(1)}, u32[]{:S(2)}, u32[]{:S(2)}) collective-permute-start(f32[36,3,256]{2,1,0:T(4,128)S(1)} %constant_dynamic-update-slice_fusion.18), channel_id=1, source_target_pairs={{0,32},{1,33},{2,34},{3,35},{4,36},{5,37},{6,38},{7,39},{8,40},{9,... | collective-permute-start | bytes 331784 | tf_op jit(solution)/shard_map/ppermute | solution.py:41
  29.6 10.2 %collective-permute-start.11 = (f32[36,3,256]{2,1,0:T(4,128)S(1)}, f32[36,3,256]{2,1,0:T(4,128)S(1)}, u32[]{:S(2)}, u32[]{:S(2)}) collective-permute-start(f32[36,3,256]{2,1,0:T(4,128)S(1)} %constant_dynamic-update-slice_fusion.18), channel_id=1, source_target_pairs={{32,0},{33,1},{34,2},{35,3},{36,4},{37,5},{38,6},{39,7},{40,8},{41... | collective-permute-start | bytes 331784 | tf_op jit(solution)/shard_map/ppermute | solution.py:42
  31.9 13.5 %collective-permute-start.2 = (f32[12,32,256]{2,1,0:T(8,128)S(1)}, f32[12,32,256]{2,1,0:T(8,128)S(1)}, u32[]{:S(2)}, u32[]{:S(2)}) collective-permute-start(f32[12,32,256]{2,1,0:T(8,128)S(1)} %constant_dynamic-update-slice_fusion), channel_id=1, source_target_pairs={{0,8},{1,9},{2,10},{3,11},{4,12},{5,13},{6,14},{7,15},{8,16},{9,17... | collective-permute-start | bytes 1179656 | tf_op jit(solution)/shard_map/ppermute | solution.py:41
  33.8 14.5 %collective-permute-start.3 = (f32[12,32,256]{2,1,0:T(8,128)S(1)}, f32[12,32,256]{2,1,0:T(8,128)S(1)}, u32[]{:S(2)}, u32[]{:S(2)}) collective-permute-start(f32[12,32,256]{2,1,0:T(8,128)S(1)} %constant_dynamic-update-slice_fusion), channel_id=1, source_target_pairs={{8,0},{9,1},{10,2},{11,3},{12,4},{13,5},{14,6},{15,7},{16,8},{17,9... | collective-permute-start | bytes 1179656 | tf_op jit(solution)/shard_map/ppermute | solution.py:42
  48.4 33.4 %collective-permute-start.4 = (f32[36,32,256]{2,1,0:T(8,128)S(1)}, f32[36,32,256]{2,1,0:T(8,128)S(1)}, u32[]{:S(2)}, u32[]{:S(2)}) collective-permute-start(f32[36,32,256]{2,1,0:T(8,128)S(1)} %constant_dynamic-update-slice_fusion.3), channel_id=1, source_target_pairs={{0,32},{1,33},{2,34},{3,35},{4,36},{5,37},{6,38},{7,39},{8,40},{9,... | collective-permute-start | bytes 3538952 | tf_op jit(solution)/shard_map/ppermute | solution.py:41
  52.6 33.9 %collective-permute-start.5 = (f32[36,32,256]{2,1,0:T(8,128)S(1)}, f32[36,32,256]{2,1,0:T(8,128)S(1)}, u32[]{:S(2)}, u32[]{:S(2)}) collective-permute-start(f32[36,32,256]{2,1,0:T(8,128)S(1)} %constant_dynamic-update-slice_fusion.3), channel_id=1, source_target_pairs={{32,0},{33,1},{34,2},{35,3},{36,4},{37,5},{38,6},{39,7},{40,8},{41... | collective-permute-start | bytes 3538952 | tf_op jit(solution)/shard_map/ppermute | solution.py:42
  104.1 55.9 %copy-start.1 = (f32[4,32,256]{2,1,0:T(8,128)S(1)}, f32[4,32,256]{2,1,0:T(8,128)}, u32[]{:S(2)}) copy-start(f32[4,32,256]{2,1,0:T(8,128)} %fusion.9) | copy-start | bytes 393220
  104.1 6.4 %collective-permute-start.12 = (f32[4,32,256]{2,1,0:T(8,128)}, f32[4,32,256]{2,1,0:T(8,128)S(1)}, u32[]{:S(2)}, u32[]{:S(2)}) collective-permute-start(f32[4,32,256]{2,1,0:T(8,128)} %fusion.9), channel_id=1, source_target_pairs={{0,1},{1,2},{2,3},{3,4},{4,5},{5,6},{6,7},{8,9},{9,10},{10,11},{11... | collective-permute-start | bytes 393224 | tf_op jit(solution)/shard_map/ppermute | solution.py:41
  108.3 5.9 %collective-permute-start.13 = (f32[4,32,256]{2,1,0:T(8,128)}, f32[4,32,256]{2,1,0:T(8,128)S(1)}, u32[]{:S(2)}, u32[]{:S(2)}) collective-permute-start(f32[4,32,256]{2,1,0:T(8,128)} %fusion.9), channel_id=1, source_target_pairs={{1,0},{2,1},{3,2},{4,3},{5,4},{6,5},{7,6},{9,8},{10,9},{11,10},{12... | collective-permute-start | bytes 393224 | tf_op jit(solution)/shard_map/ppermute | solution.py:42
  115.1 15.6 %collective-permute-start.14 = (f32[12,32,256]{2,1,0:T(8,128)S(1)}, f32[12,32,256]{2,1,0:T(8,128)S(1)}, u32[]{:S(2)}, u32[]{:S(2)}) collective-permute-start(f32[12,32,256]{2,1,0:T(8,128)S(1)} %pad_maximum_fusion.1), channel_id=1, source_target_pairs={{0,8},{1,9},{2,10},{3,11},{4,12},{5,13},{6,14},{7,15},{8,16},{9,17... | collective-permute-start | bytes 1179656 | tf_op jit(solution)/shard_map/ppermute | solution.py:41
  117.0 14.6 %collective-permute-start.15 = (f32[12,32,256]{2,1,0:T(8,128)S(1)}, f32[12,32,256]{2,1,0:T(8,128)S(1)}, u32[]{:S(2)}, u32[]{:S(2)}) collective-permute-start(f32[12,32,256]{2,1,0:T(8,128)S(1)} %pad_maximum_fusion.1), channel_id=1, source_target_pairs={{8,0},{9,1},{10,2},{11,3},{12,4},{13,5},{14,6},{15,7},{16,8},{17,9... | collective-permute-start | bytes 1179656 | tf_op jit(solution)/shard_map/ppermute | solution.py:42
  131.7 25.7 %collective-permute-start.16 = (f32[36,32,256]{2,1,0:T(8,128)S(1)}, f32[36,32,256]{2,1,0:T(8,128)S(1)}, u32[]{:S(2)}, u32[]{:S(2)}) collective-permute-start(f32[36,32,256]{2,1,0:T(8,128)S(1)} %constant_dynamic-update-slice_fusion.30), channel_id=1, source_target_pairs={{0,32},{1,33},{2,34},{3,35},{4,36},{5,37},{6,38},{7,39},{8,40},{9,... | collective-permute-start | bytes 3538952 | tf_op jit(solution)/shard_map/ppermute | solution.py:41
  136.2 26.2 %collective-permute-start.17 = (f32[36,32,256]{2,1,0:T(8,128)S(1)}, f32[36,32,256]{2,1,0:T(8,128)S(1)}, u32[]{:S(2)}, u32[]{:S(2)}) collective-permute-start(f32[36,32,256]{2,1,0:T(8,128)S(1)} %constant_dynamic-update-slice_fusion.30), channel_id=1, source_target_pairs={{32,0},{33,1},{34,2},{35,3},{36,4},{37,5},{38,6},{39,7},{40,8},{41... | collective-permute-start | bytes 3538952 | tf_op jit(solution)/shard_map/ppermute | solution.py:42
